TPU v7x, 32 devices: a whole 2x2x4 slice. The times are simulated.
32 devices in a mesh: grp: 2 (over y), seq: 16 (over z, x, core).
Axes of the slice: x: 2, y: 2, z: 4, core: 2. Of those that a mesh axis runs over, the one named last changes fastest.
Arguments:
- ssm_in: bfloat16 [2048, 4096], P(('grp', 'seq')), parts along dimension 0
- ssm_dt: bfloat16 [2048, 4096], P(('grp', 'seq')), parts along dimension 0, as said below
- ssm_a: float32 [16, 4096], replicated, as said below
- ssm_b: float32 [16, 2048], P(None, ('grp', 'seq')), parts along dimension 1, may hold values from -0.1875 to 0.1875
- ssm_c: float32 [16, 2048], P(None, ('grp', 'seq')), parts along dimension 1, may hold values from -1.5 to 1.5
- attn_q: bfloat16 [2048, 4096], P(('grp', 'seq')), parts along dimension 0
- attn_kv: bfloat16 [2048, 2048], P(('grp', 'seq')), parts along dimension 0
- moe_in: bfloat16 [2048, 4096], P(('grp', 'seq')), parts along dimension 0, may hold values from -6 to 6
- moe_routes: int32 [2048, 2], P(('grp', 'seq')), parts along dimension 0, may hold values from 0 to 15, all different within a row; in each aligned block of 64 rows (0 to 63, 64 to 127, ...) at most 12 rows name the same one
- moe_prob: float32 [2048, 2], P(('grp', 'seq')), parts along dimension 0, may hold values from 0.2 to 1
- w_gate: bfloat16 [4096, 4096], P(None, 'seq'), may hold values from -0.09375 to 0.09375
- w_up: bfloat16 [4096, 4096], P(None, 'seq'), may hold values from -0.09375 to 0.09375
- w_down: bfloat16 [4096, 4096], P('seq'), may hold values from -0.1875 to 0.1875
Outputs:
- ssm_out: bfloat16 [2048, 4096], P(('grp', 'seq')), parts along dimension 0
- attn_out: bfloat16 [2048, 4096], P(('grp', 'seq')), parts along dimension 0
- moe_out: bfloat16 [2048, 4096], P(('grp', 'seq')), parts along dimension 0
There are 2 independent parts, one for each index of `grp`. A program takes and returns all parts, laid end to end along the dimension named above; an argument that names none is the same for every part. Nothing has to cross between parts.
Inputs may be any that keep to these rules, and one draw needn't show every extreme that they name: `moe_routes`: no expert is named by more than 12 positions of one device; a position's two experts differ. `ssm_dt`: Positive. `ssm_a`: Negative.
All inputs are finite; a program needn't handle non-finite values.
Results may differ from a plain program's by a relative error of at most 0.0079.
Values may be sent and summed in bfloat16 or wider, within the bound.
No kernel may reach another device: no remote copies, remote signals or barrier semaphores. Data moves between devices by JAX's collectives and lax.ppermute only.
A program may use at most 192 MiB of HBM per device.

v0:
```python
import math

import jax
import jax.numpy as jnp
from jax import lax
from jax.sharding import PartitionSpec as P

HQ = 32
HK = 8
HEAD_SIZE = 128
EXP_WIN = 4
CAP = 12


def prefix(value, axis, join, neutral):
    count, mine = (lax.axis_size(axis), lax.axis_index(axis))
    pieces = jax.tree.map(lambda part: lax.all_gather(part, axis), value)
    running = jax.tree.map(
        lambda part, zero: jnp.full_like(part, 0) + jnp.asarray(zero, part.dtype), value, neutral
    )

    def hop(position, running):
        longer = join(running, jax.tree.map(lambda part: part[position], pieces))
        return jax.tree.map(lambda new, old: jnp.where(position < mine, new, old), longer, running)

    return lax.fori_loop(0, count - 1, hop, running)


def shifted(value, axis, by):
    devices = lax.axis_size(axis)
    pairs = [(i, i + by) for i in range(devices) if 0 <= i + by < devices]
    return lax.ppermute(value, axis, pairs)


def sweep(initial, values, deltas, rates, inject_rows, read_rows):

    def advance(carried, packet):
        value_row, delta_row, inject_row, read_row = packet
        carried = (
            jnp.exp(delta_row[None, :] * rates) * carried
            + (delta_row * value_row)[None, :] * inject_row[:, None]
        )
        return (carried, jnp.sum(read_row[:, None] * carried, axis=0))

    return lax.scan(advance, initial, (values, deltas, inject_rows.T, read_rows.T), unroll=8)


def chain_join(earlier, later):
    return (earlier[0] * later[0], later[0] * earlier[1] + later[1])


def attend(queries, window, query_pos, key_pos):
    count = queries.shape[0]
    key_count = window.shape[0]
    repeat = HQ // HK
    query_head_tensor = queries.reshape(count, HK, repeat, HEAD_SIZE)
    key_head_tensor = window[:, : HK * HEAD_SIZE].reshape(key_count, HK, HEAD_SIZE)
    value_head_tensor = window[:, HK * HEAD_SIZE :].reshape(key_count, HK, HEAD_SIZE)
    attention_scores = jnp.einsum(
        "bajq,oaq->ajbo", query_head_tensor, key_head_tensor, preferred_element_type=jnp.float32
    ) / math.sqrt(HEAD_SIZE)
    allowed = (key_pos[None, :] >= 0) & (key_pos[None, :] <= query_pos[:, None])
    attention_scores = jnp.where(allowed[None, None], attention_scores, -jnp.inf)
    row_max = jnp.max(attention_scores, axis=-1, keepdims=True)
    expd = jnp.exp(attention_scores - row_max)
    probabilities = (expd / jnp.sum(expd, axis=-1, keepdims=True)).astype(jnp.bfloat16)
    expert_mixture = jnp.einsum(
        "kyje,eku->jkyu", probabilities, value_head_tensor, preferred_element_type=jnp.float32
    )
    return expert_mixture.reshape(count, HQ * HEAD_SIZE).astype(jnp.bfloat16)


def expert_partial(gathered, w_gate, w_up, w_down):
    gate_pre = jnp.dot(gathered, w_gate, preferred_element_type=jnp.float32)
    up_pre = jnp.dot(gathered, w_up, preferred_element_type=jnp.float32)
    hidden_act = (jax.nn.silu(gate_pre) * up_pre).astype(jnp.bfloat16)
    return jnp.dot(hidden_act, w_down, preferred_element_type=jnp.float32).astype(jnp.bfloat16)


def body(
    ssm_in,
    ssm_dt,
    ssm_a,
    ssm_b,
    ssm_c,
    attn_q,
    attn_kv,
    moe_in,
    moe_routes,
    moe_prob,
    w_gate,
    w_up,
    w_down,
):
    values = ssm_in.astype(jnp.float32)
    deltas = ssm_dt.astype(jnp.float32)
    initial = jnp.zeros(ssm_a.shape, jnp.float32)
    local_end, local_read = sweep(initial, values, deltas, ssm_a, ssm_b, ssm_c)
    through = jnp.exp(ssm_a * jnp.sum(deltas, axis=0)[None, :])
    incoming = prefix(
        (through, local_end), "seq", chain_join, (jnp.ones_like(through), jnp.zeros_like(local_end))
    )[1]
    ssm_read = sweep(incoming, values, deltas, ssm_a, ssm_b, ssm_c)[1]
    ssm_out = ssm_read.astype(jnp.bfloat16)
    count = attn_q.shape[0]
    block_index = lax.axis_index("seq")
    nearer = []
    moving = attn_kv
    for hop_count in range(2):
        moving = shifted(moving, "seq", 1)
        nearer.append(moving)
    one_back = nearer[0]
    two_back = nearer[1]
    window = jnp.concatenate([two_back, one_back, attn_kv], axis=0)
    first_row = block_index * count
    query_pos = first_row + jnp.arange(count, dtype=jnp.int32)
    key_pos = first_row - 2 * count + jnp.arange(3 * count, dtype=jnp.int32)
    attn_out = attend(attn_q, window, query_pos, key_pos)
    stream = (
        moe_in.astype(jnp.float32) + ssm_out.astype(jnp.float32) + attn_out.astype(jnp.float32)
    ).astype(jnp.bfloat16)
    local_tokens = stream.shape[0]
    width = stream.shape[1]
    seq_count = lax.axis_size("seq")
    group = seq_count // EXP_WIN
    expert_ids = jnp.arange(EXP_WIN, dtype=jnp.int32)
    matches = moe_routes[:, :, None] == expert_ids[None, None, :]
    routed = jnp.any(matches, axis=1).astype(jnp.int32)
    route_share = jnp.sum(jnp.where(matches, moe_prob[:, :, None], 0.0), axis=1)
    position_rank = jnp.cumsum(routed, axis=0) - 1
    picker = (routed[:, :, None] == 1) & (
        position_rank[:, :, None] == jnp.arange(CAP, dtype=jnp.int32)[None, None, :]
    )
    packed = jnp.einsum(
        "tek,td->ekd", picker.astype(jnp.bfloat16), stream, preferred_element_type=jnp.float32
    ).astype(jnp.bfloat16)
    outgoing = jnp.repeat(packed, group, axis=0)
    arrived = lax.all_to_all(outgoing, "seq", split_axis=0, concat_axis=0, tiled=True)
    gathered = arrived.reshape(-1, arrived.shape[-1])
    partial_value = expert_partial(gathered, w_gate, w_up, w_down)
    returned = lax.all_to_all(
        partial_value.reshape(arrived.shape), "seq", split_axis=0, concat_axis=0, tiled=True
    )
    summed = jnp.sum(returned.reshape(EXP_WIN, group, CAP, width), axis=1, dtype=jnp.float32)
    weighting = (picker.astype(jnp.float32) * route_share[:, :, None]).reshape(
        local_tokens, EXP_WIN * CAP
    )
    combined = jnp.dot(
        weighting,
        summed.reshape(EXP_WIN * CAP, width),
        precision=lax.Precision.HIGHEST,
        preferred_element_type=jnp.float32,
    )
    moe_out = combined.astype(jnp.bfloat16)
    return (ssm_out, attn_out, moe_out)


def solution(mesh):
    return jax.shard_map(
        body,
        mesh=mesh,
        in_specs=(
            P(("grp", "seq"), None),
            P(("grp", "seq"), None),
            P(),
            P(None, ("grp", "seq")),
            P(None, ("grp", "seq")),
            P(("grp", "seq"), None),
            P(("grp", "seq"), None),
            P(("grp", "seq"), None),
            P(("grp", "seq"), None),
            P(("grp", "seq"), None),
            P(None, "seq"),
            P(None, "seq"),
            P("seq", None),
        ),
        out_specs=(P(("grp", "seq"), None), P(("grp", "seq"), None), P(("grp", "seq"), None)),
        check_vma=False,
    )
```

profile of v0, /device:TPU:11, one launch (start us, length us, event | category | flops | bytes accessed | tf_op | source)
XLA Modules:
  0.0 310.0 jit_solution(17598267097898350852)
XLA Ops:
  13.7 24.4 %while.38 = (s32[]{:T(128)}, f32[16,4096]{1,0:T(8,128)S(1)}, f32[8,8,4096]{2,1,0:T(8,128)}, f32[16,4096]{1,0:T(8,128)S(1)}, f32[8,8,4096]{2,1,0:T(8,128)}, /*ind...) while((s32[]{:T(128)}, f32[16,4096]{1,0:T(8,128)S(1)}, ...), condition=%wide.region_2.3_spmd.clone, body=%wide.region_1.2_spmd.clone.sunk | while | flops 2195466 | bytes 1968919 | solution.py:45
  13.7 2.3 constant_dynamic-slice_fusion.42
  16.6 2.3 constant_dynamic-slice_fusion.42
  19.6 2.6 constant_dynamic-slice_fusion.42
  22.8 2.3 constant_dynamic-slice_fusion.42
  25.7 2.3 constant_dynamic-slice_fusion.42
  28.7 2.9 constant_dynamic-slice_fusion.42
  32.2 2.3 constant_dynamic-slice_fusion.42
  35.1 2.5 constant_dynamic-slice_fusion.42
  38.9 3.7 %collective-permute-start = (bf16[64,2048]{1,0:T(8,128)(2,1)}, bf16[64,2048]{1,0:T(8,128)(2,1)S(1)}, u32[]{:S(2)}, u32[]{:S(2)}) collective-permute-start(bf16[64,2048]{1,0:T(8,128)(2,1)} %param.25), channel_id=1, source_target_pairs={{0,1},{1,2},{2,3},{3,4},{4,5},{5,6},{6,7},{7,8},{8,9},{9,10},{10,1... | collective-permute-start | bytes 786440 | tf_op jit(solution)/shard_map/ppermute | solution.py:32
  42.9 9.7 %collective-permute-done = bf16[64,2048]{1,0:T(8,128)(2,1)S(1)} collective-permute-done((bf16[64,2048]{1,0:T(8,128)(2,1)}, bf16[64,2048]{1,0:T(8,128)(2,1)S(1)}, u32[]{:S(2)}, u32[]{:S(2)}) %collective-permute-start) | collective-permute-done | bytes 262176 | tf_op jit(solution)/shard_map/ppermute | solution.py:32
  52.6 5.3 %collective-permute-start.1 = (bf16[64,2048]{1,0:T(8,128)(2,1)S(1)}, bf16[64,2048]{1,0:T(8,128)(2,1)}, u32[]{:S(2)}, u32[]{:S(2)}) collective-permute-start(bf16[64,2048]{1,0:T(8,128)(2,1)S(1)} %collective-permute-done), channel_id=1, source_target_pairs={{0,1},{1,2},{2,3},{3,4},{4,5},{5,6},{6,7},{7,8},{8,9},{9,10},{10,1... | collective-permute-start | bytes 786440 | tf_op jit(solution)/shard_map/ppermute | solution.py:32
  60.6 2.2 collective-permute-done.1
  66.8 3.6 %fusion.63 = (f32[8,4,64]{2,1,0:T(4,128)}, f32[8,4,64,192]{3,2,1,0:T(8,128)}) fusion(pred[64,192]{1,0:T(8,128)(4,1)} %compare_and_fusion, bf16[64,8,4,128]{3,2,1,0:T(4,128)(2,1)S(1)} %copy-done.6, bf16[192,8,128,1]{2,1,0,3:T(8,128)(2,1)S(1)} %bitcast.307), kind=kOutput, calls=%fused_computation.156 | convolution fusion | flops 102236352 | bytes 2510848 | tf_op jit(solution)/shard_map/sub | solution.py:65
  74.1 42.3 %all-gather.7.cloned.1.call-done = f32[256,4096]{1,0:T(8,128)} async-done(((f32[16,4096]{1,0:T(8,128)}), f32[256,4096]{1,0:T(8,128)}) %all-gather.7.cloned.1.call-update) | async-done | bytes 4194320 | tf_op jit(solution)/shard_map/all_gather | solution.py:17
  116.4 19.1 %while.39 = (s32[]{:T(128)}, f32[16,4096]{1,0:T(8,128)S(1)}, s32[]{:T(128)}, f32[16,16,4096]{2,1,0:T(8,128)}, f32[16,16,4096]{2,1,0:T(8,128)}, /*index=5*/s32[]{:T(128)}, s32[]{:T(128)}) while((s32[]{:T(128)}, f32[16,4096]{1,0:T(8,128)S(1)}, s32[]{:T(128)}, f32[16,16,4096]{2,1,0:T(8,128)}, f32[16,16,4096]{2,1,0:T(8,128)}, ...), condition=%wide.region_4.5_spmd.clone, body=%wide.region_3.4_spmd.clone.sunk | while | flops 262148 | bytes 1048685 | solution.py:26
  135.5 42.8 %while.37 = (s32[]{:T(128)}, f32[16,4096]{1,0:T(8,128)S(1)}, bf16[8,8,4096]{2,1,0:T(8,128)(2,1)}, f32[8,8,4096]{2,1,0:T(8,128)}, f32[16,4096]{1,0:T(8,128)S(1)},...) while((s32[]{:T(128)}, f32[16,4096]{1,0:T(8,128)S(1)}, ...), condition=%wide.region_14.15_spmd, body=%wide.region_5.14_spmd.sunk | while | flops 4718601 | bytes 3937953 | solution.py:45
  136.3 2.3 constant_dynamic-slice_fusion.40
  141.5 2.3 constant_dynamic-slice_fusion.40
  146.7 2.6 constant_dynamic-slice_fusion.40
  152.2 2.3 constant_dynamic-slice_fusion.40
  157.5 2.3 constant_dynamic-slice_fusion.40
  162.7 2.9 constant_dynamic-slice_fusion.40
  168.5 2.3 constant_dynamic-slice_fusion.40
  173.7 2.5 constant_dynamic-slice_fusion.40
  180.1 51.8 %all_to_all.10 = bf16[16,12,4096]{2,1,0:T(8,128)(2,1)} all-to-all(bf16[16,12,4096]{2,1,0:T(8,128)(2,1)S(1)} %bitcast.240), channel_id=1, replica_groups=mesh['grp'=2,'seq'=16] {'seq'}, dimensions={0} | all-to-all | bytes 3145728 | tf_op jit(solution)/shard_map/all_to_all | solution.py:138
  231.9 3.6 %reshape.430 = bf16[192,4096]{1,0:T(8,128)(2,1)} reshape(bf16[16,12,4096]{2,1,0:T(8,128)(2,1)} %all_to_all.10) | data formatting | bytes 3145728 | tf_op jit(solution)/shard_map/reshape | solution.py:139
  235.5 2.6 fusion.68
  238.2 5.1 %convolution_convert_fusion = bf16[192,4096]{1,0:T(8,128)(2,1)} fusion(bf16[256,4096]{1,0:T(8,128)(2,1)S(1)} %copy-done, bf16[192,4096]{1,0:T(8,128)(2,1)} %reshape.430, bf16[4096,256]{1,0:T(8,128)(2,1)} %param.30, f32[192,256]{1,0:T(8,128)S(1)} %fusion.68), kind=kOutput, calls=%fused_computation.96 | convolution fusion | flops 806387712 | bytes 7536640 | tf_op jit(solution)/shard_map/dot_general | solution.py:77
  243.3 3.4 %reshape.431 = bf16[16,12,4096]{2,1,0:T(8,128)(2,1)} reshape(bf16[192,4096]{1,0:T(8,128)(2,1)} %convolution_convert_fusion) | data formatting | bytes 3145728 | tf_op jit(solution)/shard_map/reshape | solution.py:142
  246.7 5.1 %all-to-all-start.1 = ((bf16[16,12,4096]{2,1,0:T(8,128)(2,1)}), bf16[16,12,4096]{2,1,0:T(8,128)(2,1)}, u32[]{:S(2)}, u32[]{:S(2)}) async-start(bf16[16,12,4096]{2,1,0:T(8,128)(2,1)} %reshape.431), calls=%async_computation.1 | async-start | bytes 4194304 | tf_op jit(solution)/shard_map/all_to_all | solution.py:141
  251.8 47.5 %all-to-all-done.1 = bf16[16,12,4096]{2,1,0:T(8,128)(2,1)} async-done(((bf16[16,12,4096]{2,1,0:T(8,128)(2,1)}), bf16[16,12,4096]{2,1,0:T(8,128)(2,1)}, u32[]{:S(2)}, u32[]{:S(2)}) %all-to-all-start.1) | async-done | bytes 1572896 | tf_op jit(solution)/shard_map/all_to_all | solution.py:141
  (296 shorter events, 68.7 us)
Async XLA Ops:
  7.2 231.0 %copy-start = (bf16[256,4096]{1,0:T(8,128)(2,1)S(1)}, bf16[256,4096]{1,0:T(8,128)(2,1)}, u32[]{:S(2)}) copy-start(bf16[256,4096]{1,0:T(8,128)(2,1)} %param.31) | copy-start | bytes 6291460
  7.2 5.3 %copy-start.4 = (bf16[64,4096]{1,0:T(8,128)(2,1)S(1)}, bf16[64,4096]{1,0:T(8,128)(2,1)}, u32[]{:S(2)}) copy-start(bf16[64,4096]{1,0:T(8,128)(2,1)} %param.19) | copy-start | bytes 1572868
  7.2 67.0 %all-gather.5.cloned.1.call-start = ((), (), s32[]{:S(2)}) async-start(), calls=%async_computation.2 | async-start | bytes 4456448 | tf_op jit(solution)/shard_map/all_gather | solution.py:17
  8.6 5.0 %copy-start.9 = (f32[16,64]{1,0:T(8,128)S(1)}, f32[16,64]{1,0:T(8,128)}, u32[]{:S(2)}) copy-start(f32[16,64]{1,0:T(8,128)} %param.22) | copy-start | bytes 12292
  8.6 5.1 %copy-start.1 = (f32[16,4096]{1,0:T(8,128)S(1)}, f32[16,4096]{1,0:T(8,128)}, u32[]{:S(2)}) copy-start(f32[16,4096]{1,0:T(8,128)} %param.21) | copy-start | bytes 786436
  10.4 106.1 %all-gather.7.cloned.1.call-start = ((), (), s32[]{:S(2)}) async-start(), calls=%async_computation.3 | async-start | bytes 4456448 | tf_op jit(solution)/shard_map/all_gather | solution.py:17
  13.7 29.0 %copy-start.11 = (s32[64,2]{0,1:T(2,128)S(1)}, s32[64,2]{0,1:T(2,128)}, u32[]{:S(2)}) copy-start(s32[64,2]{0,1:T(2,128)} %param.27) | copy-start | bytes 1540
  13.7 44.3 %copy-start.10 = (f32[16,64]{1,0:T(8,128)S(1)}, f32[16,64]{1,0:T(8,128)}, u32[]{:S(2)}) copy-start(f32[16,64]{1,0:T(8,128)} %param.23) | copy-start | bytes 12292
  13.7 45.0 %copy-start.5 = (bf16[64,4096]{1,0:T(8,128)(2,1)S(1)}, bf16[64,4096]{1,0:T(8,128)(2,1)}, u32[]{:S(2)}) copy-start(bf16[64,4096]{1,0:T(8,128)(2,1)} %param.24) | copy-start | bytes 1572868
  38.1 0.7 copy-start.2
  38.1 27.7 %copy-start.8 = (f32[8,8,16]{2,1,0:T(8,128)}, f32[8,8,16]{2,1,0:T(8,128)S(1)}, u32[]{:S(2)}) copy-start(f32[8,8,16]{2,1,0:T(8,128)S(1)} %get-tuple-element.727) | copy-start | bytes 12292
  38.9 13.7 %collective-permute-start = (bf16[64,2048]{1,0:T(8,128)(2,1)}, bf16[64,2048]{1,0:T(8,128)(2,1)S(1)}, u32[]{:S(2)}, u32[]{:S(2)}) collective-permute-start(bf16[64,2048]{1,0:T(8,128)(2,1)} %param.25), channel_id=1, source_target_pairs={{0,1},{1,2},{2,3},{3,4},{4,5},{5,6},{6,7},{7,8},{8,9},{9,10},{10,1... | collective-permute-start | bytes 786440 | tf_op jit(solution)/shard_map/ppermute | solution.py:32
  52.6 10.2 %copy-start.7 = (bf16[64,2048]{1,0:T(8,128)(2,1)}, bf16[64,2048]{1,0:T(8,128)(2,1)S(1)}, u32[]{:S(2)}) copy-start(bf16[64,2048]{1,0:T(8,128)(2,1)S(1)} %collective-permute-done) | copy-start | bytes 786436
  52.6 10.2 %collective-permute-start.1 = (bf16[64,2048]{1,0:T(8,128)(2,1)S(1)}, bf16[64,2048]{1,0:T(8,128)(2,1)}, u32[]{:S(2)}, u32[]{:S(2)}) collective-permute-start(bf16[64,2048]{1,0:T(8,128)(2,1)S(1)} %collective-permute-done), channel_id=1, source_target_pairs={{0,1},{1,2},{2,3},{3,4},{4,5},{5,6},{6,7},{7,8},{8,9},{9,10},{10,1... | collective-permute-start | bytes 786440 | tf_op jit(solution)/shard_map/ppermute | solution.py:32
  63.8 3.0 copy-start.6
  135.5 42.8 %copy-start.3 = (bf16[64,4096]{1,0:T(8,128)(2,1)S(1)}, bf16[64,4096]{1,0:T(8,128)(2,1)}, u32[]{:S(2)}) copy-start(bf16[64,4096]{1,0:T(8,128)(2,1)} %convert_element_type.71) | copy-start | bytes 1572868
  246.7 5.1 %copy-start.12 = (f32[64,2]{0,1:T(2,128)S(1)}, f32[64,2]{0,1:T(2,128)}, u32[]{:S(2)}) copy-start(f32[64,2]{0,1:T(2,128)} %param.28) | copy-start | bytes 1540
  246.7 52.6 %all-to-all-start.1 = ((bf16[16,12,4096]{2,1,0:T(8,128)(2,1)}), bf16[16,12,4096]{2,1,0:T(8,128)(2,1)}, u32[]{:S(2)}, u32[]{:S(2)}) async-start(bf16[16,12,4096]{2,1,0:T(8,128)(2,1)} %reshape.431), calls=%async_computation.1 | async-start | bytes 4194304 | tf_op jit(solution)/shard_map/all_to_all | solution.py:141
Sparse Core Ops, SparseCore 0:
  10.5 54.0 all-gather.4
  66.7 49.6 all-gather.6
where the time goes:
time: 312 us; the launch traced here: 310 us
  waiting for transfers between devices  102 us (33%)
  local copies, waits for them, and re-layouts  67 us (21%)
  blocking collectives  51.8 us (17%)
  other arithmetic  42 us (13%)
  matrix products  16.9 us (5%)
  between operations  14.3 us (5%)
  starting transfers between devices  14.2 us (5%)
    all_to_all x1, blocking collectives, body(): lax.all_to_all(outgoing, 'seq', split_axis=0, concat_axis=0, tiled=True)  51.8 us
    all_to_all x1, waiting for transfers between devices, body(): lax.all_to_all(partial_value.reshape(arrived.shape), 'seq', split_axis=0,...  47.5 us
    all_gather x2, waiting for transfers between devices, prefix(): pieces = jax.tree.map(lambda part: lax.all_gather(part, axis), value)  42.3 us
    slice x16, local copies, waits for them, and re-layouts, sweep(): lax.scan(advance, initial, (values, deltas, inject_rows.T, read_rows.T),...  38.9 us
    select_n x15, other arithmetic, hop(): jnp.where(position < mine, new, old)  18.7 us
    ppermute x2, waiting for transfers between devices, shifted(): return lax.ppermute(value, axis, pairs)  11.9 us
    reduce_sum x24, other arithmetic, advance(): return (carried, jnp.sum(read_row[:, None] * carried, axis=0))  9.73 us
    ppermute x2, starting transfers between devices, shifted(): return lax.ppermute(value, axis, pairs)  9.09 us
  transfers between devices with their start and end apart: 5, of which 4 were waited for; matrix products, arithmetic and copies ran while one was open for 13% of the time, Pallas kernels for 0%

commit v1 on v0

--- a/solution.py
+++ b/solution.py
@@ -43,6 +43,23 @@
         return (carried, jnp.sum(read_row[:, None] * carried, axis=0))
 
     return lax.scan(advance, initial, (values, deltas, inject_rows.T, read_rows.T), unroll=8)
+
+
+def ssm_correct(local_read, local_end, deltas, rates, read_rows):
+    mine = lax.axis_index("seq")
+    running = jnp.cumsum(deltas, axis=0)
+    ends = lax.all_gather(local_end, "seq")
+    sums = lax.all_gather(running[-1], "seq")
+    devices = sums.shape[0]
+    order = jnp.arange(devices, dtype=jnp.int32)
+    masked = jnp.where((order < mine)[:, None], sums, 0.0)
+    after = jnp.sum(masked, axis=0)[None, :] - jnp.cumsum(masked, axis=0)
+    after = jnp.maximum(after, 0.0)
+    carry = jnp.exp(rates[None] * after[:, None, :]) * ends
+    incoming = jnp.sum(jnp.where((order < mine)[:, None, None], carry, 0.0), axis=0)
+    growth = jnp.exp(rates[None] * running[:, None, :]) * incoming[None]
+    fix = jnp.sum(read_rows.T[:, :, None] * growth, axis=1)
+    return (local_read + fix).astype(jnp.bfloat16)
 
 
 def chain_join(earlier, later):
@@ -96,21 +113,11 @@
     deltas = ssm_dt.astype(jnp.float32)
     initial = jnp.zeros(ssm_a.shape, jnp.float32)
     local_end, local_read = sweep(initial, values, deltas, ssm_a, ssm_b, ssm_c)
-    through = jnp.exp(ssm_a * jnp.sum(deltas, axis=0)[None, :])
-    incoming = prefix(
-        (through, local_end), "seq", chain_join, (jnp.ones_like(through), jnp.zeros_like(local_end))
-    )[1]
-    ssm_read = sweep(incoming, values, deltas, ssm_a, ssm_b, ssm_c)[1]
-    ssm_out = ssm_read.astype(jnp.bfloat16)
+    ssm_out = ssm_correct(local_read, local_end, deltas, ssm_a, ssm_c)
     count = attn_q.shape[0]
     block_index = lax.axis_index("seq")
-    nearer = []
-    moving = attn_kv
-    for hop_count in range(2):
-        moving = shifted(moving, "seq", 1)
-        nearer.append(moving)
-    one_back = nearer[0]
-    two_back = nearer[1]
+    one_back = shifted(attn_kv, "seq", 1)
+    two_back = shifted(attn_kv, "seq", 2)
     window = jnp.concatenate([two_back, one_back, attn_kv], axis=0)
     first_row = block_index * count
     query_pos = first_row + jnp.arange(count, dtype=jnp.int32)

time: 312 us -> 244 us (0.78)
  waiting for transfers between devices: 102 us -> 58.7 us
  local copies, waits for them, and re-layouts: 67 us -> 44.3 us
  blocking collectives: 51.8 us -> 69.9 us
  other arithmetic: 42 us -> 27.3 us
    all_gather x2 -> x1, waiting for transfers between devices: 42.3 us -> 11.2 us  [ssm_correct(): ends = lax.all_gather(local_end, 'seq')]
    slice x16 -> x8, local copies, waits for them, and re-layouts: 38.9 us -> 19.2 us  [sweep(): lax.scan(advance, initial, (values, deltas, inject_rows.T, read_rows.T),...]
    select_n x15 -> x0, other arithmetic: 18.7 us -> none  [hop(): jnp.where(position < mine, new, old)]
    all_gather x0 -> x1, blocking collectives: none -> 18.1 us  [ssm_correct(): sums = lax.all_gather(running[-1], 'seq')]
    ppermute x2, waiting for transfers between devices: 11.9 us -> 0.01 us  [shifted(): return lax.ppermute(value, axis, pairs)]
    reduce_sum x1 -> x3, other arithmetic: 1.32 us -> 8.65 us  [the longest x1 5.35 us: ssm_correct(): fix = jnp.sum(read_rows.T[:, :, None] * growth, axis=1)]
    dynamic_slice x16 -> x8, local copies, waits for them, and re-layouts: 5.69 us -> 0.02 us  [sweep(): lax.scan(advance, initial, (values, deltas, inject_rows.T, read_rows.T),...]
    add x8 -> x0, other arithmetic: 3.62 us -> none  [advance(): jnp.exp(delta_row[None, :] * rates) * carried]
  transfers between devices with their start and end apart: 5 -> 4, of which waited for: 4 -> 2; matrix products, arithmetic and copies ran while one was open for 13% -> 7% of each run, Pallas kernels for 0% -> 0%
where the time goes in v1:
time: 244 us; the launch traced here: 243 us
  blocking collectives  69.9 us (29%)
  waiting for transfers between devices  58.7 us (24%)
  local copies, waits for them, and re-layouts  44.3 us (18%)
  other arithmetic  27.3 us (11%)
  matrix products  15.4 us (6%)
  between operations  14.4 us (6%)
  starting transfers between devices  12.2 us (5%)
    all_to_all x1, blocking collectives, body(): lax.all_to_all(outgoing, 'seq', split_axis=0, concat_axis=0, tiled=True)  51.8 us
    all_to_all x1, waiting for transfers between devices, body(): lax.all_to_all(partial_value.reshape(arrived.shape), 'seq', split_axis=0,...  47.5 us
    slice x8, local copies, waits for them, and re-layouts, sweep(): lax.scan(advance, initial, (values, deltas, inject_rows.T, read_rows.T),...  19.2 us
    all_gather x1, blocking collectives, ssm_correct(): sums = lax.all_gather(running[-1], 'seq')  18.1 us
    all_gather x1, waiting for transfers between devices, ssm_correct(): ends = lax.all_gather(local_end, 'seq')  11.2 us
    reduce_sum x24, other arithmetic, advance(): return (carried, jnp.sum(read_row[:, None] * carried, axis=0))  9.28 us
    ppermute x2, starting transfers between devices, shifted(): return lax.ppermute(value, axis, pairs)  7.14 us
    unnamed x36, local copies, waits for them, and re-layouts  6.72 us
  transfers between devices with their start and end apart: 4, of which 2 were waited for; matrix products, arithmetic and copies ran while one was open for 7% of the time, Pallas kernels for 0%

profile of v1, /device:TPU:11, one launch (start us, length us, event | category | flops | bytes accessed | tf_op | source)
XLA Modules:
  0.0 243.2 jit_solution(3421550089307953260)
XLA Ops:
  7.3 2.2 convert_bitcast_fusion
  9.5 2.1 bitcast_convert_fusion
  11.9 37.0 %while.13 = (s32[]{:T(128)}, f32[16,4096]{1,0:T(8,128)S(1)}, f32[8,8,4096]{2,1,0:T(8,128)}, f32[8,8,4096]{2,1,0:T(8,128)}, f32[16,4096]{1,0:T(8,128)S(1)}, /*ind...) while((s32[]{:T(128)}, f32[16,4096]{1,0:T(8,128)S(1)}, ...), condition=%wide.region_9.10_spmd.clone, body=%wide.region_0.9_spmd.clone.sunk | while | flops 4587530 | bytes 5150316 | solution.py:45
  11.9 2.1 constant_dynamic-slice_fusion.21
  16.2 2.6 %constant_dynamic-slice_fusion.21 = (f32[1,1,4096]{2,1,0:T(1,128)S(1)}, f32[1,1,4096]{2,1,0:T(1,128)S(1)}, f32[1,1,4096]{2,1,0:T(1,128)S(1)}, f32[1,1,4096]{2,1,...) fusion(f32[8,8,4096]{2,1,0:T(8,128)} %get-tuple-element.330, ...), kind=kLoop, calls=%fused_computation.24.clone.1 | loop fusion | bytes 524320 | tf_op jit(solution)/shard_map/while/body/slice | solution.py:45
  21.1 2.3 constant_dynamic-slice_fusion.21
  25.6 2.3 constant_dynamic-slice_fusion.21
  30.2 2.6 %constant_dynamic-slice_fusion.21 = (f32[1,1,4096]{2,1,0:T(1,128)S(1)}, f32[1,1,4096]{2,1,0:T(1,128)S(1)}, f32[1,1,4096]{2,1,0:T(1,128)S(1)}, f32[1,1,4096]{2,1,...) fusion(f32[8,8,4096]{2,1,0:T(8,128)} %get-tuple-element.330, ...), kind=kLoop, calls=%fused_computation.24.clone.1 | loop fusion | bytes 524320 | tf_op jit(solution)/shard_map/while/body/slice | solution.py:45
  35.0 2.3 constant_dynamic-slice_fusion.21
  39.5 2.4 constant_dynamic-slice_fusion.21
  44.1 2.5 %constant_dynamic-slice_fusion.21 = (f32[1,1,4096]{2,1,0:T(1,128)S(1)}, f32[1,1,4096]{2,1,0:T(1,128)S(1)}, f32[1,1,4096]{2,1,0:T(1,128)S(1)}, f32[1,1,4096]{2,1,...) fusion(f32[8,8,4096]{2,1,0:T(8,128)} %get-tuple-element.330, ...), kind=kLoop, calls=%fused_computation.24.clone.1 | loop fusion | bytes 524320 | tf_op jit(solution)/shard_map/while/body/slice | solution.py:45
  49.6 3.2 %collective-permute-start = (bf16[64,2048]{1,0:T(8,128)(2,1)}, bf16[64,2048]{1,0:T(8,128)(2,1)}, u32[]{:S(2)}, u32[]{:S(2)}) collective-permute-start(bf16[64,2048]{1,0:T(8,128)(2,1)} %param.21), channel_id=1, source_target_pairs={{0,2},{1,3},{2,4},{3,5},{4,6},{5,7},{6,8},{7,9},{8,10},{9,11},{10,... | collective-permute-start | bytes 786440 | tf_op jit(solution)/shard_map/ppermute | solution.py:32
  52.8 4.0 %collective-permute-start.1 = (bf16[64,2048]{1,0:T(8,128)(2,1)}, bf16[64,2048]{1,0:T(8,128)(2,1)}, u32[]{:S(2)}, u32[]{:S(2)}) collective-permute-start(bf16[64,2048]{1,0:T(8,128)(2,1)} %param.21), channel_id=1, source_target_pairs={{0,1},{1,2},{2,3},{3,4},{4,5},{5,6},{6,7},{7,8},{8,9},{9,10},{10,1... | collective-permute-start | bytes 786440 | tf_op jit(solution)/shard_map/ppermute | solution.py:32
  56.7 1.9 reduce_window_sum.33
  59.6 18.1 %all-gather.1 = f32[16,1,4096]{2,1,0:T(1,128)S(1)} all-gather(f32[1,1,4096]{2,1,0:T(1,128)S(1)} %slice_bitcast_fusion.18), channel_id=1, replica_groups=mesh['grp'=2,'seq'=16] {'seq'}, dimensions={0}, use_global_device_ids=true | all-gather | bytes 278528 | tf_op jit(solution)/shard_map/all_gather | solution.py:52
  78.6 1.2 reshape.321
  80.8 1.0 constant_dynamic-update-slice_fusion.1
  84.5 3.3 %fusion.50 = (f32[8,4,64]{2,1,0:T(4,128)S(1)}, f32[8,4,64,192]{3,2,1,0:T(8,128)}) fusion(pred[64,192]{1,0:T(8,128)(4,1)S(1)} %compare_and_fusion, bf16[64,8,4,128]{3,2,1,0:T(4,128)(2,1)S(1)} %copy-done.9, bf16[192,8,128,1]{2,1,0,3:T(8,128)(2,1)} %bitcast.206), kind=kOutput, calls=%fused_computation.119 | convolution fusion | flops 102236352 | bytes 2510848 | tf_op jit(solution)/shard_map/sub | solution.py:82
  87.8 2.2 fusion.4
  90.4 1.2 convert_element_type.67
  91.6 11.2 %all-gather.4.cloned.1.call-done = f32[256,4096]{1,0:T(8,128)} async-done(((f32[16,4096]{1,0:T(8,128)}), f32[256,4096]{1,0:T(8,128)}) %all-gather.4.cloned.1.call-update) | async-done | bytes 4194320 | tf_op jit(solution)/shard_map/all_gather | solution.py:51
  102.8 3.1 %select_reduce_fusion = f32[16,4096]{1,0:T(8,128)S(1)} fusion(f32[16,16,4096]{2,1,0:T(8,128)} %bitcast.183, f32[16,4096]{1,0:T(8,128)S(1)} %subtract_maximum_fusion, f32[16,4096]{1,0:T(8,128)S(1)} %get-tuple-element.343, pred[16]{0:T(512)(128)(4,1)S(1)} %iota_compare_fusion.2), kind=kLoop, calls=%fused_computation.59 | loop fusion | flops 4128768 | bytes 4980752 | tf_op jit(solution)/shard_map/reduce_sum | solution.py:59
  105.9 5.3 %multiply_reduce_fusion.8 = f32[64,4096]{1,0:T(8,128)S(1)} fusion(f32[16,4096]{1,0:T(8,128)S(1)} %select_reduce_fusion, f32[64,4096]{1,0:T(8,128)S(1)} %copy-done.6, f32[16,4096]{1,0:T(8,128)S(1)} %get-tuple-element.343, f32[64,16]{1,0:T(8,128)S(1)} %bitcast.209), kind=kLoop, calls=%fused_computation.53 | loop fusion | flops 16515072 | bytes 2625536 | tf_op jit(solution)/shard_map/reduce_sum | solution.py:61
  113.3 51.8 %all_to_all.10 = bf16[16,12,4096]{2,1,0:T(8,128)(2,1)} all-to-all(bf16[16,12,4096]{2,1,0:T(8,128)(2,1)S(1)} %bitcast.167), channel_id=1, replica_groups=mesh['grp'=2,'seq'=16] {'seq'}, dimensions={0} | all-to-all | bytes 3145728 | tf_op jit(solution)/shard_map/all_to_all | solution.py:145
  165.1 3.6 %reshape.323 = bf16[192,4096]{1,0:T(8,128)(2,1)} reshape(bf16[16,12,4096]{2,1,0:T(8,128)(2,1)} %all_to_all.10) | data formatting | bytes 3145728 | tf_op jit(solution)/shard_map/reshape | solution.py:146
  168.7 2.6 %fusion.55 = f32[192,256]{1,0:T(8,128)S(1)} fusion(bf16[192,4096]{1,0:T(8,128)(2,1)} %reshape.323, bf16[4096,256]{1,0:T(8,128)(2,1)} %param.25), kind=kOutput, calls=%fused_computation.120 | convolution fusion | flops 402653184 | bytes 3866624 | tf_op jit(solution)/shard_map/dot_general | solution.py:91
  171.3 5.1 %convolution_convert_fusion = bf16[192,4096]{1,0:T(8,128)(2,1)} fusion(bf16[256,4096]{1,0:T(8,128)(2,1)S(1)} %copy-done, bf16[192,4096]{1,0:T(8,128)(2,1)} %reshape.323, bf16[4096,256]{1,0:T(8,128)(2,1)} %param.26, f32[192,256]{1,0:T(8,128)S(1)} %fusion.55), kind=kOutput, calls=%fused_computation.54 | convolution fusion | flops 806387712 | bytes 7536640 | tf_op jit(solution)/shard_map/dot_general | solution.py:94
  176.4 3.4 %reshape.324 = bf16[16,12,4096]{2,1,0:T(8,128)(2,1)} reshape(bf16[192,4096]{1,0:T(8,128)(2,1)} %convolution_convert_fusion) | data formatting | bytes 3145728 | tf_op jit(solution)/shard_map/reshape | solution.py:149
  179.9 5.0 %all-to-all-start.1 = ((bf16[16,12,4096]{2,1,0:T(8,128)(2,1)}), bf16[16,12,4096]{2,1,0:T(8,128)(2,1)}, u32[]{:S(2)}, u32[]{:S(2)}) async-start(bf16[16,12,4096]{2,1,0:T(8,128)(2,1)} %reshape.324), calls=%async_computation.1 | async-start | bytes 4194304 | tf_op jit(solution)/shard_map/all_to_all | solution.py:148
  184.9 47.5 %all-to-all-done.1 = bf16[16,12,4096]{2,1,0:T(8,128)(2,1)} async-done(((bf16[16,12,4096]{2,1,0:T(8,128)(2,1)}), bf16[16,12,4096]{2,1,0:T(8,128)(2,1)}, u32[]{:S(2)}, u32[]{:S(2)}) %all-to-all-start.1) | async-done | bytes 1572896 | tf_op jit(solution)/shard_map/all_to_all | solution.py:148
  232.4 2.1 convert_reduce_fusion
  234.5 1.8 fusion.2
  (199 shorter events, 25.7 us)
Async XLA Ops:
  7.2 164.2 %copy-start = (bf16[256,4096]{1,0:T(8,128)(2,1)S(1)}, bf16[256,4096]{1,0:T(8,128)(2,1)}, u32[]{:S(2)}) copy-start(bf16[256,4096]{1,0:T(8,128)(2,1)} %param.27) | copy-start | bytes 6291460
  7.2 4.5 %copy-start.11 = (f32[16,64]{1,0:T(8,128)S(1)}, f32[16,64]{1,0:T(8,128)}, u32[]{:S(2)}) copy-start(f32[16,64]{1,0:T(8,128)} %param.18) | copy-start | bytes 12292
  7.2 4.6 %copy-start.12 = (f32[16,64]{1,0:T(8,128)S(1)}, f32[16,64]{1,0:T(8,128)}, u32[]{:S(2)}) copy-start(f32[16,64]{1,0:T(8,128)} %param.19) | copy-start | bytes 12292
  7.2 4.6 %copy-start.1 = (f32[16,4096]{1,0:T(8,128)S(1)}, f32[16,4096]{1,0:T(8,128)}, u32[]{:S(2)}) copy-start(f32[16,4096]{1,0:T(8,128)} %param.17) | copy-start | bytes 786436
  7.2 95.6 %all-gather.4.cloned.1.call-start = ((), (), s32[]{:S(2)}) async-start(), calls=%async_computation.2 | async-start | bytes 4456448 | tf_op jit(solution)/shard_map/all_gather | solution.py:51
  11.8 44.9 %copy-start.3 = (bf16[64,4096]{1,0:T(8,128)(2,1)S(1)}, bf16[64,4096]{1,0:T(8,128)(2,1)}, u32[]{:S(2)}) copy-start(bf16[64,4096]{1,0:T(8,128)(2,1)} %param.16) | copy-start | bytes 1572868
  48.8 0.7 copy-start.2
  48.8 29.3 %copy-start.13 = (s32[64,2]{0,1:T(2,128)S(1)}, s32[64,2]{0,1:T(2,128)}, u32[]{:S(2)}) copy-start(s32[64,2]{0,1:T(2,128)} %param.23) | copy-start | bytes 1540
  49.6 30.2 %collective-permute-start = (bf16[64,2048]{1,0:T(8,128)(2,1)}, bf16[64,2048]{1,0:T(8,128)(2,1)}, u32[]{:S(2)}, u32[]{:S(2)}) collective-permute-start(bf16[64,2048]{1,0:T(8,128)(2,1)} %param.21), channel_id=1, source_target_pairs={{0,2},{1,3},{2,4},{3,5},{4,6},{5,7},{6,8},{7,9},{8,10},{9,11},{10,... | collective-permute-start | bytes 786440 | tf_op jit(solution)/shard_map/ppermute | solution.py:32
  52.8 28.1 %collective-permute-start.1 = (bf16[64,2048]{1,0:T(8,128)(2,1)}, bf16[64,2048]{1,0:T(8,128)(2,1)}, u32[]{:S(2)}, u32[]{:S(2)}) collective-permute-start(bf16[64,2048]{1,0:T(8,128)(2,1)} %param.21), channel_id=1, source_target_pairs={{0,1},{1,2},{2,3},{3,4},{4,5},{5,6},{6,7},{7,8},{8,9},{9,10},{10,1... | collective-permute-start | bytes 786440 | tf_op jit(solution)/shard_map/ppermute | solution.py:32
  58.6 19.9 %copy-start.8 = (bf16[64,4096]{1,0:T(8,128)(2,1)S(1)}, bf16[64,4096]{1,0:T(8,128)(2,1)}, u32[]{:S(2)}) copy-start(bf16[64,4096]{1,0:T(8,128)(2,1)} %param.20) | copy-start | bytes 1572868
  80.8 3.7 %copy-start.9 = (bf16[64,8,4,128]{3,2,1,0:T(4,128)(2,1)S(1)}, bf16[64,8,4,128]{3,2,1,0:T(4,128)(2,1)}, u32[]{:S(2)}) copy-start(bf16[64,8,4,128]{3,2,1,0:T(4,128)(2,1)} %reshape.321) | copy-start | bytes 1572868
  102.8 3.1 %copy-start.6 = (f32[64,4096]{1,0:T(8,128)S(1)}, f32[64,4096]{1,0:T(8,128)}, u32[]{:S(2)}) copy-start(f32[64,4096]{1,0:T(8,128)} %reduce_window_sum.33) | copy-start | bytes 3145732
  105.9 5.4 %copy-start.7 = (f32[8,8,4096]{2,1,0:T(8,128)S(1)}, f32[8,8,4096]{2,1,0:T(8,128)}, u32[]{:S(2)}) copy-start(f32[8,8,4096]{2,1,0:T(8,128)} %get-tuple-element.46) | copy-start | bytes 3145732
  111.3 1.0 copy-start.5
  111.3 1.4 copy-start.10
  111.4 1.8 copy-start.4
  179.9 5.0 %copy-start.14 = (f32[64,2]{0,1:T(2,128)S(1)}, f32[64,2]{0,1:T(2,128)}, u32[]{:S(2)}) copy-start(f32[64,2]{0,1:T(2,128)} %param.24) | copy-start | bytes 1540
  179.9 52.6 %all-to-all-start.1 = ((bf16[16,12,4096]{2,1,0:T(8,128)(2,1)}), bf16[16,12,4096]{2,1,0:T(8,128)(2,1)}, u32[]{:S(2)}, u32[]{:S(2)}) async-start(bf16[16,12,4096]{2,1,0:T(8,128)(2,1)} %reshape.324), calls=%async_computation.1 | async-start | bytes 4194304 | tf_op jit(solution)/shard_map/all_to_all | solution.py:148
Sparse Core Ops, SparseCore 0:
  49.7 53.0 all-gather.3

commit v2 on v1

--- a/solution.py
+++ b/solution.py
@@ -1,33 +1,20 @@
+import functools
 import math
 
 import jax
 import jax.numpy as jnp
 from jax import lax
-from jax.sharding import PartitionSpec as P
+from jax.sharding import Mesh, PartitionSpec as P
 
 HQ = 32
 HK = 8
 HEAD_SIZE = 128
 EXP_WIN = 4
 CAP = 12
+SEQ = ("eg", "kg")
 
 
-def prefix(value, axis, join, neutral):
-    count, mine = (lax.axis_size(axis), lax.axis_index(axis))
-    pieces = jax.tree.map(lambda part: lax.all_gather(part, axis), value)
-    running = jax.tree.map(
-        lambda part, zero: jnp.full_like(part, 0) + jnp.asarray(zero, part.dtype), value, neutral
-    )
-
-    def hop(position, running):
-        longer = join(running, jax.tree.map(lambda part: part[position], pieces))
-        return jax.tree.map(lambda new, old: jnp.where(position < mine, new, old), longer, running)
-
-    return lax.fori_loop(0, count - 1, hop, running)
-
-
-def shifted(value, axis, by):
-    devices = lax.axis_size(axis)
+def shifted(value, axis, by, devices):
     pairs = [(i, i + by) for i in range(devices) if 0 <= i + by < devices]
     return lax.ppermute(value, axis, pairs)
 
@@ -46,10 +33,11 @@
 
 
 def ssm_correct(local_read, local_end, deltas, rates, read_rows):
-    mine = lax.axis_index("seq")
+    mine = lax.axis_index(SEQ)
     running = jnp.cumsum(deltas, axis=0)
-    ends = lax.all_gather(local_end, "seq")
-    sums = lax.all_gather(running[-1], "seq")
+    both = lax.all_gather(jnp.concatenate([local_end, running[-1:]], axis=0), SEQ)
+    ends = both[:, :-1]
+    sums = both[:, -1]
     devices = sums.shape[0]
     order = jnp.arange(devices, dtype=jnp.int32)
     masked = jnp.where((order < mine)[:, None], sums, 0.0)
@@ -60,10 +48,6 @@
     growth = jnp.exp(rates[None] * running[:, None, :]) * incoming[None]
     fix = jnp.sum(read_rows.T[:, :, None] * growth, axis=1)
     return (local_read + fix).astype(jnp.bfloat16)
-
-
-def chain_join(earlier, later):
-    return (earlier[0] * later[0], later[0] * earlier[1] + later[1])
 
 
 def attend(queries, window, query_pos, key_pos):
@@ -108,6 +92,8 @@
     w_gate,
     w_up,
     w_down,
+    *,
+    seq_count,
 ):
     values = ssm_in.astype(jnp.float32)
     deltas = ssm_dt.astype(jnp.float32)
@@ -115,9 +101,9 @@
     local_end, local_read = sweep(initial, values, deltas, ssm_a, ssm_b, ssm_c)
     ssm_out = ssm_correct(local_read, local_end, deltas, ssm_a, ssm_c)
     count = attn_q.shape[0]
-    block_index = lax.axis_index("seq")
-    one_back = shifted(attn_kv, "seq", 1)
-    two_back = shifted(attn_kv, "seq", 2)
+    block_index = lax.axis_index(SEQ)
+    one_back = shifted(attn_kv, SEQ, 1, seq_count)
+    two_back = shifted(attn_kv, SEQ, 2, seq_count)
     window = jnp.concatenate([two_back, one_back, attn_kv], axis=0)
     first_row = block_index * count
     query_pos = first_row + jnp.arange(count, dtype=jnp.int32)
@@ -128,8 +114,6 @@
     ).astype(jnp.bfloat16)
     local_tokens = stream.shape[0]
     width = stream.shape[1]
-    seq_count = lax.axis_size("seq")
-    group = seq_count // EXP_WIN
     expert_ids = jnp.arange(EXP_WIN, dtype=jnp.int32)
     matches = moe_routes[:, :, None] == expert_ids[None, None, :]
     routed = jnp.any(matches, axis=1).astype(jnp.int32)
@@ -141,15 +125,26 @@
     packed = jnp.einsum(
         "tek,td->ekd", picker.astype(jnp.bfloat16), stream, preferred_element_type=jnp.float32
     ).astype(jnp.bfloat16)
-    outgoing = jnp.repeat(packed, group, axis=0)
-    arrived = lax.all_to_all(outgoing, "seq", split_axis=0, concat_axis=0, tiled=True)
-    gathered = arrived.reshape(-1, arrived.shape[-1])
+    own = lax.axis_index("eg")
+    pieces = [lax.dynamic_index_in_dim(packed, own, 0, keepdims=False)]
+    for by in range(1, EXP_WIN):
+        piece = lax.dynamic_index_in_dim(packed, (own + by) % EXP_WIN, 0, keepdims=False)
+        pairs = [(i, (i + by) % EXP_WIN) for i in range(EXP_WIN)]
+        pieces.append(lax.ppermute(piece, "eg", pairs))
+    local_block = jnp.stack(pieces)
+    arrived = lax.all_gather(local_block, "kg")
+    gathered = arrived.reshape(-1, width)
     partial_value = expert_partial(gathered, w_gate, w_up, w_down)
-    returned = lax.all_to_all(
-        partial_value.reshape(arrived.shape), "seq", split_axis=0, concat_axis=0, tiled=True
-    )
-    summed = jnp.sum(returned.reshape(EXP_WIN, group, CAP, width), axis=1, dtype=jnp.float32)
-    weighting = (picker.astype(jnp.float32) * route_share[:, :, None]).reshape(
+    reduced = lax.psum_scatter(
+        partial_value.reshape(arrived.shape).astype(jnp.float32), "kg", scatter_dimension=0, tiled=True
+    )[0]
+    back = [reduced[0]]
+    for by in range(1, EXP_WIN):
+        pairs = [(i, (i - by) % EXP_WIN) for i in range(EXP_WIN)]
+        back.append(lax.ppermute(reduced[by], "eg", pairs))
+    summed = jnp.stack(back)
+    turn = (own + jnp.arange(EXP_WIN, dtype=jnp.int32)) % EXP_WIN
+    weighting = (picker.astype(jnp.float32) * route_share[:, :, None])[:, turn, :].reshape(
         local_tokens, EXP_WIN * CAP
     )
     combined = jnp.dot(
@@ -163,24 +158,30 @@
 
 
 def solution(mesh):
+    groups = mesh.shape["grp"]
+    seq_count = mesh.shape["seq"]
+    fine = Mesh(
+        mesh.devices.reshape(groups, EXP_WIN, seq_count // EXP_WIN), ("grp", "eg", "kg")
+    )
+    rows = P(("grp",) + SEQ, None)
     return jax.shard_map(
-        body,
-        mesh=mesh,
+        functools.partial(body, seq_count=seq_count),
+        mesh=fine,
         in_specs=(
-            P(("grp", "seq"), None),
-            P(("grp", "seq"), None),
+            rows,
+            rows,
             P(),
-            P(None, ("grp", "seq")),
-            P(None, ("grp", "seq")),
-            P(("grp", "seq"), None),
-            P(("grp", "seq"), None),
-            P(("grp", "seq"), None),
-            P(("grp", "seq"), None),
-            P(("grp", "seq"), None),
-            P(None, "seq"),
-            P(None, "seq"),
-            P("seq", None),
+            P(None, ("grp",) + SEQ),
+            P(None, ("grp",) + SEQ),
+            rows,
+            rows,
+            rows,
+            rows,
+            rows,
+            P(None, SEQ),
+            P(None, SEQ),
+            P(SEQ, None),
         ),
-        out_specs=(P(("grp", "seq"), None), P(("grp", "seq"), None), P(("grp", "seq"), None)),
+        out_specs=(rows, rows, rows),
         check_vma=False,
     )

time: 244 us -> 280 us (1.15)
  waiting for transfers between devices: 58.7 us -> 144 us
  blocking collectives: 69.9 us -> 0 us
  local copies, waits for them, and re-layouts: 44.3 us -> 54.2 us
  other arithmetic: 27.3 us -> 33.2 us
    all_to_all x1 -> x0, blocking collectives: 51.8 us -> none  [body(): lax.all_to_all(outgoing, 'seq', split_axis=0, concat_axis=0, tiled=True)]
    all_gather x1 -> x2, waiting for transfers between devices: 11.2 us -> 59.8 us  [the longest x1 37.1 us: ssm_correct(): lax.all_gather(jnp.concatenate([local_end, running[-1:]], axis=0), SEQ)]
    all_to_all x1 -> x0, waiting for transfers between devices: 47.5 us -> none  [body(): lax.all_to_all(partial_value.reshape(arrived.shape), 'seq', split_axis=0,...]
    reduce_scatter x0 -> x1, waiting for transfers between devices: none -> 43.6 us  [body(): lax.psum_scatter(partial_value.reshape(arrived.shape).astype(jnp.float32)...]
    ppermute x0 -> x6, waiting for transfers between devices: none -> 32.1 us  [the longest x3 21.8 us: body(): back.append(lax.ppermute(reduced[by], 'eg', pairs))]
    all_gather x1 -> x0, blocking collectives: 18.1 us -> none  [ssm_correct(): sums = lax.all_gather(running[-1], 'seq')]
    ppermute x2, waiting for transfers between devices: 0.01 us -> 8.42 us  [shifted(): return lax.ppermute(value, axis, pairs)]
    ppermute x0 -> x6, starting transfers between devices: none -> 6.85 us  [the longest x3 3.65 us: body(): back.append(lax.ppermute(reduced[by], 'eg', pairs))]
  transfers between devices with their start and end apart: 4 -> 11, of which waited for: 2 -> 10; matrix products, arithmetic and copies ran while one was open for 7% -> 4% of each run, Pallas kernels for 0% -> 0%
where the time goes in v2:
time: 280 us; the launch traced here: 278 us
  waiting for transfers between devices  144 us (51%)
  local copies, waits for them, and re-layouts  54.2 us (19%)
  other arithmetic  33.2 us (12%)
  matrix products  16.7 us (6%)
  starting transfers between devices  14.3 us (5%)
  between operations  14.1 us (5%)
    reduce_scatter x1, waiting for transfers between devices, body(): lax.psum_scatter(partial_value.reshape(arrived.shape).astype(jnp.float32)...  43.6 us
    all_gather x1, waiting for transfers between devices, ssm_correct(): lax.all_gather(jnp.concatenate([local_end, running[-1:]], axis=0), SEQ)  37.1 us
    all_gather x1, waiting for transfers between devices, body(): arrived = lax.all_gather(local_block, 'kg')  22.7 us
    ppermute x3, waiting for transfers between devices, body(): back.append(lax.ppermute(reduced[by], 'eg', pairs))  21.8 us
    slice x8, local copies, waits for them, and re-layouts, sweep(): lax.scan(advance, initial, (values, deltas, inject_rows.T, read_rows.T),...  19 us
    reduce_sum x24, other arithmetic, advance(): return (carried, jnp.sum(read_row[:, None] * carried, axis=0))  14.5 us
    ppermute x3, waiting for transfers between devices, body(): pieces.append(lax.ppermute(piece, 'eg', pairs))  10.2 us
    ppermute x2, waiting for transfers between devices, shifted(): return lax.ppermute(value, axis, pairs)  8.42 us
  transfers between devices with their start and end apart: 11, of which 10 were waited for; matrix products, arithmetic and copies ran while one was open for 4% of the time, Pallas kernels for 0%

profile of v2, /device:TPU:11, one launch (start us, length us, event | category | flops | bytes accessed | tf_op | source)
XLA Modules:
  0.0 277.6 jit_solution(8505957999368220229)
XLA Ops:
  7.3 3.1 %reduce_window_sum.35 = f32[64,4096]{1,0:T(8,128)} reduce-window(bf16[64,4096]{1,0:T(8,128)(2,1)} %param.16, f32[]{:T(128)} %constant.89.clone.1), window={size=64x1 pad=63_0x0_0}, to_apply=%region_10.11 | reduce-window | flops 16515072 | bytes 1572868 | tf_op jit(solution)/shard_map/jit(cumsum)/reduce_window_sum | solution.py:37
  11.3 2.8 bitcast_convert_fusion
  14.3 51.0 %while.13 = (s32[]{:T(128)}, f32[16,4096]{1,0:T(8,128)S(1)}, f32[8,8,4096]{2,1,0:T(8,128)}, f32[8,8,4096]{2,1,0:T(8,128)}, f32[16,4096]{1,0:T(8,128)S(1)}, /*ind...) while((s32[]{:T(128)}, f32[16,4096]{1,0:T(8,128)S(1)}, ...), condition=%wide.region_9.10_spmd.clone, body=%wide.region_0.9_spmd.clone.sunk | while | flops 4587530 | bytes 5151168 | solution.py:32
  15.4 2.1 constant_dynamic-slice_fusion.22
  21.5 2.6 constant_dynamic-slice_fusion.22
  28.1 2.3 constant_dynamic-slice_fusion.22
  34.4 2.3 constant_dynamic-slice_fusion.22
  40.7 2.5 constant_dynamic-slice_fusion.22
  47.2 2.3 constant_dynamic-slice_fusion.22
  53.5 2.3 constant_dynamic-slice_fusion.22
  59.8 2.5 constant_dynamic-slice_fusion.22
  66.1 3.2 %collective-permute-start = (bf16[64,2048]{1,0:T(8,128)(2,1)}, bf16[64,2048]{1,0:T(8,128)(2,1)S(1)}, u32[]{:S(2)}, u32[]{:S(2)}) collective-permute-start(bf16[64,2048]{1,0:T(8,128)(2,1)} %param.21), channel_id=1, source_target_pairs={{0,2},{1,3},{2,4},{3,5},{4,6},{5,7},{6,8},{7,9},{8,10},{9,11},{10,... | collective-permute-start | bytes 786440 | tf_op jit(solution)/shard_map/ppermute | solution.py:19
  69.3 4.0 %collective-permute-start.1 = (bf16[64,2048]{1,0:T(8,128)(2,1)}, bf16[64,2048]{1,0:T(8,128)(2,1)}, u32[]{:S(2)}, u32[]{:S(2)}) collective-permute-start(bf16[64,2048]{1,0:T(8,128)(2,1)} %param.21), channel_id=1, source_target_pairs={{0,1},{1,2},{2,3},{3,4},{4,5},{5,6},{6,7},{7,8},{8,9},{9,10},{10,1... | collective-permute-start | bytes 786440 | tf_op jit(solution)/shard_map/ppermute | solution.py:19
  76.2 8.4 %collective-permute-done.1 = bf16[64,2048]{1,0:T(8,128)(2,1)} collective-permute-done((bf16[64,2048]{1,0:T(8,128)(2,1)}, bf16[64,2048]{1,0:T(8,128)(2,1)}, u32[]{:S(2)}, u32[]{:S(2)}) %collective-permute-start.1) | collective-permute-done | bytes 262176 | tf_op jit(solution)/shard_map/ppermute | solution.py:19
  86.6 3.0 %fusion.58 = (f32[8,4,64]{2,1,0:T(4,128)S(1)}, f32[8,4,64,192]{3,2,1,0:T(8,128)}) fusion(pred[64,192]{1,0:T(8,128)(4,1)} %compare_and_fusion, bf16[64,8,4,128]{3,2,1,0:T(4,128)(2,1)S(1)} %copy-done.7, bf16[192,8,128,1]{2,1,0,3:T(8,128)(2,1)S(1)} %bitcast.226), kind=kOutput, calls=%fused_computation.143 | convolution fusion | flops 102236352 | bytes 2510848 | tf_op jit(solution)/shard_map/sub | solution.py:66
  89.6 2.2 fusion.7
  93.4 37.1 %all-gather.8.cloned.1.call-done = f32[16,17,4096]{2,1,0:T(8,128)} async-done(((f32[1,17,4096]{2,1,0:T(8,128)}), f32[16,17,4096]{2,1,0:T(8,128)}) %all-gather.8.cloned.1.call-update) | async-done | bytes 4456464 | tf_op jit(solution)/shard_map/all_gather | solution.py:38
  130.4 1.7 slice.206
  132.8 3.1 %fusion.5 = f32[16,4096]{1,0:T(8,128)S(1)} fusion(f32[16,17,4096]{2,1,0:T(8,128)} %all-gather.8.cloned.1.call-done, f32[16,4096]{1,0:T(8,128)S(1)} %subtract_maximum_fusion, f32[16,4096]{1,0:T(8,128)S(1)} %get-tuple-element.353, pred[16]{0:T(512)(128)(4,1)S(1)} %iota_compare_fusion.2), kind=kLoop, calls=%fused_computation.62 | loop fusion | flops 4128768 | bytes 4980752 | tf_op jit(solution)/shard_map/reduce_sum | solution.py:47
  136.0 5.3 %multiply_reduce_fusion.8 = f32[64,4096]{1,0:T(8,128)S(1)} fusion(f32[16,4096]{1,0:T(8,128)S(1)} %fusion.5, f32[64,4096]{1,0:T(8,128)S(1)} %copy-done.4, f32[16,4096]{1,0:T(8,128)S(1)} %get-tuple-element.353, f32[64,16]{1,0:T(8,128)S(1)} %bitcast.232), kind=kLoop, calls=%fused_computation.54 | loop fusion | flops 16515072 | bytes 2625536 | tf_op jit(solution)/shard_map/reduce_sum | solution.py:49
  148.0 5.7 %collective-permute-done.3 = bf16[12,4096]{1,0:T(8,128)(2,1)S(1)} collective-permute-done((bf16[12,4096]{1,0:T(8,128)(2,1)S(1)}, bf16[12,4096]{1,0:T(8,128)(2,1)S(1)}, u32[]{:S(2)}, u32[]{:S(2)}) %collective-permute-start.3) | collective-permute-done | bytes 98336 | tf_op jit(solution)/shard_map/ppermute | solution.py:133
  153.8 2.8 %collective-permute-done.2 = bf16[12,4096]{1,0:T(8,128)(2,1)S(1)} collective-permute-done((bf16[12,4096]{1,0:T(8,128)(2,1)S(1)}, bf16[12,4096]{1,0:T(8,128)(2,1)S(1)}, u32[]{:S(2)}, u32[]{:S(2)}) %collective-permute-start.2) | collective-permute-done | bytes 98336 | tf_op jit(solution)/shard_map/ppermute | solution.py:133
  157.7 22.7 %all-gather.6.cloned.1.call-done = bf16[16,12,4096]{2,1,0:T(8,128)(2,1)} async-done(((bf16[4,12,4096]{2,1,0:T(8,128)(2,1)}), bf16[16,12,4096]{2,1,0:T(8,128)(2,1)}) %all-gather.6.cloned.1.call-update) | async-done | bytes 1572880 | tf_op jit(solution)/shard_map/all_gather | solution.py:135
  180.5 3.6 %reshape.375 = bf16[192,4096]{1,0:T(8,128)(2,1)} reshape(bf16[16,12,4096]{2,1,0:T(8,128)(2,1)} %all-gather.6.cloned.1.call-done) | data formatting | bytes 3145728 | tf_op jit(solution)/shard_map/reshape | solution.py:136
  184.0 2.6 fusion.63
  186.7 5.6 %fusion.2 = f32[192,4096]{1,0:T(8,128)} fusion(bf16[256,4096]{1,0:T(8,128)(2,1)S(1)} %copy-done, bf16[192,4096]{1,0:T(8,128)(2,1)} %reshape.375, bf16[4096,256]{1,0:T(8,128)(2,1)} %param.26, f32[192,256]{1,0:T(8,128)S(1)} %fusion.63), kind=kOutput, calls=%fused_computation.56 | convolution fusion | flops 807174144 | bytes 9109504 | tf_op jit(solution)/shard_map/dot_general | solution.py:78
  192.3 4.3 %reshape.378 = f32[4,4,12,4096]{3,2,1,0:T(8,128)} reshape(f32[192,4096]{1,0:T(8,128)} %fusion.2) | data formatting | bytes 6291456 | tf_op jit(solution)/shard_map/convert_element_type | solution.py:139
  197.3 43.6 %reduce-scatter.2.cloned.1.call-done = f32[1,4,12,4096]{3,2,1,0:T(8,128)} async-done(((f32[4,4,12,4096]{3,2,1,0:T(8,128)}), f32[1,4,12,4096]{3,2,1,0:T(8,128)}) %reduce-scatter.2.cloned.1.call-update) | async-done | bytes 786448 | tf_op jit(solution)/shard_map/reduce_scatter | solution.py:138
  246.3 3.1 %collective-permute-done.7 = f32[12,4096]{1,0:T(8,128)} collective-permute-done((f32[12,4096]{1,0:T(8,128)S(1)}, f32[12,4096]{1,0:T(8,128)}, u32[]{:S(2)}, u32[]{:S(2)}) %collective-permute-start.7) | collective-permute-done | bytes 196640 | tf_op jit(solution)/shard_map/ppermute | solution.py:144
  249.5 15.8 %collective-permute-done.6 = f32[12,4096]{1,0:T(8,128)} collective-permute-done((f32[12,4096]{1,0:T(8,128)S(1)}, f32[12,4096]{1,0:T(8,128)}, u32[]{:S(2)}, u32[]{:S(2)}) %collective-permute-start.6) | collective-permute-done | bytes 196640 | tf_op jit(solution)/shard_map/ppermute | solution.py:144
  265.2 3.0 %collective-permute-done.5 = f32[12,4096]{1,0:T(8,128)} collective-permute-done((f32[12,4096]{1,0:T(8,128)S(1)}, f32[12,4096]{1,0:T(8,128)}, u32[]{:S(2)}, u32[]{:S(2)}) %collective-permute-start.5) | collective-permute-done | bytes 196640 | tf_op jit(solution)/shard_map/ppermute | solution.py:144
  268.2 2.9 %fusion.3 = bf16[64,4096]{1,0:T(8,128)(2,1)} fusion(f32[1,12,4096]{2,1,0:T(8,128)} %bitcast.29, f32[1,12,4096]{2,1,0:T(8,128)} %bitcast.27, f32[1,12,4096]{2,1,0:T(8,128)} %bitcast.25, f32[1,12,4096]{2,1,0:T(8,128)S(1)} %get-tuple-element.144, f32[4,64,12]{1,2,0:T(8,128)S(1)} %gather_fusion), kind=kOutput, calls=%fused_computation.58 | convolution fusion | flops 151846912 | bytes 1323008 | tf_op jit(solution)/shard_map/dot_general | solution.py:150
  (270 shorter events, 53.6 us)
Async XLA Ops:
  7.2 179.5 %copy-start = (bf16[256,4096]{1,0:T(8,128)(2,1)S(1)}, bf16[256,4096]{1,0:T(8,128)(2,1)}, u32[]{:S(2)}) copy-start(bf16[256,4096]{1,0:T(8,128)(2,1)} %param.27) | copy-start | bytes 6291460
  7.2 123.3 %all-gather.8.cloned.1.call-start = ((), (), s32[]{:S(2)}) async-start(), calls=%async_computation.3 | async-start | bytes 6684672 | tf_op jit(solution)/shard_map/all_gather | solution.py:38
  7.2 6.9 %copy-start.15 = (f32[16,64]{1,0:T(8,128)S(1)}, f32[16,64]{1,0:T(8,128)}, u32[]{:S(2)}) copy-start(f32[16,64]{1,0:T(8,128)} %param.18) | copy-start | bytes 12292
  7.3 6.9 %copy-start.16 = (f32[16,64]{1,0:T(8,128)S(1)}, f32[16,64]{1,0:T(8,128)}, u32[]{:S(2)}) copy-start(f32[16,64]{1,0:T(8,128)} %param.19) | copy-start | bytes 12292
  7.3 7.0 %copy-start.1 = (f32[16,4096]{1,0:T(8,128)S(1)}, f32[16,4096]{1,0:T(8,128)}, u32[]{:S(2)}) copy-start(f32[16,4096]{1,0:T(8,128)} %param.17) | copy-start | bytes 786436
  14.3 60.6 %copy-start.6 = (bf16[64,4096]{1,0:T(8,128)(2,1)S(1)}, bf16[64,4096]{1,0:T(8,128)(2,1)}, u32[]{:S(2)}) copy-start(bf16[64,4096]{1,0:T(8,128)(2,1)} %param.20) | copy-start | bytes 1572868
  17.6 1.5 copy-start.12
  17.6 1.5 copy-start.13
  24.2 1.5 copy-start.12
  30.5 1.5 copy-start.12
  36.8 1.5 copy-start.12
  43.3 1.5 copy-start.12
  49.6 1.5 copy-start.12
  56.0 1.5 copy-start.12
  62.5 1.5 copy-start.12
  65.3 8.7 %copy-start.10 = (f32[8,8,16]{2,1,0:T(8,128)}, f32[8,8,16]{2,1,0:T(8,128)S(1)}, u32[]{:S(2)}) copy-start(f32[8,8,16]{2,1,0:T(8,128)S(1)} %get-tuple-element.375) | copy-start | bytes 12292
  66.0 19.5 %copy-start.9 = (bf16[64,2048]{1,0:T(8,128)(2,1)S(1)}, bf16[64,2048]{1,0:T(8,128)(2,1)}, u32[]{:S(2)}) copy-start(bf16[64,2048]{1,0:T(8,128)(2,1)} %param.21) | copy-start | bytes 786436
  66.1 114.4 %all-gather.6.cloned.1.call-start = ((), (), s32[]{:S(2)}) async-start(), calls=%async_computation.2 | async-start | bytes 2621440 | tf_op jit(solution)/shard_map/all_gather | solution.py:135
  66.1 10.0 %collective-permute-start = (bf16[64,2048]{1,0:T(8,128)(2,1)}, bf16[64,2048]{1,0:T(8,128)(2,1)S(1)}, u32[]{:S(2)}, u32[]{:S(2)}) collective-permute-start(bf16[64,2048]{1,0:T(8,128)(2,1)} %param.21), channel_id=1, source_target_pairs={{0,2},{1,3},{2,4},{3,5},{4,6},{5,7},{6,8},{7,9},{8,10},{9,11},{10,... | collective-permute-start | bytes 786440 | tf_op jit(solution)/shard_map/ppermute | solution.py:19
  69.3 15.3 %collective-permute-start.1 = (bf16[64,2048]{1,0:T(8,128)(2,1)}, bf16[64,2048]{1,0:T(8,128)(2,1)}, u32[]{:S(2)}, u32[]{:S(2)}) collective-permute-start(bf16[64,2048]{1,0:T(8,128)(2,1)} %param.21), channel_id=1, source_target_pairs={{0,1},{1,2},{2,3},{3,4},{4,5},{5,6},{6,7},{7,8},{8,9},{9,10},{10,1... | collective-permute-start | bytes 786440 | tf_op jit(solution)/shard_map/ppermute | solution.py:19
  76.2 10.4 %copy-start.7 = (bf16[64,8,4,128]{3,2,1,0:T(4,128)(2,1)S(1)}, bf16[64,8,4,128]{3,2,1,0:T(4,128)(2,1)}, u32[]{:S(2)}) copy-start(bf16[64,8,4,128]{3,2,1,0:T(4,128)(2,1)} %reshape.374) | copy-start | bytes 1572868
  132.8 3.1 %copy-start.4 = (f32[64,4096]{1,0:T(8,128)S(1)}, f32[64,4096]{1,0:T(8,128)}, u32[]{:S(2)}) copy-start(f32[64,4096]{1,0:T(8,128)} %reduce_window_sum.35) | copy-start | bytes 3145732
  132.8 3.1 %copy-start.11 = (f32[8,8,16]{2,1,0:T(8,128)S(1)}, f32[8,8,16]{2,1,0:T(8,128)}, u32[]{:S(2)}) copy-start(f32[8,8,16]{2,1,0:T(8,128)} %copy-done.10) | copy-start | bytes 12292
  136.0 5.4 %copy-start.5 = (f32[8,8,4096]{2,1,0:T(8,128)S(1)}, f32[8,8,4096]{2,1,0:T(8,128)}, u32[]{:S(2)}) copy-start(f32[8,8,4096]{2,1,0:T(8,128)} %get-tuple-element.46) | copy-start | bytes 3145732
  141.5 16.0 %copy-start.2 = (bf16[64,4096]{1,0:T(8,128)(2,1)}, bf16[64,4096]{1,0:T(8,128)(2,1)S(1)}, u32[]{:S(2)}) copy-start(bf16[64,4096]{1,0:T(8,128)(2,1)S(1)} %fusion.16) | copy-start | bytes 1572868
  143.1 4.9 %collective-permute-start.4 = (bf16[12,4096]{1,0:T(8,128)(2,1)S(1)}, bf16[12,4096]{1,0:T(8,128)(2,1)S(1)}, u32[]{:S(2)}, u32[]{:S(2)}) collective-permute-start(bf16[12,4096]{1,0:T(8,128)(2,1)S(1)} %get-tuple-element.151), channel_id=1, source_target_pairs={{0,12},{4,0},{8,4},{12,8},{1,13},{5,1},{9,5},{13,9},{2,14},{6,2},{... | collective-permute-start | bytes 294920 | tf_op jit(solution)/shard_map/ppermute | solution.py:133
  143.5 10.3 %collective-permute-start.3 = (bf16[12,4096]{1,0:T(8,128)(2,1)S(1)}, bf16[12,4096]{1,0:T(8,128)(2,1)S(1)}, u32[]{:S(2)}, u32[]{:S(2)}) collective-permute-start(bf16[12,4096]{1,0:T(8,128)(2,1)S(1)} %get-tuple-element.152), channel_id=1, source_target_pairs={{0,8},{4,12},{8,0},{12,4},{1,9},{5,13},{9,1},{13,5},{2,10},{6,14},... | collective-permute-start | bytes 294920 | tf_op jit(solution)/shard_map/ppermute | solution.py:133
  145.1 11.5 %collective-permute-start.2 = (bf16[12,4096]{1,0:T(8,128)(2,1)S(1)}, bf16[12,4096]{1,0:T(8,128)(2,1)S(1)}, u32[]{:S(2)}, u32[]{:S(2)}) collective-permute-start(bf16[12,4096]{1,0:T(8,128)(2,1)S(1)} %get-tuple-element.153), channel_id=1, source_target_pairs={{0,4},{4,8},{8,12},{12,0},{1,5},{5,9},{9,13},{13,1},{2,6},{6,10},{... | collective-permute-start | bytes 294920 | tf_op jit(solution)/shard_map/ppermute | solution.py:133
  157.5 83.4 %reduce-scatter.2.cloned.1.call-start = ((), (), s32[]{:S(2)}) async-start(), calls=%async_computation.1 | async-start | bytes 5242880 | tf_op jit(solution)/shard_map/reduce_scatter | solution.py:138
  242.1 7.3 %collective-permute-start.7 = (f32[12,4096]{1,0:T(8,128)S(1)}, f32[12,4096]{1,0:T(8,128)}, u32[]{:S(2)}, u32[]{:S(2)}) collective-permute-start(f32[12,4096]{1,0:T(8,128)S(1)} %get-tuple-element.145), channel_id=1, source_target_pairs={{0,4},{4,8},{8,12},{12,0},{1,5},{5,9},{9,13},{13,1},{2,6},{6,10},{... | collective-permute-start | bytes 589832 | tf_op jit(solution)/shard_map/ppermute | solution.py:144
  243.4 21.8 %collective-permute-start.6 = (f32[12,4096]{1,0:T(8,128)S(1)}, f32[12,4096]{1,0:T(8,128)}, u32[]{:S(2)}, u32[]{:S(2)}) collective-permute-start(f32[12,4096]{1,0:T(8,128)S(1)} %get-tuple-element.146), channel_id=1, source_target_pairs={{0,8},{4,12},{8,0},{12,4},{1,9},{5,13},{9,1},{13,5},{2,10},{6,14},... | collective-permute-start | bytes 589832 | tf_op jit(solution)/shard_map/ppermute | solution.py:144
  244.4 23.8 %collective-permute-start.5 = (f32[12,4096]{1,0:T(8,128)S(1)}, f32[12,4096]{1,0:T(8,128)}, u32[]{:S(2)}, u32[]{:S(2)}) collective-permute-start(f32[12,4096]{1,0:T(8,128)S(1)} %get-tuple-element.147), channel_id=1, source_target_pairs={{0,12},{4,0},{8,4},{12,8},{1,13},{5,1},{9,5},{13,9},{2,14},{6,2},{... | collective-permute-start | bytes 589832 | tf_op jit(solution)/shard_map/ppermute | solution.py:144
  (19 other events, 26.7 us)
Sparse Core Ops, SparseCore 0:
  66.2 64.1 all-gather.7
  157.6 22.8 all-gather.5
  196.7 44.1 reduce-scatter.1

commit v3 on v1

--- a/solution.py
+++ b/solution.py
@@ -3,6 +3,8 @@
 import jax
 import jax.numpy as jnp
 from jax import lax
+from jax.experimental import pallas as pl
+from jax.experimental.pallas import tpu as pltpu
 from jax.sharding import PartitionSpec as P
 
 HQ = 32
@@ -12,37 +14,58 @@
 CAP = 12
 
 
-def prefix(value, axis, join, neutral):
-    count, mine = (lax.axis_size(axis), lax.axis_index(axis))
-    pieces = jax.tree.map(lambda part: lax.all_gather(part, axis), value)
-    running = jax.tree.map(
-        lambda part, zero: jnp.full_like(part, 0) + jnp.asarray(zero, part.dtype), value, neutral
-    )
-
-    def hop(position, running):
-        longer = join(running, jax.tree.map(lambda part: part[position], pieces))
-        return jax.tree.map(lambda new, old: jnp.where(position < mine, new, old), longer, running)
-
-    return lax.fori_loop(0, count - 1, hop, running)
-
-
 def shifted(value, axis, by):
     devices = lax.axis_size(axis)
     pairs = [(i, i + by) for i in range(devices) if 0 <= i + by < devices]
     return lax.ppermute(value, axis, pairs)
 
 
-def sweep(initial, values, deltas, rates, inject_rows, read_rows):
-
-    def advance(carried, packet):
-        value_row, delta_row, inject_row, read_row = packet
-        carried = (
-            jnp.exp(delta_row[None, :] * rates) * carried
-            + (delta_row * value_row)[None, :] * inject_row[:, None]
-        )
-        return (carried, jnp.sum(read_row[:, None] * carried, axis=0))
-
-    return lax.scan(advance, initial, (values, deltas, inject_rows.T, read_rows.T), unroll=8)
+def scan_kernel(b_ref, c_ref, dt_ref, inj_ref, a_ref, read_ref, end_ref):
+    states = a_ref.shape[0]
+    steps = dt_ref.shape[0]
+    h = [jnp.zeros(dt_ref.shape[1:], jnp.float32) for _ in range(states)]
+    for t in range(steps):
+        d = dt_ref[t]
+        u = inj_ref[t]
+        total = None
+        for n in range(states):
+            h[n] = jnp.exp(d * a_ref[n]) * h[n] + b_ref[n, t] * u
+            term = c_ref[n, t] * h[n]
+            total = term if total is None else total + term
+        read_ref[t] = total
+    for n in range(states):
+        end_ref[n] = h[n]
+
+
+def sweep(values, deltas, rates, inject_rows, read_rows):
+    steps, channels = deltas.shape
+    states = rates.shape[0]
+    lanes = 128
+    rows = channels // lanes
+    tile = 8
+    dt3 = deltas.reshape(steps, rows, lanes)
+    inj3 = (deltas * values).reshape(steps, rows, lanes)
+    a3 = rates.reshape(states, rows, lanes)
+    read3, end3 = pl.pallas_call(
+        scan_kernel,
+        grid=(rows // tile,),
+        in_specs=[
+            pl.BlockSpec(memory_space=pltpu.SMEM),
+            pl.BlockSpec(memory_space=pltpu.SMEM),
+            pl.BlockSpec((steps, tile, lanes), lambda j: (0, j, 0)),
+            pl.BlockSpec((steps, tile, lanes), lambda j: (0, j, 0)),
+            pl.BlockSpec((states, tile, lanes), lambda j: (0, j, 0)),
+        ],
+        out_specs=[
+            pl.BlockSpec((steps, tile, lanes), lambda j: (0, j, 0)),
+            pl.BlockSpec((states, tile, lanes), lambda j: (0, j, 0)),
+        ],
+        out_shape=[
+            jax.ShapeDtypeStruct((steps, rows, lanes), jnp.float32),
+            jax.ShapeDtypeStruct((states, rows, lanes), jnp.float32),
+        ],
+    )(inject_rows, read_rows, dt3, inj3, a3)
+    return end3.reshape(states, channels), read3.reshape(steps, channels)
 
 
 def ssm_correct(local_read, local_end, deltas, rates, read_rows):
@@ -60,10 +83,6 @@
     growth = jnp.exp(rates[None] * running[:, None, :]) * incoming[None]
     fix = jnp.sum(read_rows.T[:, :, None] * growth, axis=1)
     return (local_read + fix).astype(jnp.bfloat16)
-
-
-def chain_join(earlier, later):
-    return (earlier[0] * later[0], later[0] * earlier[1] + later[1])
 
 
 def attend(queries, window, query_pos, key_pos):
@@ -111,8 +130,7 @@
 ):
     values = ssm_in.astype(jnp.float32)
     deltas = ssm_dt.astype(jnp.float32)
-    initial = jnp.zeros(ssm_a.shape, jnp.float32)
-    local_end, local_read = sweep(initial, values, deltas, ssm_a, ssm_b, ssm_c)
+    local_end, local_read = sweep(values, deltas, ssm_a, ssm_b, ssm_c)
     ssm_out = ssm_correct(local_read, local_end, deltas, ssm_a, ssm_c)
     count = attn_q.shape[0]
     block_index = lax.axis_index("seq")

time: 244 us -> 215 us (0.88)
  local copies, waits for them, and re-layouts: 44.3 us -> 18.7 us
  other arithmetic: 27.3 us -> 15.9 us
  Pallas kernels: 0 us -> 7.33 us
  waiting for transfers between devices: 58.7 us -> 61.2 us
    slice x8 -> x0, local copies, waits for them, and re-layouts: 19.2 us -> none  [sweep(): lax.scan(advance, initial, (values, deltas, inject_rows.T, read_rows.T),...]
    reduce_sum x24 -> x0, other arithmetic: 9.28 us -> none  [advance(): return (carried, jnp.sum(read_row[:, None] * carried, axis=0))]
    pallas_call x0 -> x1, Pallas kernels: none -> 7.33 us  [sweep(): pl.pallas_call(scan_kernel, grid=(rows // tile,), in_specs=[pl.BlockSpec(...]
    dynamic_update_slice x8 -> x0, local copies, waits for them, and re-layouts: 5.29 us -> none  [sweep(): lax.scan(advance, initial, (values, deltas, inject_rows.T, read_rows.T),...]
    reshape x2 -> x0, other arithmetic: 4.39 us -> none  [sweep(): lax.scan(advance, initial, (values, deltas, inject_rows.T, read_rows.T),...]
    all_gather x1, waiting for transfers between devices: 11.2 us -> 13.7 us  [ssm_correct(): ends = lax.all_gather(local_end, 'seq')]
    unnamed x36 -> x35, local copies, waits for them, and re-layouts: 6.72 us -> 7.37 us
where the time goes in v3:
time: 215 us; the launch traced here: 214 us
  blocking collectives  70.2 us (33%)
  waiting for transfers between devices  61.2 us (28%)
  local copies, waits for them, and re-layouts  18.7 us (9%)
  other arithmetic  15.9 us (7%)
  matrix products  14.4 us (7%)
  between operations  14.3 us (7%)
  starting transfers between devices  12.3 us (6%)
  Pallas kernels  7.33 us (3%)
    all_to_all x1, blocking collectives, body(): lax.all_to_all(outgoing, 'seq', split_axis=0, concat_axis=0, tiled=True)  51.8 us
    all_to_all x1, waiting for transfers between devices, body(): lax.all_to_all(partial_value.reshape(arrived.shape), 'seq', split_axis=0,...  47.5 us
    all_gather x1, blocking collectives, ssm_correct(): sums = lax.all_gather(running[-1], 'seq')  18.4 us
    all_gather x1, waiting for transfers between devices, ssm_correct(): ends = lax.all_gather(local_end, 'seq')  13.7 us
    unnamed x35, local copies, waits for them, and re-layouts  7.37 us
    pallas_call x1, Pallas kernels, sweep(): pl.pallas_call(scan_kernel, grid=(rows // tile,), in_specs=[pl.BlockSpec(...  7.33 us
    ppermute x2, starting transfers between devices, shifted(): return lax.ppermute(value, axis, pairs)  7.27 us
    reduce_sum x1, other arithmetic, ssm_correct(): fix = jnp.sum(read_rows.T[:, :, None] * growth, axis=1)  5.35 us
  transfers between devices with their start and end apart: 4, of which 2 were waited for; matrix products, arithmetic and copies ran while one was open for 7% of the time, Pallas kernels for 0%

profile of v3, /device:TPU:11, one launch (start us, length us, event | category | flops | bytes accessed | tf_op | source)
XLA Modules:
  0.0 214.4 jit_solution(8123004499207410166)
XLA Ops:
  7.2 1.3 convert_bitcast_fusion
  8.5 1.2 copy.54
  9.8 1.2 copy.55
  11.0 0.8 copy.56
  11.8 7.3 %shard_map.148 = (f32[64,32,128]{2,1,0:T(8,128)}, f32[16,32,128]{2,1,0:T(8,128)}) custom-call(f32[16,64]{1,0:T(8,128)} %b_ref.1, f32[16,64]{1,0:T(8,128)} %c_ref.1, f32[64,32,128]{2,1,0:T(8,128)} %bitcast.56, f32[64,32,128]{2,1,0:T(8,128)} %bitcast.57, f32[16,32,128]{2,1,0:T(8,128)} %bitcast.59), custom_call_target="tpu_custom_call" | custom-call | tf_op jit(solution)/shard_map/pallas_call | solution.py:49
  19.1 1.7 all_gather_reshape.3
  20.9 3.3 %collective-permute-start = (bf16[64,2048]{1,0:T(8,128)(2,1)}, bf16[64,2048]{1,0:T(8,128)(2,1)}, u32[]{:S(2)}, u32[]{:S(2)}) collective-permute-start(bf16[64,2048]{1,0:T(8,128)(2,1)} %param.19), channel_id=1, source_target_pairs={{0,2},{1,3},{2,4},{3,5},{4,6},{5,7},{6,8},{7,9},{8,10},{9,11},{10,... | collective-permute-start | bytes 786440 | tf_op jit(solution)/shard_map/ppermute | solution.py:20
  24.2 4.0 %collective-permute-start.1 = (bf16[64,2048]{1,0:T(8,128)(2,1)}, bf16[64,2048]{1,0:T(8,128)(2,1)}, u32[]{:S(2)}, u32[]{:S(2)}) collective-permute-start(bf16[64,2048]{1,0:T(8,128)(2,1)} %param.19), channel_id=1, source_target_pairs={{0,1},{1,2},{2,3},{3,4},{4,5},{5,6},{6,7},{7,8},{8,9},{9,10},{10,1... | collective-permute-start | bytes 786440 | tf_op jit(solution)/shard_map/ppermute | solution.py:20
  28.2 1.9 reduce_window_sum.33
  30.0 0.9 slice_bitcast_fusion.2
  30.9 18.4 %all-gather = f32[16,1,4096]{2,1,0:T(1,128)S(1)} all-gather(f32[1,1,4096]{2,1,0:T(1,128)S(1)} %slice_bitcast_fusion.2), channel_id=1, replica_groups=mesh['grp'=2,'seq'=16] {'seq'}, dimensions={0}, use_global_device_ids=true | all-gather | bytes 278528 | tf_op jit(solution)/shard_map/all_gather | solution.py:75
  50.0 0.7 subtract_maximum_fusion
  51.4 1.0 constant_dynamic-update-slice_fusion.2
  52.4 1.0 constant_dynamic-update-slice_fusion.1
  53.4 1.0 constant_dynamic-update-slice_fusion
  54.5 0.8 copy.58
  55.3 2.2 %fusion.49 = (f32[8,4,64]{2,1,0:T(4,128)S(1)}, f32[8,4,64,192]{3,2,1,0:T(8,128)}) fusion(pred[64,192]{1,0:T(8,128)(4,1)S(1)} %compare_and_fusion, bf16[64,8,4,128]{3,2,1,0:T(4,128)(2,1)S(1)} %reshape.153, bf16[192,8,128,1]{2,1,0,3:T(8,128)(2,1)S(1)} %bitcast.61), kind=kOutput, calls=%fused_computation.67 | convolution fusion | flops 102236352 | bytes 2510848 | tf_op jit(solution)/shard_map/sub | solution.py:101
  57.5 2.3 %fusion.3 = bf16[64,8,4,128]{3,0,2,1:T(8,128)(2,1)S(1)} fusion(f32[8,4,64,192]{3,2,1,0:T(8,128)} %get-tuple-element.14, f32[8,4,64]{2,1,0:T(4,128)S(1)} %get-tuple-element.13, bf16[192,8,128,1]{2,1,0,3:T(8,128)(2,1)} %bitcast.62), kind=kOutput, calls=%fused_computation.13 | convolution fusion | flops 101711872 | bytes 2498560 | tf_op jit(solution)/shard_map/kyje,eku->jkyu/dot_general | solution.py:103
  59.8 0.4 copy.44
  60.6 13.7 %all-gather.3.cloned.1.call-done = f32[16,16,4096]{2,1,0:T(8,128)} async-done(((f32[1,16,4096]{2,1,0:T(8,128)}), f32[16,16,4096]{2,1,0:T(8,128)}) %all-gather.3.cloned.1.call-update) | async-done | bytes 4194320 | tf_op jit(solution)/shard_map/all_gather | solution.py:74
  74.3 3.1 %select_reduce_fusion = f32[16,4096]{1,0:T(8,128)S(1)} fusion(f32[16,16,4096]{2,1,0:T(8,128)} %all-gather.3.cloned.1.call-done, f32[16,4096]{1,0:T(8,128)} %subtract_maximum_fusion, f32[16,4096]{1,0:T(8,128)S(1)} %copy-done.5, pred[16]{0:T(512)(128)(4,1)S(1)} %iota_compare_fusion.2), kind=kLoop, calls=%fused_computation.7 | loop fusion | flops 4128768 | bytes 4980752 | tf_op jit(solution)/shard_map/reduce_sum | solution.py:82
  77.5 5.3 %multiply_reduce_fusion = f32[64,4096]{1,0:T(8,128)S(1)} fusion(f32[16,4096]{1,0:T(8,128)S(1)} %select_reduce_fusion, f32[64,4096]{1,0:T(8,128)S(1)} %copy-done.4, f32[16,4096]{1,0:T(8,128)S(1)} %copy-done.5, f32[64,16]{1,0:T(8,128)S(1)} %copy.40), kind=kLoop, calls=%fused_computation.1 | loop fusion | flops 16515072 | bytes 2625536 | tf_op jit(solution)/shard_map/reduce_sum | solution.py:84
  82.8 0.7 fusion.5
  84.5 51.8 %all_to_all.10 = bf16[16,12,4096]{2,1,0:T(8,128)(2,1)} all-to-all(bf16[16,12,4096]{2,1,0:T(8,128)(2,1)S(1)} %bitcast.55), channel_id=1, replica_groups=mesh['grp'=2,'seq'=16] {'seq'}, dimensions={0} | all-to-all | bytes 3145728 | tf_op jit(solution)/shard_map/all_to_all | solution.py:163
  136.3 3.6 %reshape.155 = bf16[192,4096]{1,0:T(8,128)(2,1)} reshape(bf16[16,12,4096]{2,1,0:T(8,128)(2,1)} %all_to_all.10) | data formatting | bytes 3145728 | tf_op jit(solution)/shard_map/reshape | solution.py:164
  139.9 2.6 %fusion.54 = f32[192,256]{1,0:T(8,128)S(1)} fusion(bf16[192,4096]{1,0:T(8,128)(2,1)} %reshape.155, bf16[4096,256]{1,0:T(8,128)(2,1)} %param.23), kind=kOutput, calls=%fused_computation.68 | convolution fusion | flops 402653184 | bytes 3866624 | tf_op jit(solution)/shard_map/dot_general | solution.py:110
  142.5 5.1 %convolution_convert_fusion = bf16[192,4096]{1,0:T(8,128)(2,1)} fusion(bf16[256,4096]{1,0:T(8,128)(2,1)S(1)} %copy-done, bf16[192,4096]{1,0:T(8,128)(2,1)} %reshape.155, bf16[4096,256]{1,0:T(8,128)(2,1)} %param.24, f32[192,256]{1,0:T(8,128)S(1)} %fusion.54), kind=kOutput, calls=%fused_computation.2 | convolution fusion | flops 806387712 | bytes 7536640 | tf_op jit(solution)/shard_map/dot_general | solution.py:113
  147.6 3.4 %reshape.156 = bf16[16,12,4096]{2,1,0:T(8,128)(2,1)} reshape(bf16[192,4096]{1,0:T(8,128)(2,1)} %convolution_convert_fusion) | data formatting | bytes 3145728 | tf_op jit(solution)/shard_map/reshape | solution.py:167
  151.0 5.0 %all-to-all-start.1 = ((bf16[16,12,4096]{2,1,0:T(8,128)(2,1)}), bf16[16,12,4096]{2,1,0:T(8,128)(2,1)}, u32[]{:S(2)}, u32[]{:S(2)}) async-start(bf16[16,12,4096]{2,1,0:T(8,128)(2,1)} %reshape.156), calls=%async_computation.1 | async-start | bytes 4194304 | tf_op jit(solution)/shard_map/all_to_all | solution.py:166
  156.1 47.5 %all-to-all-done.1 = bf16[16,12,4096]{2,1,0:T(8,128)(2,1)} async-done(((bf16[16,12,4096]{2,1,0:T(8,128)(2,1)}), bf16[16,12,4096]{2,1,0:T(8,128)(2,1)}, u32[]{:S(2)}, u32[]{:S(2)}) %all-to-all-start.1) | async-done | bytes 1572896 | tf_op jit(solution)/shard_map/all_to_all | solution.py:166
  203.6 2.1 convert_reduce_fusion
  205.7 1.8 fusion.1
  (52 shorter events, 2.9 us)
Async XLA Ops:
  7.2 135.3 %copy-start = (bf16[256,4096]{1,0:T(8,128)(2,1)S(1)}, bf16[256,4096]{1,0:T(8,128)(2,1)}, u32[]{:S(2)}) copy-start(bf16[256,4096]{1,0:T(8,128)(2,1)} %param.25) | copy-start | bytes 6291460
  7.2 2.5 %copy-start.1 = (bf16[64,4096]{1,0:T(8,128)(2,1)S(1)}, bf16[64,4096]{1,0:T(8,128)(2,1)}, u32[]{:S(2)}) copy-start(bf16[64,4096]{1,0:T(8,128)(2,1)} %param.14) | copy-start | bytes 1572868
  7.2 2.5 %copy-start.8 = (bf16[64,4096]{1,0:T(8,128)(2,1)S(1)}, bf16[64,4096]{1,0:T(8,128)(2,1)}, u32[]{:S(2)}) copy-start(bf16[64,4096]{1,0:T(8,128)(2,1)} %param.13) | copy-start | bytes 1572868
  7.2 67.1 %all-gather.3.cloned.1.call-start = ((), (), s32[]{:S(2)}) async-start(), calls=%async_computation.2 | async-start | bytes 4456448 | tf_op jit(solution)/shard_map/all_gather | solution.py:74
  9.7 1.3 copy-start.5
  19.1 30.6 %copy-start.11 = (s32[64,2]{0,1:T(2,128)S(1)}, s32[64,2]{0,1:T(2,128)}, u32[]{:S(2)}) copy-start(s32[64,2]{0,1:T(2,128)} %param.21) | copy-start | bytes 1540
  20.8 30.0 %copy-start.10 = (f32[16,64]{1,0:T(8,128)S(1)}, f32[16,64]{1,0:T(8,128)}, u32[]{:S(2)}) copy-start(f32[16,64]{1,0:T(8,128)} %c_ref.1) | copy-start | bytes 12292
  20.8 30.1 %copy-start.7 = (bf16[64,4096]{1,0:T(8,128)(2,1)S(1)}, bf16[64,4096]{1,0:T(8,128)(2,1)}, u32[]{:S(2)}) copy-start(bf16[64,4096]{1,0:T(8,128)(2,1)} %param.18) | copy-start | bytes 1572868
  20.9 30.5 %collective-permute-start = (bf16[64,2048]{1,0:T(8,128)(2,1)}, bf16[64,2048]{1,0:T(8,128)(2,1)}, u32[]{:S(2)}, u32[]{:S(2)}) collective-permute-start(bf16[64,2048]{1,0:T(8,128)(2,1)} %param.19), channel_id=1, source_target_pairs={{0,2},{1,3},{2,4},{3,5},{4,6},{5,7},{6,8},{7,9},{8,10},{9,11},{10,... | collective-permute-start | bytes 786440 | tf_op jit(solution)/shard_map/ppermute | solution.py:20
  24.2 28.2 %collective-permute-start.1 = (bf16[64,2048]{1,0:T(8,128)(2,1)}, bf16[64,2048]{1,0:T(8,128)(2,1)}, u32[]{:S(2)}, u32[]{:S(2)}) collective-permute-start(bf16[64,2048]{1,0:T(8,128)(2,1)} %param.19), channel_id=1, source_target_pairs={{0,1},{1,2},{2,3},{3,4},{4,5},{5,6},{6,7},{7,8},{8,9},{9,10},{10,1... | collective-permute-start | bytes 786440 | tf_op jit(solution)/shard_map/ppermute | solution.py:20
  60.6 22.9 %copy-start.3 = (bf16[64,4096]{1,0:T(8,128)(2,1)}, bf16[64,4096]{1,0:T(8,128)(2,1)S(1)}, u32[]{:S(2)}) copy-start(bf16[64,4096]{1,0:T(8,128)(2,1)S(1)} %convert_element_type.70) | copy-start | bytes 1572868
  74.3 3.1 %copy-start.4 = (f32[64,4096]{1,0:T(8,128)S(1)}, f32[64,4096]{1,0:T(8,128)}, u32[]{:S(2)}) copy-start(f32[64,4096]{1,0:T(8,128)} %reduce_window_sum.33) | copy-start | bytes 3145732
  77.5 5.4 %copy-start.6 = (f32[64,32,128]{2,1,0:T(8,128)S(1)}, f32[64,32,128]{2,1,0:T(8,128)}, u32[]{:S(2)}) copy-start(f32[64,32,128]{2,1,0:T(8,128)} %get-tuple-element.5) | copy-start | bytes 3145732
  82.8 1.0 copy-start.9
  83.5 0.9 copy-start.2
  151.0 5.0 %copy-start.12 = (f32[64,2]{0,1:T(2,128)S(1)}, f32[64,2]{0,1:T(2,128)}, u32[]{:S(2)}) copy-start(f32[64,2]{0,1:T(2,128)} %param.22) | copy-start | bytes 1540
  151.0 52.6 %all-to-all-start.1 = ((bf16[16,12,4096]{2,1,0:T(8,128)(2,1)}), bf16[16,12,4096]{2,1,0:T(8,128)(2,1)}, u32[]{:S(2)}, u32[]{:S(2)}) async-start(bf16[16,12,4096]{2,1,0:T(8,128)(2,1)} %reshape.156), calls=%async_computation.1 | async-start | bytes 4194304 | tf_op jit(solution)/shard_map/all_to_all | solution.py:166
Sparse Core Ops, SparseCore 0:
  21.0 53.2 all-gather.2

commit v4 on v3

--- a/solution.py
+++ b/solution.py
@@ -72,7 +72,7 @@
     mine = lax.axis_index("seq")
     running = jnp.cumsum(deltas, axis=0)
     ends = lax.all_gather(local_end, "seq")
-    sums = lax.all_gather(running[-1], "seq")
+    sums = lax.optimization_barrier(lax.all_gather(running[-8:], "seq"))[:, -1]
     devices = sums.shape[0]
     order = jnp.arange(devices, dtype=jnp.int32)
     masked = jnp.where((order < mine)[:, None], sums, 0.0)

time: 215 us -> 248 us (1.15)
  waiting for transfers between devices: 61.2 us -> 109 us
  blocking collectives: 70.2 us -> 51.8 us
  local copies, waits for them, and re-layouts: 18.7 us -> 21.2 us
    all_gather x1, waiting for transfers between devices: 13.7 us -> 48.9 us  [ssm_correct(): ends = lax.all_gather(local_end, 'seq')]
    all_gather x1 -> x0, blocking collectives: 18.4 us -> none  [ssm_correct(): sums = lax.all_gather(running[-1], 'seq')]
    all_gather x0 -> x1, waiting for transfers between devices: none -> 7.71 us  [ssm_correct(): sums = lax.optimization_barrier(lax.all_gather(running[-8:], 'seq'))[:, -1]]
    ppermute x2, waiting for transfers between devices: 0.01 us -> 4.59 us  [shifted(): return lax.ppermute(value, axis, pairs)]
    slice x0 -> x2, local copies, waits for them, and re-layouts: none -> 3.49 us  [ssm_correct(): sums = lax.optimization_barrier(lax.all_gather(running[-8:], 'seq'))[:, -1]]
    unnamed x35 -> x34, local copies, waits for them, and re-layouts: 7.37 us -> 6.36 us
  transfers between devices with their start and end apart: 4 -> 5, of which waited for: 2 -> 5; matrix products, arithmetic and copies ran while one was open for 7% -> 8% of each run, Pallas kernels for 0% -> 3%
where the time goes in v4:
time: 248 us; the launch traced here: 247 us
  waiting for transfers between devices  109 us (44%)
  blocking collectives  51.8 us (21%)
  local copies, waits for them, and re-layouts  21.2 us (9%)
  other arithmetic  17.1 us (7%)
  matrix products  14.4 us (6%)
  between operations  14.4 us (6%)
  starting transfers between devices  12.3 us (5%)
  Pallas kernels  7.34 us (3%)
    all_to_all x1, blocking collectives, body(): lax.all_to_all(outgoing, 'seq', split_axis=0, concat_axis=0, tiled=True)  51.8 us
    all_gather x1, waiting for transfers between devices, ssm_correct(): ends = lax.all_gather(local_end, 'seq')  48.9 us
    all_to_all x1, waiting for transfers between devices, body(): lax.all_to_all(partial_value.reshape(arrived.shape), 'seq', split_axis=0,...  47.5 us
    all_gather x1, waiting for transfers between devices, ssm_correct(): sums = lax.optimization_barrier(lax.all_gather(running[-8:], 'seq'))[:, -1]  7.71 us
    pallas_call x1, Pallas kernels, sweep(): pl.pallas_call(scan_kernel, grid=(rows // tile,), in_specs=[pl.BlockSpec(...  7.34 us
    ppermute x2, starting transfers between devices, shifted(): return lax.ppermute(value, axis, pairs)  7.14 us
    unnamed x34, local copies, waits for them, and re-layouts  6.36 us
    reduce_sum x1, other arithmetic, ssm_correct(): fix = jnp.sum(read_rows.T[:, :, None] * growth, axis=1)  5.35 us
  transfers between devices with their start and end apart: 5, of which 5 were waited for; matrix products, arithmetic and copies ran while one was open for 8% of the time, Pallas kernels for 3%

profile of v4, /device:TPU:11, one launch (start us, length us, event | category | flops | bytes accessed | tf_op | source)
XLA Modules:
  0.0 247.3 jit_solution(6327912505723678757)
XLA Ops:
  7.2 3.2 %reduce_window_sum.35 = f32[64,4096]{1,0:T(8,128)} reduce-window(bf16[64,4096]{1,0:T(8,128)(2,1)} %param.14, f32[]{:T(128)} %constant.12.clone.1), window={size=64x1 pad=63_0x0_0}, to_apply=%region_0.0 | reduce-window | flops 16515072 | bytes 1572868 | tf_op jit(solution)/shard_map/jit(cumsum)/reduce_window_sum | solution.py:73
  10.4 1.6 slice.16
  12.2 1.2 copy.58
  13.5 1.2 copy.59
  15.4 7.3 %shard_map.148 = (f32[64,32,128]{2,1,0:T(8,128)}, f32[16,32,128]{2,1,0:T(8,128)}) custom-call(f32[16,64]{1,0:T(8,128)} %b_ref.1, f32[16,64]{1,0:T(8,128)} %c_ref.1, f32[64,32,128]{2,1,0:T(8,128)} %bitcast.58, f32[64,32,128]{2,1,0:T(8,128)} %bitcast.59, f32[16,32,128]{2,1,0:T(8,128)} %bitcast.61), custom_call_target="tpu_custom_call" | custom-call | tf_op jit(solution)/shard_map/pallas_call | solution.py:49
  22.8 1.7 all_gather_reshape.3
  24.5 3.2 %collective-permute-start = (bf16[64,2048]{1,0:T(8,128)(2,1)}, bf16[64,2048]{1,0:T(8,128)(2,1)}, u32[]{:S(2)}, u32[]{:S(2)}) collective-permute-start(bf16[64,2048]{1,0:T(8,128)(2,1)} %param.19), channel_id=1, source_target_pairs={{0,2},{1,3},{2,4},{3,5},{4,6},{5,7},{6,8},{7,9},{8,10},{9,11},{10,... | collective-permute-start | bytes 786440 | tf_op jit(solution)/shard_map/ppermute | solution.py:20
  27.7 4.0 %collective-permute-start.1 = (bf16[64,2048]{1,0:T(8,128)(2,1)}, bf16[64,2048]{1,0:T(8,128)(2,1)}, u32[]{:S(2)}, u32[]{:S(2)}) collective-permute-start(bf16[64,2048]{1,0:T(8,128)(2,1)} %param.19), channel_id=1, source_target_pairs={{0,1},{1,2},{2,3},{3,4},{4,5},{5,6},{6,7},{7,8},{8,9},{9,10},{10,1... | collective-permute-start | bytes 786440 | tf_op jit(solution)/shard_map/ppermute | solution.py:20
  32.6 2.0 collective-permute-done
  34.6 1.0 constant_dynamic-update-slice_fusion.2
  35.5 2.6 %collective-permute-done.1 = bf16[64,2048]{1,0:T(8,128)(2,1)} collective-permute-done((bf16[64,2048]{1,0:T(8,128)(2,1)}, bf16[64,2048]{1,0:T(8,128)(2,1)}, u32[]{:S(2)}, u32[]{:S(2)}) %collective-permute-start.1) | collective-permute-done | bytes 262176 | tf_op jit(solution)/shard_map/ppermute | solution.py:20
  38.1 1.0 constant_dynamic-update-slice_fusion.1
  39.1 1.0 constant_dynamic-update-slice_fusion
  40.3 0.8 copy.62
  41.1 2.3 fusion.49
  43.4 2.2 fusion.3
  46.4 7.7 %all-gather.6.cloned.1.call-done = f32[128,4096]{1,0:T(8,128)} async-done(((f32[8,4096]{1,0:T(8,128)}), f32[128,4096]{1,0:T(8,128)}) %all-gather.6.cloned.1.call-update) | async-done | bytes 2097168 | tf_op jit(solution)/shard_map/all_gather | solution.py:75
  54.1 1.9 slice.17
  56.2 0.9 reduce_window_sum.37
  57.3 1.0 subtract_maximum_fusion
  58.3 48.9 %all-gather.4.cloned.1.call-done = f32[16,16,4096]{2,1,0:T(8,128)} async-done(((f32[1,16,4096]{2,1,0:T(8,128)}), f32[16,16,4096]{2,1,0:T(8,128)}) %all-gather.4.cloned.1.call-update) | async-done | bytes 4194320 | tf_op jit(solution)/shard_map/all_gather | solution.py:74
  107.2 3.1 %select_reduce_fusion = f32[16,4096]{1,0:T(8,128)S(1)} fusion(f32[16,16,4096]{2,1,0:T(8,128)} %all-gather.4.cloned.1.call-done, f32[16,4096]{1,0:T(8,128)S(1)} %subtract_maximum_fusion, f32[16,4096]{1,0:T(8,128)S(1)} %copy-done.5, pred[16]{0:T(512)(128)(4,1)S(1)} %iota_compare_fusion.2), kind=kLoop, calls=%fused_computation.7 | loop fusion | flops 4128768 | bytes 4980752 | tf_op jit(solution)/shard_map/reduce_sum | solution.py:82
  110.4 5.3 %multiply_reduce_fusion = f32[64,4096]{1,0:T(8,128)S(1)} fusion(f32[16,4096]{1,0:T(8,128)S(1)} %select_reduce_fusion, f32[64,4096]{1,0:T(8,128)S(1)} %copy-done.4, f32[16,4096]{1,0:T(8,128)S(1)} %copy-done.5, f32[64,16]{1,0:T(8,128)S(1)} %copy.43), kind=kLoop, calls=%fused_computation.1 | loop fusion | flops 16515072 | bytes 2625536 | tf_op jit(solution)/shard_map/reduce_sum | solution.py:84
  117.4 51.8 %all_to_all.10 = bf16[16,12,4096]{2,1,0:T(8,128)(2,1)} all-to-all(bf16[16,12,4096]{2,1,0:T(8,128)(2,1)S(1)} %bitcast.57), channel_id=1, replica_groups=mesh['grp'=2,'seq'=16] {'seq'}, dimensions={0} | all-to-all | bytes 3145728 | tf_op jit(solution)/shard_map/all_to_all | solution.py:163
  169.2 3.6 %reshape.158 = bf16[192,4096]{1,0:T(8,128)(2,1)} reshape(bf16[16,12,4096]{2,1,0:T(8,128)(2,1)} %all_to_all.10) | data formatting | bytes 3145728 | tf_op jit(solution)/shard_map/reshape | solution.py:164
  172.8 2.6 %fusion.54 = f32[192,256]{1,0:T(8,128)S(1)} fusion(bf16[192,4096]{1,0:T(8,128)(2,1)} %reshape.158, bf16[4096,256]{1,0:T(8,128)(2,1)} %param.23), kind=kOutput, calls=%fused_computation.68 | convolution fusion | flops 402653184 | bytes 3866624 | tf_op jit(solution)/shard_map/dot_general | solution.py:110
  175.4 5.1 %convolution_convert_fusion = bf16[192,4096]{1,0:T(8,128)(2,1)} fusion(bf16[256,4096]{1,0:T(8,128)(2,1)S(1)} %copy-done, bf16[192,4096]{1,0:T(8,128)(2,1)} %reshape.158, bf16[4096,256]{1,0:T(8,128)(2,1)} %param.24, f32[192,256]{1,0:T(8,128)S(1)} %fusion.54), kind=kOutput, calls=%fused_computation.2 | convolution fusion | flops 806387712 | bytes 7536640 | tf_op jit(solution)/shard_map/dot_general | solution.py:113
  180.5 3.4 %reshape.159 = bf16[16,12,4096]{2,1,0:T(8,128)(2,1)} reshape(bf16[192,4096]{1,0:T(8,128)(2,1)} %convolution_convert_fusion) | data formatting | bytes 3145728 | tf_op jit(solution)/shard_map/reshape | solution.py:167
  183.9 5.0 %all-to-all-start.1 = ((bf16[16,12,4096]{2,1,0:T(8,128)(2,1)}), bf16[16,12,4096]{2,1,0:T(8,128)(2,1)}, u32[]{:S(2)}, u32[]{:S(2)}) async-start(bf16[16,12,4096]{2,1,0:T(8,128)(2,1)} %reshape.159), calls=%async_computation.1 | async-start | bytes 4194304 | tf_op jit(solution)/shard_map/all_to_all | solution.py:166
  189.0 47.5 %all-to-all-done.1 = bf16[16,12,4096]{2,1,0:T(8,128)(2,1)} async-done(((bf16[16,12,4096]{2,1,0:T(8,128)(2,1)}), bf16[16,12,4096]{2,1,0:T(8,128)(2,1)}, u32[]{:S(2)}, u32[]{:S(2)}) %all-to-all-start.1) | async-done | bytes 1572896 | tf_op jit(solution)/shard_map/all_to_all | solution.py:166
  236.5 2.1 convert_reduce_fusion
  238.6 1.8 fusion.1
  (56 shorter events, 4.8 us)
Async XLA Ops:
  7.2 168.2 %copy-start = (bf16[256,4096]{1,0:T(8,128)(2,1)S(1)}, bf16[256,4096]{1,0:T(8,128)(2,1)}, u32[]{:S(2)}) copy-start(bf16[256,4096]{1,0:T(8,128)(2,1)} %param.25) | copy-start | bytes 6291460
  7.2 4.9 %copy-start.1 = (bf16[64,4096]{1,0:T(8,128)(2,1)S(1)}, bf16[64,4096]{1,0:T(8,128)(2,1)}, u32[]{:S(2)}) copy-start(bf16[64,4096]{1,0:T(8,128)(2,1)} %param.14) | copy-start | bytes 1572868
  7.2 46.9 %all-gather.6.cloned.1.call-start = ((), (), s32[]{:S(2)}) async-start(), calls=%async_computation.3 | async-start | bytes 2228224 | tf_op jit(solution)/shard_map/all_gather | solution.py:75
  10.4 3.0 %copy-start.8 = (bf16[64,4096]{1,0:T(8,128)(2,1)S(1)}, bf16[64,4096]{1,0:T(8,128)(2,1)}, u32[]{:S(2)}) copy-start(bf16[64,4096]{1,0:T(8,128)(2,1)} %param.13) | copy-start | bytes 1572868
  12.0 95.2 %all-gather.4.cloned.1.call-start = ((), (), s32[]{:S(2)}) async-start(), calls=%async_computation.2 | async-start | bytes 4456448 | tf_op jit(solution)/shard_map/all_gather | solution.py:74
  13.4 1.3 copy-start.5
  14.7 17.0 %copy-start.11 = (s32[64,2]{0,1:T(2,128)S(1)}, s32[64,2]{0,1:T(2,128)}, u32[]{:S(2)}) copy-start(s32[64,2]{0,1:T(2,128)} %param.21) | copy-start | bytes 1540
  14.7 17.4 %copy-start.7 = (bf16[64,4096]{1,0:T(8,128)(2,1)S(1)}, bf16[64,4096]{1,0:T(8,128)(2,1)}, u32[]{:S(2)}) copy-start(bf16[64,4096]{1,0:T(8,128)(2,1)} %param.18) | copy-start | bytes 1572868
  15.4 17.0 %copy-start.10 = (f32[16,64]{1,0:T(8,128)S(1)}, f32[16,64]{1,0:T(8,128)}, u32[]{:S(2)}) copy-start(f32[16,64]{1,0:T(8,128)} %c_ref.1) | copy-start | bytes 12292
  24.5 10.1 %collective-permute-start = (bf16[64,2048]{1,0:T(8,128)(2,1)}, bf16[64,2048]{1,0:T(8,128)(2,1)}, u32[]{:S(2)}, u32[]{:S(2)}) collective-permute-start(bf16[64,2048]{1,0:T(8,128)(2,1)} %param.19), channel_id=1, source_target_pairs={{0,2},{1,3},{2,4},{3,5},{4,6},{5,7},{6,8},{7,9},{8,10},{9,11},{10,... | collective-permute-start | bytes 786440 | tf_op jit(solution)/shard_map/ppermute | solution.py:20
  27.7 10.5 %collective-permute-start.1 = (bf16[64,2048]{1,0:T(8,128)(2,1)}, bf16[64,2048]{1,0:T(8,128)(2,1)}, u32[]{:S(2)}, u32[]{:S(2)}) collective-permute-start(bf16[64,2048]{1,0:T(8,128)(2,1)} %param.19), channel_id=1, source_target_pairs={{0,1},{1,2},{2,3},{3,4},{4,5},{5,6},{6,7},{7,8},{8,9},{9,10},{10,1... | collective-permute-start | bytes 786440 | tf_op jit(solution)/shard_map/ppermute | solution.py:20
  46.4 70.0 %copy-start.3 = (bf16[64,4096]{1,0:T(8,128)(2,1)}, bf16[64,4096]{1,0:T(8,128)(2,1)S(1)}, u32[]{:S(2)}) copy-start(bf16[64,4096]{1,0:T(8,128)(2,1)S(1)} %convert_element_type.70) | copy-start | bytes 1572868
  107.2 3.1 %copy-start.4 = (f32[64,4096]{1,0:T(8,128)S(1)}, f32[64,4096]{1,0:T(8,128)}, u32[]{:S(2)}) copy-start(f32[64,4096]{1,0:T(8,128)} %reduce_window_sum.35) | copy-start | bytes 3145732
  110.3 5.4 %copy-start.6 = (f32[64,32,128]{2,1,0:T(8,128)S(1)}, f32[64,32,128]{2,1,0:T(8,128)}, u32[]{:S(2)}) copy-start(f32[64,32,128]{2,1,0:T(8,128)} %get-tuple-element.5) | copy-start | bytes 3145732
  115.7 1.0 copy-start.9
  116.4 0.9 copy-start.2
  183.9 5.0 %copy-start.12 = (f32[64,2]{0,1:T(2,128)S(1)}, f32[64,2]{0,1:T(2,128)}, u32[]{:S(2)}) copy-start(f32[64,2]{0,1:T(2,128)} %param.22) | copy-start | bytes 1540
  183.9 52.6 %all-to-all-start.1 = ((bf16[16,12,4096]{2,1,0:T(8,128)(2,1)}), bf16[16,12,4096]{2,1,0:T(8,128)(2,1)}, u32[]{:S(2)}, u32[]{:S(2)}) async-start(bf16[16,12,4096]{2,1,0:T(8,128)(2,1)} %reshape.159), calls=%async_computation.1 | async-start | bytes 4194304 | tf_op jit(solution)/shard_map/all_to_all | solution.py:166
Sparse Core Ops, SparseCore 0:
  12.2 41.9 all-gather.5
  56.9 50.2 all-gather.3

commit v5 on v4

--- a/solution.py
+++ b/solution.py
@@ -14,8 +14,8 @@
 CAP = 12
 
 
-def shifted(value, axis, by):
-    devices = lax.axis_size(axis)
+def shifted(value, axis, by, devices=None):
+    devices = devices or lax.axis_size(axis)
     pairs = [(i, i + by) for i in range(devices) if 0 <= i + by < devices]
     return lax.ppermute(value, axis, pairs)
 
@@ -68,18 +68,23 @@
     return end3.reshape(states, channels), read3.reshape(steps, channels)
 
 
-def ssm_correct(local_read, local_end, deltas, rates, read_rows):
-    mine = lax.axis_index("seq")
+def ssm_correct(local_read, local_end, deltas, rates, read_rows, devices):
     running = jnp.cumsum(deltas, axis=0)
-    ends = lax.all_gather(local_end, "seq")
-    sums = lax.optimization_barrier(lax.all_gather(running[-8:], "seq"))[:, -1]
-    devices = sums.shape[0]
-    order = jnp.arange(devices, dtype=jnp.int32)
-    masked = jnp.where((order < mine)[:, None], sums, 0.0)
-    after = jnp.sum(masked, axis=0)[None, :] - jnp.cumsum(masked, axis=0)
-    after = jnp.maximum(after, 0.0)
-    carry = jnp.exp(rates[None] * after[:, None, :]) * ends
-    incoming = jnp.sum(jnp.where((order < mine)[:, None, None], carry, 0.0), axis=0)
+    span = running[-1]
+
+    def join(earlier, later):
+        return (earlier[0] + later[0], jnp.exp(rates * later[0][None, :]) * earlier[1] + later[1])
+
+    closest = (shifted(span, "seq", 1, devices), shifted(local_end, "seq", 1, devices))
+    if devices > 2:
+        before = (shifted(span, "seq", 2, devices), shifted(local_end, "seq", 2, devices))
+        closest = join(before, closest)
+    reach = 2
+    while reach < devices:
+        earlier = (shifted(closest[0], "seq", reach, devices), shifted(closest[1], "seq", reach, devices))
+        closest = join(earlier, closest)
+        reach *= 2
+    incoming = closest[1]
     growth = jnp.exp(rates[None] * running[:, None, :]) * incoming[None]
     fix = jnp.sum(read_rows.T[:, :, None] * growth, axis=1)
     return (local_read + fix).astype(jnp.bfloat16)
@@ -131,7 +136,7 @@
     values = ssm_in.astype(jnp.float32)
     deltas = ssm_dt.astype(jnp.float32)
     local_end, local_read = sweep(values, deltas, ssm_a, ssm_b, ssm_c)
-    ssm_out = ssm_correct(local_read, local_end, deltas, ssm_a, ssm_c)
+    ssm_out = ssm_correct(local_read, local_end, deltas, ssm_a, ssm_c, lax.axis_size("seq"))
     count = attn_q.shape[0]
     block_index = lax.axis_index("seq")
     one_back = shifted(attn_kv, "seq", 1)

time: 248 us -> 224 us (0.903)
  waiting for transfers between devices: 109 us -> 67 us
  starting transfers between devices: 12.3 us -> 35 us
  between operations: 14.4 us -> 1.08 us
  blocking collectives: 51.8 us -> 57.5 us
  other arithmetic: 17.1 us -> 20.3 us
    all_gather x2 -> x0, waiting for transfers between devices: 56.6 us -> none  [the longest x1 48.9 us: ssm_correct(): ends = lax.all_gather(local_end, 'seq')]
    ppermute x2 -> x11, starting transfers between devices: 7.14 us -> 29.7 us  [shifted(): return lax.ppermute(value, axis, pairs)]
    ppermute x2 -> x11, waiting for transfers between devices: 4.59 us -> 19.5 us  [shifted(): return lax.ppermute(value, axis, pairs)]
    all_to_all x1, blocking collectives: 51.8 us -> 57.5 us  [body(): lax.all_to_all(outgoing, 'seq', split_axis=0, concat_axis=0, tiled=True)]
    add x0 -> x7, other arithmetic: none -> 5.25 us  [the longest x4 4.64 us: join(): jnp.exp(rates * later[0][None, :]) * earlier[1] + later[1]]
    reduce_sum x2 -> x0, other arithmetic: 3.3 us -> none  [the longest x1 3.12 us: ssm_correct(): jnp.sum(jnp.where((order < mine)[:, None, None], carry, 0.0), axis=0)]
    slice x2 -> x1, local copies, waits for them, and re-layouts: 3.49 us -> 0.96 us  [ssm_correct(): span = running[-1]]
    unnamed x34 -> x49, local copies, waits for them, and re-layouts: 6.36 us -> 7.23 us
  transfers between devices with their start and end apart: 5 -> 12, of which waited for: 5 -> 5; matrix products, arithmetic and copies ran while one was open for 8% -> 8% of each run, Pallas kernels for 3% -> 0%
where the time goes in v5:
time: 224 us; the launch traced here: 223 us
  waiting for transfers between devices  67 us (30%)
  blocking collectives  57.5 us (26%)
  starting transfers between devices  35 us (16%)
  other arithmetic  20.3 us (9%)
  local copies, waits for them, and re-layouts  18.8 us (8%)
  matrix products  15.9 us (7%)
  Pallas kernels  7.39 us (3%)
    all_to_all x1, blocking collectives, body(): lax.all_to_all(outgoing, 'seq', split_axis=0, concat_axis=0, tiled=True)  57.5 us
    all_to_all x1, waiting for transfers between devices, body(): lax.all_to_all(partial_value.reshape(arrived.shape), 'seq', split_axis=0,...  47.5 us
    ppermute x11, starting transfers between devices, shifted(): return lax.ppermute(value, axis, pairs)  29.7 us
    ppermute x11, waiting for transfers between devices, shifted(): return lax.ppermute(value, axis, pairs)  19.5 us
    pallas_call x1, Pallas kernels, sweep(): pl.pallas_call(scan_kernel, grid=(rows // tile,), in_specs=[pl.BlockSpec(...  7.39 us
    unnamed x49, local copies, waits for them, and re-layouts  7.23 us
    reduce_sum x1, other arithmetic, ssm_correct(): fix = jnp.sum(read_rows.T[:, :, None] * growth, axis=1)  6.41 us
    all_to_all x1, starting transfers between devices, body(): lax.all_to_all(partial_value.reshape(arrived.shape), 'seq', split_axis=0,...  5.25 us
  transfers between devices with their start and end apart: 12, of which 5 were waited for; matrix products, arithmetic and copies ran while one was open for 8% of the time, Pallas kernels for 0%

profile of v5, /device:TPU:11, one launch (start us, length us, event | category | flops | bytes accessed | tf_op | source)
XLA Modules:
  0.0 222.9 jit_solution(4904130484406290863)
XLA Ops:
  5.2 7.4 %shard_map.148 = (f32[64,32,128]{2,1,0:T(8,128)}, f32[16,32,128]{2,1,0:T(8,128)}) custom-call(f32[16,64]{1,0:T(8,128)} %b_ref.1, f32[16,64]{1,0:T(8,128)} %c_ref.1, f32[64,32,128]{2,1,0:T(8,128)} %bitcast.57, f32[64,32,128]{2,1,0:T(8,128)} %bitcast.58, f32[16,32,128]{2,1,0:T(8,128)} %bitcast.59), custom_call_target="tpu_custom_call" | custom-call | tf_op jit(solution)/shard_map/pallas_call | solution.py:49
  12.6 1.8 copy.75
  14.4 3.2 %collective-permute-start.4 = (f32[16,4096]{1,0:T(8,128)}, f32[16,4096]{1,0:T(8,128)}, u32[]{:S(2)}, u32[]{:S(2)}) collective-permute-start(f32[16,4096]{1,0:T(8,128)} %bitcast.54), channel_id=1, source_target_pairs={{0,2},{1,3},{2,4},{3,5},{4,6},{5,7},{6,8},{7,9},{8,10},{9,11},{10,... | collective-permute-start | bytes 786440 | tf_op jit(solution)/shard_map/ppermute | solution.py:20
  17.5 4.0 %collective-permute-start.5 = (f32[16,4096]{1,0:T(8,128)}, f32[16,4096]{1,0:T(8,128)}, u32[]{:S(2)}, u32[]{:S(2)}) collective-permute-start(f32[16,4096]{1,0:T(8,128)} %bitcast.54), channel_id=1, source_target_pairs={{0,1},{1,2},{2,3},{3,4},{4,5},{5,6},{6,7},{7,8},{8,9},{9,10},{10,1... | collective-permute-start | bytes 786440 | tf_op jit(solution)/shard_map/ppermute | solution.py:20
  21.5 1.9 reduce_window_sum.22
  24.3 1.9 collective-permute-start.1
  26.3 3.2 %collective-permute-start = (f32[4096]{0:T(1024)S(1)}, f32[4096]{0:T(1024)S(1)}, u32[]{:S(2)}, u32[]{:S(2)}) collective-permute-start(f32[4096]{0:T(1024)S(1)} %bitcast.66), channel_id=1, source_target_pairs={{0,2},{1,3},{2,4},{3,5},{4,6},{5,7},{6,8},{7,9},{8,10},{9,11},{10,... | collective-permute-start | bytes 49160 | tf_op jit(solution)/shard_map/ppermute | solution.py:20
  29.5 3.1 %collective-permute-start.9 = (bf16[64,2048]{1,0:T(8,128)(2,1)}, bf16[64,2048]{1,0:T(8,128)(2,1)S(1)}, u32[]{:S(2)}, u32[]{:S(2)}) collective-permute-start(bf16[64,2048]{1,0:T(8,128)(2,1)} %param.19), channel_id=1, source_target_pairs={{0,2},{1,3},{2,4},{3,5},{4,6},{5,7},{6,8},{7,9},{8,10},{9,11},{10,... | collective-permute-start | bytes 786440 | tf_op jit(solution)/shard_map/ppermute | solution.py:20
  33.9 2.6 %collective-permute-start.10 = (bf16[64,2048]{1,0:T(8,128)(2,1)}, bf16[64,2048]{1,0:T(8,128)(2,1)}, u32[]{:S(2)}, u32[]{:S(2)}) collective-permute-start(bf16[64,2048]{1,0:T(8,128)(2,1)} %param.19), channel_id=1, source_target_pairs={{0,1},{1,2},{2,3},{3,4},{4,5},{5,6},{6,7},{7,8},{8,9},{9,10},{10,1... | collective-permute-start | bytes 786440 | tf_op jit(solution)/shard_map/ppermute | solution.py:20
  36.5 1.9 collective-permute-start.2
  38.5 4.5 %collective-permute-done.2 = f32[4096]{0:T(1024)S(1)} collective-permute-done((f32[4096]{0:T(1024)S(1)}, f32[4096]{0:T(1024)S(1)}, u32[]{:S(2)}, u32[]{:S(2)}) %collective-permute-start.2) | collective-permute-done | bytes 16416 | tf_op jit(solution)/shard_map/ppermute | solution.py:20
  43.0 1.9 collective-permute-start.3
  44.9 1.4 compare_and_fusion
  50.5 4.0 %collective-permute-start.6 = (f32[16,4096]{1,0:T(8,128)S(1)}, f32[16,4096]{1,0:T(8,128)S(1)}, u32[]{:S(2)}, u32[]{:S(2)}) collective-permute-start(f32[16,4096]{1,0:T(8,128)S(1)} %multiply_add_fusion.3), channel_id=1, source_target_pairs={{0,2},{1,3},{2,4},{3,5},{4,6},{5,7},{6,8},{7,9},{8,10},{9,11},{10,... | collective-permute-start | bytes 786440 | tf_op jit(solution)/shard_map/ppermute | solution.py:20
  56.5 4.2 %collective-permute-done.6 = f32[16,4096]{1,0:T(8,128)S(1)} collective-permute-done((f32[16,4096]{1,0:T(8,128)S(1)}, f32[16,4096]{1,0:T(8,128)S(1)}, u32[]{:S(2)}, u32[]{:S(2)}) %collective-permute-start.6) | collective-permute-done | bytes 262176 | tf_op jit(solution)/shard_map/ppermute | solution.py:20
  61.5 1.9 collective-permute-start.7
  63.4 3.9 %fusion.48 = (f32[8,4,64]{2,1,0:T(4,128)}, f32[8,4,64,192]{3,2,1,0:T(8,128)}) fusion(pred[64,192]{1,0:T(8,128)(4,1)} %compare_and_fusion, bf16[64,8,4,128]{3,2,1,0:T(4,128)(2,1)S(1)} %copy-done.7, bf16[192,8,128,1]{2,1,0,3:T(8,128)(2,1)} %bitcast.62), kind=kOutput, calls=%fused_computation.66 | convolution fusion | flops 102236352 | bytes 2510848 | tf_op jit(solution)/shard_map/sub | solution.py:106
  67.3 4.0 %collective-permute-done.7 = f32[16,4096]{1,0:T(8,128)} collective-permute-done((f32[16,4096]{1,0:T(8,128)S(1)}, f32[16,4096]{1,0:T(8,128)}, u32[]{:S(2)}, u32[]{:S(2)}) %collective-permute-start.7) | collective-permute-done | bytes 262176 | tf_op jit(solution)/shard_map/ppermute | solution.py:20
  71.3 1.7 multiply_add_fusion.1
  73.0 2.0 collective-permute-start.8
  75.0 2.1 fusion.3
  77.9 6.9 %collective-permute-done.8 = f32[16,4096]{1,0:T(8,128)} collective-permute-done((f32[16,4096]{1,0:T(8,128)}, f32[16,4096]{1,0:T(8,128)}, u32[]{:S(2)}, u32[]{:S(2)}) %collective-permute-start.8) | collective-permute-done | bytes 262176 | tf_op jit(solution)/shard_map/ppermute | solution.py:20
  85.9 6.4 %multiply_reduce_fusion = f32[64,4096]{1,0:T(8,128)S(1)} fusion(f32[16,4096]{1,0:T(8,128)S(1)} %multiply_add_fusion, f32[64,4096]{1,0:T(8,128)} %reduce_window_sum.22, f32[16,4096]{1,0:T(8,128)S(1)} %copy-done.1, f32[64,16]{1,0:T(8,128)S(1)} %copy-done.14), kind=kLoop, calls=%fused_computation.1 | loop fusion | flops 16515072 | bytes 2625536 | tf_op jit(solution)/shard_map/reduce_sum | solution.py:89
  93.9 57.5 %all_to_all.10 = bf16[16,12,4096]{2,1,0:T(8,128)(2,1)} all-to-all(bf16[16,12,4096]{2,1,0:T(8,128)(2,1)S(1)} %bitcast.55), channel_id=1, replica_groups=mesh['grp'=2,'seq'=16] {'seq'}, dimensions={0} | all-to-all | bytes 3145728 | tf_op jit(solution)/shard_map/all_to_all | solution.py:168
  151.5 3.6 %reshape.136 = bf16[192,4096]{1,0:T(8,128)(2,1)} reshape(bf16[16,12,4096]{2,1,0:T(8,128)(2,1)} %all_to_all.10) | data formatting | bytes 3145728 | tf_op jit(solution)/shard_map/reshape | solution.py:169
  155.0 2.6 %fusion.53 = f32[192,256]{1,0:T(8,128)S(1)} fusion(bf16[192,4096]{1,0:T(8,128)(2,1)} %reshape.136, bf16[4096,256]{1,0:T(8,128)(2,1)} %param.23), kind=kOutput, calls=%fused_computation.67 | convolution fusion | flops 402653184 | bytes 3866624 | tf_op jit(solution)/shard_map/dot_general | solution.py:115
  157.7 5.1 %convolution_convert_fusion = bf16[192,4096]{1,0:T(8,128)(2,1)} fusion(bf16[256,4096]{1,0:T(8,128)(2,1)S(1)} %copy-done, bf16[192,4096]{1,0:T(8,128)(2,1)} %reshape.136, bf16[4096,256]{1,0:T(8,128)(2,1)} %param.24, f32[192,256]{1,0:T(8,128)S(1)} %fusion.53), kind=kOutput, calls=%fused_computation.2 | convolution fusion | flops 806387712 | bytes 7536640 | tf_op jit(solution)/shard_map/dot_general | solution.py:118
  162.8 3.4 %reshape.137 = bf16[16,12,4096]{2,1,0:T(8,128)(2,1)} reshape(bf16[192,4096]{1,0:T(8,128)(2,1)} %convolution_convert_fusion) | data formatting | bytes 3145728 | tf_op jit(solution)/shard_map/reshape | solution.py:172
  166.2 5.3 %all-to-all-start.1 = ((bf16[16,12,4096]{2,1,0:T(8,128)(2,1)}), bf16[16,12,4096]{2,1,0:T(8,128)(2,1)}, u32[]{:S(2)}, u32[]{:S(2)}) async-start(bf16[16,12,4096]{2,1,0:T(8,128)(2,1)} %reshape.137), calls=%async_computation.1 | async-start | bytes 4194304 | tf_op jit(solution)/shard_map/all_to_all | solution.py:171
  171.5 47.5 %all-to-all-done.1 = bf16[16,12,4096]{2,1,0:T(8,128)(2,1)} async-done(((bf16[16,12,4096]{2,1,0:T(8,128)(2,1)}), bf16[16,12,4096]{2,1,0:T(8,128)(2,1)}, u32[]{:S(2)}, u32[]{:S(2)}) %all-to-all-start.1) | async-done | bytes 1572896 | tf_op jit(solution)/shard_map/all_to_all | solution.py:171
  219.0 2.1 convert_reduce_fusion
  221.1 1.8 fusion.1
  (82 shorter events, 17.2 us)
Async XLA Ops:
  0.6 157.1 %copy-start = (bf16[256,4096]{1,0:T(8,128)(2,1)S(1)}, bf16[256,4096]{1,0:T(8,128)(2,1)}, u32[]{:S(2)}) copy-start(bf16[256,4096]{1,0:T(8,128)(2,1)} %param.25) | copy-start | bytes 6291460
  0.6 2.5 %copy-start.2 = (bf16[64,4096]{1,0:T(8,128)(2,1)S(1)}, bf16[64,4096]{1,0:T(8,128)(2,1)}, u32[]{:S(2)}) copy-start(bf16[64,4096]{1,0:T(8,128)(2,1)} %param.14) | copy-start | bytes 1572868
  0.7 2.5 %copy-start.8 = (bf16[64,4096]{1,0:T(8,128)(2,1)S(1)}, bf16[64,4096]{1,0:T(8,128)(2,1)}, u32[]{:S(2)}) copy-start(bf16[64,4096]{1,0:T(8,128)(2,1)} %param.13) | copy-start | bytes 1572868
  3.1 1.3 copy-start.1
  5.2 28.0 %copy-start.17 = (s32[64,2]{0,1:T(2,128)S(1)}, s32[64,2]{0,1:T(2,128)}, u32[]{:S(2)}) copy-start(s32[64,2]{0,1:T(2,128)} %param.21) | copy-start | bytes 1540
  5.2 41.1 %copy-start.13 = (f32[16,64]{1,0:T(8,128)S(1)}, f32[16,64]{1,0:T(8,128)}, u32[]{:S(2)}) copy-start(f32[16,64]{1,0:T(8,128)} %c_ref.1) | copy-start | bytes 12292
  5.2 41.8 %copy-start.6 = (bf16[64,4096]{1,0:T(8,128)(2,1)S(1)}, bf16[64,4096]{1,0:T(8,128)(2,1)}, u32[]{:S(2)}) copy-start(bf16[64,4096]{1,0:T(8,128)(2,1)} %param.18) | copy-start | bytes 1572868
  14.4 35.1 %collective-permute-start.4 = (f32[16,4096]{1,0:T(8,128)}, f32[16,4096]{1,0:T(8,128)}, u32[]{:S(2)}, u32[]{:S(2)}) collective-permute-start(f32[16,4096]{1,0:T(8,128)} %bitcast.54), channel_id=1, source_target_pairs={{0,2},{1,3},{2,4},{3,5},{4,6},{5,7},{6,8},{7,9},{8,10},{9,11},{10,... | collective-permute-start | bytes 786440 | tf_op jit(solution)/shard_map/ppermute | solution.py:20
  17.5 31.9 %collective-permute-start.5 = (f32[16,4096]{1,0:T(8,128)}, f32[16,4096]{1,0:T(8,128)}, u32[]{:S(2)}, u32[]{:S(2)}) collective-permute-start(f32[16,4096]{1,0:T(8,128)} %bitcast.54), channel_id=1, source_target_pairs={{0,1},{1,2},{2,3},{3,4},{4,5},{5,6},{6,7},{7,8},{8,9},{9,10},{10,1... | collective-permute-start | bytes 786440 | tf_op jit(solution)/shard_map/ppermute | solution.py:20
  23.4 32.1 %copy-start.10 = (bf16[64,2048]{1,0:T(8,128)(2,1)S(1)}, bf16[64,2048]{1,0:T(8,128)(2,1)}, u32[]{:S(2)}) copy-start(bf16[64,2048]{1,0:T(8,128)(2,1)} %param.19) | copy-start | bytes 786436
  24.3 9.6 %collective-permute-start.1 = (f32[4096]{0:T(1024)S(1)}, f32[4096]{0:T(1024)S(1)}, u32[]{:S(2)}, u32[]{:S(2)}) collective-permute-start(f32[4096]{0:T(1024)S(1)} %bitcast.65), channel_id=1, source_target_pairs={{0,1},{1,2},{2,3},{3,4},{4,5},{5,6},{6,7},{7,8},{8,9},{9,10},{10,1... | collective-permute-start | bytes 49160 | tf_op jit(solution)/shard_map/ppermute | solution.py:20
  26.3 10.2 %collective-permute-start = (f32[4096]{0:T(1024)S(1)}, f32[4096]{0:T(1024)S(1)}, u32[]{:S(2)}, u32[]{:S(2)}) collective-permute-start(f32[4096]{0:T(1024)S(1)} %bitcast.66), channel_id=1, source_target_pairs={{0,2},{1,3},{2,4},{3,5},{4,6},{5,7},{6,8},{7,9},{8,10},{9,11},{10,... | collective-permute-start | bytes 49160 | tf_op jit(solution)/shard_map/ppermute | solution.py:20
  29.5 25.0 %collective-permute-start.9 = (bf16[64,2048]{1,0:T(8,128)(2,1)}, bf16[64,2048]{1,0:T(8,128)(2,1)S(1)}, u32[]{:S(2)}, u32[]{:S(2)}) collective-permute-start(bf16[64,2048]{1,0:T(8,128)(2,1)} %param.19), channel_id=1, source_target_pairs={{0,2},{1,3},{2,4},{3,5},{4,6},{5,7},{6,8},{7,9},{8,10},{9,11},{10,... | collective-permute-start | bytes 786440 | tf_op jit(solution)/shard_map/ppermute | solution.py:20
  33.9 20.6 %collective-permute-start.10 = (bf16[64,2048]{1,0:T(8,128)(2,1)}, bf16[64,2048]{1,0:T(8,128)(2,1)}, u32[]{:S(2)}, u32[]{:S(2)}) collective-permute-start(bf16[64,2048]{1,0:T(8,128)(2,1)} %param.19), channel_id=1, source_target_pairs={{0,1},{1,2},{2,3},{3,4},{4,5},{5,6},{6,7},{7,8},{8,9},{9,10},{10,1... | collective-permute-start | bytes 786440 | tf_op jit(solution)/shard_map/ppermute | solution.py:20
  36.5 19.1 %copy-start.11 = (f32[4096]{0:T(1024)}, f32[4096]{0:T(1024)S(1)}, u32[]{:S(2)}) copy-start(f32[4096]{0:T(1024)S(1)} %add.63) | copy-start | bytes 49156
  36.5 6.4 %collective-permute-start.2 = (f32[4096]{0:T(1024)S(1)}, f32[4096]{0:T(1024)S(1)}, u32[]{:S(2)}, u32[]{:S(2)}) collective-permute-start(f32[4096]{0:T(1024)S(1)} %add.63), channel_id=1, source_target_pairs={{0,2},{1,3},{2,4},{3,5},{4,6},{5,7},{6,8},{7,9},{8,10},{9,11},{10,... | collective-permute-start | bytes 49160 | tf_op jit(solution)/shard_map/ppermute | solution.py:20
  43.0 5.8 %collective-permute-start.3 = (f32[4096]{0:T(1024)S(1)}, f32[4096]{0:T(1024)S(1)}, u32[]{:S(2)}, u32[]{:S(2)}) collective-permute-start(f32[4096]{0:T(1024)S(1)} %add.64), channel_id=1, source_target_pairs={{0,4},{1,5},{2,6},{3,7},{4,8},{5,9},{6,10},{7,11},{8,12},{9,13},{1... | collective-permute-start | bytes 49160 | tf_op jit(solution)/shard_map/ppermute | solution.py:20
  50.5 10.2 %collective-permute-start.6 = (f32[16,4096]{1,0:T(8,128)S(1)}, f32[16,4096]{1,0:T(8,128)S(1)}, u32[]{:S(2)}, u32[]{:S(2)}) collective-permute-start(f32[16,4096]{1,0:T(8,128)S(1)} %multiply_add_fusion.3), channel_id=1, source_target_pairs={{0,2},{1,3},{2,4},{3,5},{4,6},{5,7},{6,8},{7,9},{8,10},{9,11},{10,... | collective-permute-start | bytes 786440 | tf_op jit(solution)/shard_map/ppermute | solution.py:20
  55.6 7.9 %copy-start.7 = (bf16[64,8,4,128]{3,2,1,0:T(4,128)(2,1)S(1)}, bf16[64,8,4,128]{3,2,1,0:T(4,128)(2,1)}, u32[]{:S(2)}) copy-start(bf16[64,8,4,128]{3,2,1,0:T(4,128)(2,1)} %reshape.134) | copy-start | bytes 1572868
  61.5 9.8 %collective-permute-start.7 = (f32[16,4096]{1,0:T(8,128)S(1)}, f32[16,4096]{1,0:T(8,128)}, u32[]{:S(2)}, u32[]{:S(2)}) collective-permute-start(f32[16,4096]{1,0:T(8,128)S(1)} %multiply_add_fusion.2), channel_id=1, source_target_pairs={{0,4},{1,5},{2,6},{3,7},{4,8},{5,9},{6,10},{7,11},{8,12},{9,13},{1... | collective-permute-start | bytes 786440 | tf_op jit(solution)/shard_map/ppermute | solution.py:20
  73.0 11.8 %collective-permute-start.8 = (f32[16,4096]{1,0:T(8,128)}, f32[16,4096]{1,0:T(8,128)}, u32[]{:S(2)}, u32[]{:S(2)}) collective-permute-start(f32[16,4096]{1,0:T(8,128)} %multiply_add_fusion.1), channel_id=1, source_target_pairs={{0,8},{1,9},{2,10},{3,11},{4,12},{5,13},{6,14},{7,15},{16,24},{17,... | collective-permute-start | bytes 786440 | tf_op jit(solution)/shard_map/ppermute | solution.py:20
  77.0 7.7 %copy-start.12 = (f32[4096]{0:T(1024)S(1)}, f32[4096]{0:T(1024)}, u32[]{:S(2)}) copy-start(f32[4096]{0:T(1024)} %add.65) | copy-start | bytes 49156
  77.1 8.8 %copy-start.14 = (f32[64,16]{1,0:T(8,128)S(1)}, f32[64,16]{1,0:T(8,128)}, u32[]{:S(2)}) copy-start(f32[64,16]{1,0:T(8,128)} %copy.31) | copy-start | bytes 12292
  77.9 15.1 %copy-start.4 = (bf16[64,4096]{1,0:T(8,128)(2,1)}, bf16[64,4096]{1,0:T(8,128)(2,1)S(1)}, u32[]{:S(2)}) copy-start(bf16[64,4096]{1,0:T(8,128)(2,1)S(1)} %convert_element_type.70) | copy-start | bytes 1572868
  85.8 6.5 %copy-start.5 = (f32[64,32,128]{2,1,0:T(8,128)S(1)}, f32[64,32,128]{2,1,0:T(8,128)}, u32[]{:S(2)}) copy-start(f32[64,32,128]{2,1,0:T(8,128)} %get-tuple-element.5) | copy-start | bytes 3145732
  92.3 1.0 copy-start.9
  92.3 1.0 copy-start.15
  92.3 1.0 copy-start.16
  93.0 0.9 copy-start.3
  166.2 5.3 %copy-start.18 = (s32[64,2]{0,1:T(2,128)S(1)}, s32[64,2]{0,1:T(2,128)}, u32[]{:S(2)}) copy-start(s32[64,2]{0,1:T(2,128)} %param.21) | copy-start | bytes 1540
  166.2 5.3 %copy-start.19 = (f32[64,2]{0,1:T(2,128)S(1)}, f32[64,2]{0,1:T(2,128)}, u32[]{:S(2)}) copy-start(f32[64,2]{0,1:T(2,128)} %param.22) | copy-start | bytes 1540
  166.2 52.8 %all-to-all-start.1 = ((bf16[16,12,4096]{2,1,0:T(8,128)(2,1)}), bf16[16,12,4096]{2,1,0:T(8,128)(2,1)}, u32[]{:S(2)}, u32[]{:S(2)}) async-start(bf16[16,12,4096]{2,1,0:T(8,128)(2,1)} %reshape.137), calls=%async_computation.1 | async-start | bytes 4194304 | tf_op jit(solution)/shard_map/all_to_all | solution.py:171

commit v6 on v3

--- a/solution.py
+++ b/solution.py
@@ -12,6 +12,7 @@
 HEAD_SIZE = 128
 EXP_WIN = 4
 CAP = 12
+SLOTS = -(-CAP // 16) * 16
 
 
 def shifted(value, axis, by):
@@ -154,7 +155,7 @@
     route_share = jnp.sum(jnp.where(matches, moe_prob[:, :, None], 0.0), axis=1)
     position_rank = jnp.cumsum(routed, axis=0) - 1
     picker = (routed[:, :, None] == 1) & (
-        position_rank[:, :, None] == jnp.arange(CAP, dtype=jnp.int32)[None, None, :]
+        position_rank[:, :, None] == jnp.arange(SLOTS, dtype=jnp.int32)[None, None, :]
     )
     packed = jnp.einsum(
         "tek,td->ekd", picker.astype(jnp.bfloat16), stream, preferred_element_type=jnp.float32
@@ -166,13 +167,13 @@
     returned = lax.all_to_all(
         partial_value.reshape(arrived.shape), "seq", split_axis=0, concat_axis=0, tiled=True
     )
-    summed = jnp.sum(returned.reshape(EXP_WIN, group, CAP, width), axis=1, dtype=jnp.float32)
+    summed = jnp.sum(returned.reshape(EXP_WIN, group, SLOTS, width), axis=1, dtype=jnp.float32)
     weighting = (picker.astype(jnp.float32) * route_share[:, :, None]).reshape(
-        local_tokens, EXP_WIN * CAP
+        local_tokens, EXP_WIN * SLOTS
     )
     combined = jnp.dot(
         weighting,
-        summed.reshape(EXP_WIN * CAP, width),
+        summed.reshape(EXP_WIN * SLOTS, width),
         precision=lax.Precision.HIGHEST,
         preferred_element_type=jnp.float32,
     )

time: 215 us -> 208 us (0.967)
  local copies, waits for them, and re-layouts: 18.7 us -> 13 us
    reshape x2 -> x0, local copies, waits for them, and re-layouts: 6.98 us -> none  [the longest x1 3.57 us: body(): gathered = arrived.reshape(-1, arrived.shape[-1])]
    unnamed x35 -> x39, local copies, waits for them, and re-layouts: 7.37 us -> 8.67 us
where the time goes in v6:
time: 208 us
  blocking collectives  70 us (34%)
  waiting for transfers between devices  61.2 us (29%)
  other arithmetic  15.8 us (8%)
  between operations  14.3 us (7%)
  matrix products  13.3 us (6%)
  local copies, waits for them, and re-layouts  13 us (6%)
  starting transfers between devices  12.6 us (6%)
  Pallas kernels  7.33 us (4%)
    all_to_all x1, blocking collectives, body(): lax.all_to_all(outgoing, 'seq', split_axis=0, concat_axis=0, tiled=True)  51.7 us
    all_to_all x1, waiting for transfers between devices, body(): lax.all_to_all(partial_value.reshape(arrived.shape), 'seq', split_axis=0,...  47.5 us
    all_gather x1, blocking collectives, ssm_correct(): sums = lax.all_gather(running[-1], 'seq')  18.4 us
    all_gather x1, waiting for transfers between devices, ssm_correct(): ends = lax.all_gather(local_end, 'seq')  13.7 us
    unnamed x39, local copies, waits for them, and re-layouts  8.67 us
    pallas_call x1, Pallas kernels, sweep(): pl.pallas_call(scan_kernel, grid=(rows // tile,), in_specs=[pl.BlockSpec(...  7.33 us
    ppermute x2, starting transfers between devices, shifted(): return lax.ppermute(value, axis, pairs)  7.27 us
    dot_general x1, matrix products, expert_partial(): jnp.dot(hidden_act, w_down, preferred_element_type=jnp.float32)  5.95 us
  transfers between devices with their start and end apart: 4, of which 2 were waited for; matrix products, arithmetic and copies ran while one was open for 7% of the time, Pallas kernels for 0%

profile of v6, /device:TPU:11, one launch (start us, length us, event | category | flops | bytes accessed | tf_op | source)
XLA Modules:
  0.0 207.6 jit_solution(10030485909977200582)
XLA Ops:
  7.2 1.3 convert_bitcast_fusion
  8.5 1.2 copy.54
  9.8 1.2 copy.55
  11.0 0.8 copy.56
  11.8 7.3 %shard_map.148 = (f32[64,32,128]{2,1,0:T(8,128)}, f32[16,32,128]{2,1,0:T(8,128)}) custom-call(f32[16,64]{1,0:T(8,128)} %b_ref.1, f32[16,64]{1,0:T(8,128)} %c_ref.1, f32[64,32,128]{2,1,0:T(8,128)} %bitcast.61, f32[64,32,128]{2,1,0:T(8,128)} %bitcast.62, f32[16,32,128]{2,1,0:T(8,128)} %bitcast.64), custom_call_target="tpu_custom_call" | custom-call | tf_op jit(solution)/shard_map/pallas_call | solution.py:50
  19.1 1.7 all_gather_reshape.3
  20.9 3.3 %collective-permute-start = (bf16[64,2048]{1,0:T(8,128)(2,1)}, bf16[64,2048]{1,0:T(8,128)(2,1)}, u32[]{:S(2)}, u32[]{:S(2)}) collective-permute-start(bf16[64,2048]{1,0:T(8,128)(2,1)} %param.19), channel_id=1, source_target_pairs={{0,2},{1,3},{2,4},{3,5},{4,6},{5,7},{6,8},{7,9},{8,10},{9,11},{10,... | collective-permute-start | bytes 786440 | tf_op jit(solution)/shard_map/ppermute | solution.py:21
  24.2 4.0 %collective-permute-start.1 = (bf16[64,2048]{1,0:T(8,128)(2,1)}, bf16[64,2048]{1,0:T(8,128)(2,1)}, u32[]{:S(2)}, u32[]{:S(2)}) collective-permute-start(bf16[64,2048]{1,0:T(8,128)(2,1)} %param.19), channel_id=1, source_target_pairs={{0,1},{1,2},{2,3},{3,4},{4,5},{5,6},{6,7},{7,8},{8,9},{9,10},{10,1... | collective-permute-start | bytes 786440 | tf_op jit(solution)/shard_map/ppermute | solution.py:21
  28.2 1.9 reduce_window_sum.33
  30.0 0.9 slice_bitcast_fusion.2
  30.9 18.4 %all-gather = f32[16,1,4096]{2,1,0:T(1,128)S(1)} all-gather(f32[1,1,4096]{2,1,0:T(1,128)S(1)} %slice_bitcast_fusion.2), channel_id=1, replica_groups=mesh['grp'=2,'seq'=16] {'seq'}, dimensions={0}, use_global_device_ids=true | all-gather | bytes 278528 | tf_op jit(solution)/shard_map/all_gather | solution.py:76
  50.0 0.7 subtract_maximum_fusion
  51.4 1.0 constant_dynamic-update-slice_fusion.2
  52.4 1.0 constant_dynamic-update-slice_fusion.1
  53.4 1.0 constant_dynamic-update-slice_fusion
  54.5 0.8 copy.58
  55.3 2.2 %fusion.49 = (f32[8,4,64]{2,1,0:T(4,128)S(1)}, f32[8,4,64,192]{3,2,1,0:T(8,128)}) fusion(pred[64,192]{1,0:T(8,128)(4,1)S(1)} %compare_and_fusion, bf16[64,8,4,128]{3,2,1,0:T(4,128)(2,1)S(1)} %reshape.153, bf16[192,8,128,1]{2,1,0,3:T(8,128)(2,1)S(1)} %bitcast.66), kind=kOutput, calls=%fused_computation.67 | convolution fusion | flops 102236352 | bytes 2510848 | tf_op jit(solution)/shard_map/sub | solution.py:102
  57.5 2.3 %fusion.3 = bf16[64,8,4,128]{3,0,2,1:T(8,128)(2,1)S(1)} fusion(f32[8,4,64,192]{3,2,1,0:T(8,128)} %get-tuple-element.14, f32[8,4,64]{2,1,0:T(4,128)S(1)} %get-tuple-element.13, bf16[192,8,128,1]{2,1,0,3:T(8,128)(2,1)} %bitcast.67), kind=kOutput, calls=%fused_computation.13 | convolution fusion | flops 101711872 | bytes 2498560 | tf_op jit(solution)/shard_map/kyje,eku->jkyu/dot_general | solution.py:104
  59.8 0.4 copy.44
  60.2 0.4 convert_element_type.70
  60.6 13.7 %all-gather.3.cloned.1.call-done = f32[16,16,4096]{2,1,0:T(8,128)} async-done(((f32[1,16,4096]{2,1,0:T(8,128)}), f32[16,16,4096]{2,1,0:T(8,128)}) %all-gather.3.cloned.1.call-update) | async-done | bytes 4194320 | tf_op jit(solution)/shard_map/all_gather | solution.py:75
  74.3 3.1 %select_reduce_fusion = f32[16,4096]{1,0:T(8,128)S(1)} fusion(f32[16,16,4096]{2,1,0:T(8,128)} %all-gather.3.cloned.1.call-done, f32[16,4096]{1,0:T(8,128)} %subtract_maximum_fusion, f32[16,4096]{1,0:T(8,128)S(1)} %copy-done.7, pred[16]{0:T(512)(128)(4,1)S(1)} %iota_compare_fusion.2), kind=kLoop, calls=%fused_computation.7 | loop fusion | flops 4128768 | bytes 4980752 | tf_op jit(solution)/shard_map/reduce_sum | solution.py:83
  77.5 5.3 %multiply_reduce_fusion = f32[64,4096]{1,0:T(8,128)S(1)} fusion(f32[16,4096]{1,0:T(8,128)S(1)} %select_reduce_fusion, f32[64,4096]{1,0:T(8,128)S(1)} %copy-done.6, f32[16,4096]{1,0:T(8,128)S(1)} %copy-done.7, f32[64,16]{1,0:T(8,128)S(1)} %copy.40), kind=kLoop, calls=%fused_computation.1 | loop fusion | flops 16515072 | bytes 2625536 | tf_op jit(solution)/shard_map/reduce_sum | solution.py:85
  82.8 0.7 fusion.5
  84.5 51.7 %all_to_all.10 = bf16[16,16,4096]{2,1,0:T(8,128)(2,1)S(1)} all-to-all(bf16[16,16,4096]{2,1,0:T(8,128)(2,1)S(1)} %bitcast.59), channel_id=1, replica_groups=mesh['grp'=2,'seq'=16] {'seq'}, dimensions={0} | all-to-all | bytes 4194304 | tf_op jit(solution)/shard_map/all_to_all | solution.py:164
  136.2 1.3 copy-done.1
  137.5 0.7 fusion.54
  138.2 5.9 %convolution_convert_fusion = bf16[256,4096]{1,0:T(8,128)(2,1)} fusion(bf16[256,4096]{1,0:T(8,128)(2,1)S(1)} %copy-done, bf16[256,4096]{1,0:T(8,128)(2,1)} %bitcast.58, bf16[4096,256]{1,0:T(8,128)(2,1)} %param.24, f32[256,256]{1,0:T(8,128)S(1)} %fusion.54), kind=kOutput, calls=%fused_computation.2 | convolution fusion | flops 1075183616 | bytes 8650752 | tf_op jit(solution)/shard_map/dot_general | solution.py:114
  144.1 5.3 %all-to-all-start.1 = ((bf16[16,16,4096]{2,1,0:T(8,128)(2,1)}), bf16[16,16,4096]{2,1,0:T(8,128)(2,1)}, u32[]{:S(2)}, u32[]{:S(2)}) async-start(bf16[16,16,4096]{2,1,0:T(8,128)(2,1)} %bitcast.60), calls=%async_computation.1 | async-start | bytes 4194304 | tf_op jit(solution)/shard_map/all_to_all | solution.py:167
  149.4 47.5 %all-to-all-done.1 = bf16[16,16,4096]{2,1,0:T(8,128)(2,1)} async-done(((bf16[16,16,4096]{2,1,0:T(8,128)(2,1)}), bf16[16,16,4096]{2,1,0:T(8,128)(2,1)}, u32[]{:S(2)}, u32[]{:S(2)}) %all-to-all-start.1) | async-done | bytes 2097184 | tf_op jit(solution)/shard_map/all_to_all | solution.py:167
  196.9 2.1 convert_reduce_fusion
  199.0 1.8 fusion.1
  (54 shorter events, 2.5 us)
Async XLA Ops:
  7.2 131.0 %copy-start = (bf16[256,4096]{1,0:T(8,128)(2,1)S(1)}, bf16[256,4096]{1,0:T(8,128)(2,1)}, u32[]{:S(2)}) copy-start(bf16[256,4096]{1,0:T(8,128)(2,1)} %param.25) | copy-start | bytes 6291460
  7.2 2.5 %copy-start.2 = (bf16[64,4096]{1,0:T(8,128)(2,1)S(1)}, bf16[64,4096]{1,0:T(8,128)(2,1)}, u32[]{:S(2)}) copy-start(bf16[64,4096]{1,0:T(8,128)(2,1)} %param.14) | copy-start | bytes 1572868
  7.2 2.5 %copy-start.10 = (bf16[64,4096]{1,0:T(8,128)(2,1)S(1)}, bf16[64,4096]{1,0:T(8,128)(2,1)}, u32[]{:S(2)}) copy-start(bf16[64,4096]{1,0:T(8,128)(2,1)} %param.13) | copy-start | bytes 1572868
  7.2 67.1 %all-gather.3.cloned.1.call-start = ((), (), s32[]{:S(2)}) async-start(), calls=%async_computation.2 | async-start | bytes 4456448 | tf_op jit(solution)/shard_map/all_gather | solution.py:75
  9.7 1.3 copy-start.7
  19.1 30.6 %copy-start.13 = (s32[64,2]{0,1:T(2,128)S(1)}, s32[64,2]{0,1:T(2,128)}, u32[]{:S(2)}) copy-start(s32[64,2]{0,1:T(2,128)} %param.21) | copy-start | bytes 1540
  20.8 30.0 %copy-start.12 = (f32[16,64]{1,0:T(8,128)S(1)}, f32[16,64]{1,0:T(8,128)}, u32[]{:S(2)}) copy-start(f32[16,64]{1,0:T(8,128)} %c_ref.1) | copy-start | bytes 12292
  20.8 30.1 %copy-start.9 = (bf16[64,4096]{1,0:T(8,128)(2,1)S(1)}, bf16[64,4096]{1,0:T(8,128)(2,1)}, u32[]{:S(2)}) copy-start(bf16[64,4096]{1,0:T(8,128)(2,1)} %param.18) | copy-start | bytes 1572868
  20.9 30.5 %collective-permute-start = (bf16[64,2048]{1,0:T(8,128)(2,1)}, bf16[64,2048]{1,0:T(8,128)(2,1)}, u32[]{:S(2)}, u32[]{:S(2)}) collective-permute-start(bf16[64,2048]{1,0:T(8,128)(2,1)} %param.19), channel_id=1, source_target_pairs={{0,2},{1,3},{2,4},{3,5},{4,6},{5,7},{6,8},{7,9},{8,10},{9,11},{10,... | collective-permute-start | bytes 786440 | tf_op jit(solution)/shard_map/ppermute | solution.py:21
  24.2 28.2 %collective-permute-start.1 = (bf16[64,2048]{1,0:T(8,128)(2,1)}, bf16[64,2048]{1,0:T(8,128)(2,1)}, u32[]{:S(2)}, u32[]{:S(2)}) collective-permute-start(bf16[64,2048]{1,0:T(8,128)(2,1)} %param.19), channel_id=1, source_target_pairs={{0,1},{1,2},{2,3},{3,4},{4,5},{5,6},{6,7},{7,8},{8,9},{9,10},{10,1... | collective-permute-start | bytes 786440 | tf_op jit(solution)/shard_map/ppermute | solution.py:21
  60.6 22.9 %copy-start.5 = (bf16[64,4096]{1,0:T(8,128)(2,1)}, bf16[64,4096]{1,0:T(8,128)(2,1)S(1)}, u32[]{:S(2)}) copy-start(bf16[64,4096]{1,0:T(8,128)(2,1)S(1)} %convert_element_type.70) | copy-start | bytes 1572868
  74.3 3.1 %copy-start.6 = (f32[64,4096]{1,0:T(8,128)S(1)}, f32[64,4096]{1,0:T(8,128)}, u32[]{:S(2)}) copy-start(f32[64,4096]{1,0:T(8,128)} %reduce_window_sum.33) | copy-start | bytes 3145732
  77.5 5.4 %copy-start.8 = (f32[64,32,128]{2,1,0:T(8,128)S(1)}, f32[64,32,128]{2,1,0:T(8,128)}, u32[]{:S(2)}) copy-start(f32[64,32,128]{2,1,0:T(8,128)} %get-tuple-element.5) | copy-start | bytes 3145732
  82.8 1.0 copy-start.11
  83.5 0.9 copy-start.4
  84.5 53.0 %copy-start.3 = (bf16[4096,256]{1,0:T(8,128)(2,1)S(1)}, bf16[4096,256]{1,0:T(8,128)(2,1)}, u32[]{:S(2)}) copy-start(bf16[4096,256]{1,0:T(8,128)(2,1)} %param.23) | copy-start | bytes 6291460
  136.2 1.3 copy-start.1
  144.1 5.3 %copy-start.14 = (f32[64,2]{0,1:T(2,128)S(1)}, f32[64,2]{0,1:T(2,128)}, u32[]{:S(2)}) copy-start(f32[64,2]{0,1:T(2,128)} %param.22) | copy-start | bytes 1540
  144.1 52.8 %all-to-all-start.1 = ((bf16[16,16,4096]{2,1,0:T(8,128)(2,1)}), bf16[16,16,4096]{2,1,0:T(8,128)(2,1)}, u32[]{:S(2)}, u32[]{:S(2)}) async-start(bf16[16,16,4096]{2,1,0:T(8,128)(2,1)} %bitcast.60), calls=%async_computation.1 | async-start | bytes 4194304 | tf_op jit(solution)/shard_map/all_to_all | solution.py:167
Sparse Core Ops, SparseCore 0:
  21.0 53.2 all-gather.2

commit v7 on v6

--- a/solution.py
+++ b/solution.py
@@ -72,7 +72,7 @@
 def ssm_correct(local_read, local_end, deltas, rates, read_rows):
     mine = lax.axis_index("seq")
     running = jnp.cumsum(deltas, axis=0)
-    ends = lax.all_gather(local_end, "seq")
+    ends = lax.all_gather(local_end.astype(jnp.bfloat16), "seq").astype(jnp.float32)
     sums = lax.all_gather(running[-1], "seq")
     devices = sums.shape[0]
     order = jnp.arange(devices, dtype=jnp.int32)

time: 208 us -> 203 us (0.976)
  waiting for transfers between devices: 61.2 us -> 58.2 us
    all_gather x1, blocking collectives: 18.4 us -> 15.3 us  [ssm_correct(): sums = lax.all_gather(running[-1], 'seq')]
    all_gather x1, waiting for transfers between devices: 13.7 us -> 10.6 us  [ssm_correct(): lax.all_gather(local_end.astype(jnp.bfloat16), 'seq').astype(jnp.float32)]
  transfers between devices with their start and end apart: 4 -> 4, of which waited for: 2 -> 2; matrix products, arithmetic and copies ran while one was open for 7% -> 10% of each run, Pallas kernels for 0% -> 4%
where the time goes in v7:
time: 203 us; the launch traced here: 202 us
  blocking collectives  68.2 us (34%)
  waiting for transfers between devices  58.2 us (29%)
  other arithmetic  16.3 us (8%)
  between operations  14.3 us (7%)
  matrix products  13.2 us (7%)
  starting transfers between devices  12.7 us (6%)
  local copies, waits for them, and re-layouts  12 us (6%)
  Pallas kernels  7.34 us (4%)
    all_to_all x1, blocking collectives, body(): lax.all_to_all(outgoing, 'seq', split_axis=0, concat_axis=0, tiled=True)  52.9 us
    all_to_all x1, waiting for transfers between devices, body(): lax.all_to_all(partial_value.reshape(arrived.shape), 'seq', split_axis=0,...  47.5 us
    all_gather x1, blocking collectives, ssm_correct(): sums = lax.all_gather(running[-1], 'seq')  15.3 us
    all_gather x1, waiting for transfers between devices, ssm_correct(): lax.all_gather(local_end.astype(jnp.bfloat16), 'seq').astype(jnp.float32)  10.6 us
    unnamed x39, local copies, waits for them, and re-layouts  8.64 us
    ppermute x2, starting transfers between devices, shifted(): return lax.ppermute(value, axis, pairs)  7.41 us
    pallas_call x1, Pallas kernels, sweep(): pl.pallas_call(scan_kernel, grid=(rows // tile,), in_specs=[pl.BlockSpec(...  7.34 us
    dot_general x1, matrix products, expert_partial(): jnp.dot(hidden_act, w_down, preferred_element_type=jnp.float32)  5.95 us
  transfers between devices with their start and end apart: 4, of which 2 were waited for; matrix products, arithmetic and copies ran while one was open for 10% of the time, Pallas kernels for 4%

profile of v7, /device:TPU:11, one launch (start us, length us, event | category | flops | bytes accessed | tf_op | source)
XLA Modules:
  0.0 202.2 jit_solution(12463435414767696000)
XLA Ops:
  7.2 3.4 %collective-permute-start = (bf16[64,2048]{1,0:T(8,128)(2,1)}, bf16[64,2048]{1,0:T(8,128)(2,1)}, u32[]{:S(2)}, u32[]{:S(2)}) collective-permute-start(bf16[64,2048]{1,0:T(8,128)(2,1)} %param.19), channel_id=1, source_target_pairs={{0,2},{1,3},{2,4},{3,5},{4,6},{5,7},{6,8},{7,9},{8,10},{9,11},{10,... | collective-permute-start | bytes 786440 | tf_op jit(solution)/shard_map/ppermute | solution.py:21
  10.7 4.0 %collective-permute-start.1 = (bf16[64,2048]{1,0:T(8,128)(2,1)}, bf16[64,2048]{1,0:T(8,128)(2,1)}, u32[]{:S(2)}, u32[]{:S(2)}) collective-permute-start(bf16[64,2048]{1,0:T(8,128)(2,1)} %param.19), channel_id=1, source_target_pairs={{0,1},{1,2},{2,3},{3,4},{4,5},{5,6},{6,7},{7,8},{8,9},{9,10},{10,1... | collective-permute-start | bytes 786440 | tf_op jit(solution)/shard_map/ppermute | solution.py:21
  14.7 1.1 convert_bitcast_fusion
  15.8 1.2 copy.54
  17.1 1.2 copy.55
  18.3 0.8 copy.56
  19.1 7.3 %shard_map.148 = (f32[64,32,128]{2,1,0:T(8,128)}, f32[16,32,128]{2,1,0:T(8,128)}) custom-call(f32[16,64]{1,0:T(8,128)} %b_ref.1, f32[16,64]{1,0:T(8,128)} %c_ref.1, f32[64,32,128]{2,1,0:T(8,128)} %bitcast.61, f32[64,32,128]{2,1,0:T(8,128)} %bitcast.62, f32[16,32,128]{2,1,0:T(8,128)} %bitcast.64), custom_call_target="tpu_custom_call" | custom-call | tf_op jit(solution)/shard_map/pallas_call | solution.py:50
  26.4 1.0 convert_element_type.82
  27.4 0.7 convert_element_type.83
  28.1 1.9 reduce_window_sum.33
  30.0 0.9 slice_bitcast_fusion.2
  31.0 15.3 %all-gather = f32[16,1,4096]{2,1,0:T(1,128)S(1)} all-gather(f32[1,1,4096]{2,1,0:T(1,128)S(1)} %slice_bitcast_fusion.2), channel_id=1, replica_groups=mesh['grp'=2,'seq'=16] {'seq'}, dimensions={0}, use_global_device_ids=true | all-gather | bytes 278528 | tf_op jit(solution)/shard_map/all_gather | solution.py:76
  46.9 0.7 subtract_maximum_fusion
  48.3 1.0 constant_dynamic-update-slice_fusion.2
  49.3 1.0 constant_dynamic-update-slice_fusion.1
  50.2 1.0 constant_dynamic-update-slice_fusion
  51.3 0.8 copy.58
  52.2 2.2 %fusion.49 = (f32[8,4,64]{2,1,0:T(4,128)S(1)}, f32[8,4,64,192]{3,2,1,0:T(8,128)}) fusion(pred[64,192]{1,0:T(8,128)(4,1)S(1)} %compare_and_fusion, bf16[64,8,4,128]{3,2,1,0:T(4,128)(2,1)S(1)} %reshape.165, bf16[192,8,128,1]{2,1,0,3:T(8,128)(2,1)S(1)} %bitcast.66), kind=kOutput, calls=%fused_computation.67 | convolution fusion | flops 102236352 | bytes 2510848 | tf_op jit(solution)/shard_map/sub | solution.py:102
  54.4 2.2 %fusion.3 = bf16[64,8,4,128]{3,0,2,1:T(8,128)(2,1)S(1)} fusion(f32[8,4,64,192]{3,2,1,0:T(8,128)} %get-tuple-element.14, f32[8,4,64]{2,1,0:T(4,128)S(1)} %get-tuple-element.13, bf16[192,8,128,1]{2,1,0,3:T(8,128)(2,1)} %bitcast.67), kind=kOutput, calls=%fused_computation.13 | convolution fusion | flops 101711872 | bytes 2498560 | tf_op jit(solution)/shard_map/kyje,eku->jkyu/dot_general | solution.py:104
  56.6 0.4 copy.44
  57.4 10.6 %all-gather.3.cloned.1.call-done = bf16[16,16,4096]{2,1,0:T(8,128)(2,1)} async-done(((bf16[1,16,4096]{2,1,0:T(8,128)(2,1)}), bf16[16,16,4096]{2,1,0:T(8,128)(2,1)}) %all-gather.3.cloned.1.call-update) | async-done | bytes 2097168 | tf_op jit(solution)/shard_map/all_gather | solution.py:75
  68.1 2.7 %select_reduce_fusion = f32[16,4096]{1,0:T(8,128)S(1)} fusion(bf16[16,16,4096]{2,1,0:T(8,128)(2,1)} %all-gather.3.cloned.1.call-done, f32[16,4096]{1,0:T(8,128)} %subtract_maximum_fusion, f32[16,4096]{1,0:T(8,128)S(1)} %copy-done.7, pred[16]{0:T(512)(128)(4,1)S(1)} %iota_compare_fusion.2), kind=kLoop, calls=%fused_computation.7 | loop fusion | flops 5177344 | bytes 2883600 | tf_op jit(solution)/shard_map/reduce_sum | solution.py:83
  70.8 5.4 %multiply_reduce_fusion = f32[64,4096]{1,0:T(8,128)S(1)} fusion(f32[16,4096]{1,0:T(8,128)S(1)} %select_reduce_fusion, f32[64,4096]{1,0:T(8,128)S(1)} %copy-done.6, f32[16,4096]{1,0:T(8,128)S(1)} %copy-done.7, f32[64,16]{1,0:T(8,128)S(1)} %copy.40), kind=kLoop, calls=%fused_computation.1 | loop fusion | flops 16515072 | bytes 2625536 | tf_op jit(solution)/shard_map/reduce_sum | solution.py:85
  76.2 0.7 fusion.5
  77.8 52.9 %all_to_all.10 = bf16[16,16,4096]{2,1,0:T(8,128)(2,1)S(1)} all-to-all(bf16[16,16,4096]{2,1,0:T(8,128)(2,1)S(1)} %bitcast.59), channel_id=1, replica_groups=mesh['grp'=2,'seq'=16] {'seq'}, dimensions={0} | all-to-all | bytes 4194304 | tf_op jit(solution)/shard_map/all_to_all | solution.py:164
  130.8 1.3 copy-done.1
  132.0 0.7 fusion.54
  132.8 5.9 %convolution_convert_fusion = bf16[256,4096]{1,0:T(8,128)(2,1)} fusion(bf16[256,4096]{1,0:T(8,128)(2,1)S(1)} %copy-done, bf16[256,4096]{1,0:T(8,128)(2,1)} %bitcast.58, bf16[4096,256]{1,0:T(8,128)(2,1)} %param.24, f32[256,256]{1,0:T(8,128)S(1)} %fusion.54), kind=kOutput, calls=%fused_computation.2 | convolution fusion | flops 1075183616 | bytes 8650752 | tf_op jit(solution)/shard_map/dot_general | solution.py:114
  138.7 5.3 %all-to-all-start.1 = ((bf16[16,16,4096]{2,1,0:T(8,128)(2,1)}), bf16[16,16,4096]{2,1,0:T(8,128)(2,1)}, u32[]{:S(2)}, u32[]{:S(2)}) async-start(bf16[16,16,4096]{2,1,0:T(8,128)(2,1)} %bitcast.60), calls=%async_computation.1 | async-start | bytes 4194304 | tf_op jit(solution)/shard_map/all_to_all | solution.py:167
  144.0 47.5 %all-to-all-done.1 = bf16[16,16,4096]{2,1,0:T(8,128)(2,1)} async-done(((bf16[16,16,4096]{2,1,0:T(8,128)(2,1)}), bf16[16,16,4096]{2,1,0:T(8,128)(2,1)}, u32[]{:S(2)}, u32[]{:S(2)}) %all-to-all-start.1) | async-done | bytes 2097184 | tf_op jit(solution)/shard_map/all_to_all | solution.py:167
  191.5 2.1 %convert_reduce_fusion = f32[4,16,4096]{2,1,0:T(8,128)S(1)} fusion(bf16[16,16,4096]{2,1,0:T(8,128)(2,1)} %all-to-all-done.1), kind=kLoop, calls=%fused_computation.6 | loop fusion | flops 1835008 | bytes 3145728 | tf_op jit(solution)/shard_map/reduce_sum | solution.py:170
  193.6 1.8 fusion.1
  (55 shorter events, 2.9 us)
Async XLA Ops:
  7.2 125.6 %copy-start = (bf16[256,4096]{1,0:T(8,128)(2,1)S(1)}, bf16[256,4096]{1,0:T(8,128)(2,1)}, u32[]{:S(2)}) copy-start(bf16[256,4096]{1,0:T(8,128)(2,1)} %param.25) | copy-start | bytes 6291460
  7.2 9.8 %copy-start.2 = (bf16[64,4096]{1,0:T(8,128)(2,1)S(1)}, bf16[64,4096]{1,0:T(8,128)(2,1)}, u32[]{:S(2)}) copy-start(bf16[64,4096]{1,0:T(8,128)(2,1)} %param.14) | copy-start | bytes 1572868
  7.2 9.8 %copy-start.10 = (bf16[64,4096]{1,0:T(8,128)(2,1)S(1)}, bf16[64,4096]{1,0:T(8,128)(2,1)}, u32[]{:S(2)}) copy-start(bf16[64,4096]{1,0:T(8,128)(2,1)} %param.13) | copy-start | bytes 1572868
  7.2 60.9 %all-gather.3.cloned.1.call-start = ((), (), s32[]{:S(2)}) async-start(), calls=%async_computation.2 | async-start | bytes 2228224 | tf_op jit(solution)/shard_map/all_gather | solution.py:75
  7.2 41.0 %collective-permute-start = (bf16[64,2048]{1,0:T(8,128)(2,1)}, bf16[64,2048]{1,0:T(8,128)(2,1)}, u32[]{:S(2)}, u32[]{:S(2)}) collective-permute-start(bf16[64,2048]{1,0:T(8,128)(2,1)} %param.19), channel_id=1, source_target_pairs={{0,2},{1,3},{2,4},{3,5},{4,6},{5,7},{6,8},{7,9},{8,10},{9,11},{10,... | collective-permute-start | bytes 786440 | tf_op jit(solution)/shard_map/ppermute | solution.py:21
  10.7 38.6 %collective-permute-start.1 = (bf16[64,2048]{1,0:T(8,128)(2,1)}, bf16[64,2048]{1,0:T(8,128)(2,1)}, u32[]{:S(2)}, u32[]{:S(2)}) collective-permute-start(bf16[64,2048]{1,0:T(8,128)(2,1)} %param.19), channel_id=1, source_target_pairs={{0,1},{1,2},{2,3},{3,4},{4,5},{5,6},{6,7},{7,8},{8,9},{9,10},{10,1... | collective-permute-start | bytes 786440 | tf_op jit(solution)/shard_map/ppermute | solution.py:21
  17.0 1.3 copy-start.7
  26.4 20.2 %copy-start.13 = (s32[64,2]{0,1:T(2,128)S(1)}, s32[64,2]{0,1:T(2,128)}, u32[]{:S(2)}) copy-start(s32[64,2]{0,1:T(2,128)} %param.21) | copy-start | bytes 1540
  28.1 19.6 %copy-start.9 = (bf16[64,4096]{1,0:T(8,128)(2,1)S(1)}, bf16[64,4096]{1,0:T(8,128)(2,1)}, u32[]{:S(2)}) copy-start(bf16[64,4096]{1,0:T(8,128)(2,1)} %param.18) | copy-start | bytes 1572868
  28.1 20.0 %copy-start.12 = (f32[16,64]{1,0:T(8,128)S(1)}, f32[16,64]{1,0:T(8,128)}, u32[]{:S(2)}) copy-start(f32[16,64]{1,0:T(8,128)} %c_ref.1) | copy-start | bytes 12292
  57.4 19.5 %copy-start.5 = (bf16[64,4096]{1,0:T(8,128)(2,1)}, bf16[64,4096]{1,0:T(8,128)(2,1)S(1)}, u32[]{:S(2)}) copy-start(bf16[64,4096]{1,0:T(8,128)(2,1)S(1)} %convert_element_type.89) | copy-start | bytes 1572868
  68.1 2.7 %copy-start.6 = (f32[64,4096]{1,0:T(8,128)S(1)}, f32[64,4096]{1,0:T(8,128)}, u32[]{:S(2)}) copy-start(f32[64,4096]{1,0:T(8,128)} %reduce_window_sum.33) | copy-start | bytes 3145732
  70.8 5.4 %copy-start.8 = (f32[64,32,128]{2,1,0:T(8,128)S(1)}, f32[64,32,128]{2,1,0:T(8,128)}, u32[]{:S(2)}) copy-start(f32[64,32,128]{2,1,0:T(8,128)} %get-tuple-element.5) | copy-start | bytes 3145732
  76.2 1.0 copy-start.11
  76.9 0.9 copy-start.4
  77.8 54.2 %copy-start.3 = (bf16[4096,256]{1,0:T(8,128)(2,1)S(1)}, bf16[4096,256]{1,0:T(8,128)(2,1)}, u32[]{:S(2)}) copy-start(bf16[4096,256]{1,0:T(8,128)(2,1)} %param.23) | copy-start | bytes 6291460
  130.7 1.3 copy-start.1
  138.7 5.3 %copy-start.14 = (f32[64,2]{0,1:T(2,128)S(1)}, f32[64,2]{0,1:T(2,128)}, u32[]{:S(2)}) copy-start(f32[64,2]{0,1:T(2,128)} %param.22) | copy-start | bytes 1540
  138.7 52.8 %all-to-all-start.1 = ((bf16[16,16,4096]{2,1,0:T(8,128)(2,1)}), bf16[16,16,4096]{2,1,0:T(8,128)(2,1)}, u32[]{:S(2)}, u32[]{:S(2)}) async-start(bf16[16,16,4096]{2,1,0:T(8,128)(2,1)} %bitcast.60), calls=%async_computation.1 | async-start | bytes 4194304 | tf_op jit(solution)/shard_map/all_to_all | solution.py:167
Sparse Core Ops, SparseCore 0:
  28.2 39.7 all-gather.2

commit v8 on v7

--- a/solution.py
+++ b/solution.py
@@ -1,3 +1,4 @@
+import functools
 import math
 
 import jax
@@ -5,7 +6,7 @@
 from jax import lax
 from jax.experimental import pallas as pl
 from jax.experimental.pallas import tpu as pltpu
-from jax.sharding import PartitionSpec as P
+from jax.sharding import Mesh, PartitionSpec as P
 
 HQ = 32
 HK = 8
@@ -13,10 +14,10 @@
 EXP_WIN = 4
 CAP = 12
 SLOTS = -(-CAP // 16) * 16
-
-
-def shifted(value, axis, by):
-    devices = lax.axis_size(axis)
+SEQ = ("eg", "kg")
+
+
+def shifted(value, axis, by, devices):
     pairs = [(i, i + by) for i in range(devices) if 0 <= i + by < devices]
     return lax.ppermute(value, axis, pairs)
 
@@ -70,10 +71,10 @@
 
 
 def ssm_correct(local_read, local_end, deltas, rates, read_rows):
-    mine = lax.axis_index("seq")
+    mine = lax.axis_index(SEQ)
     running = jnp.cumsum(deltas, axis=0)
-    ends = lax.all_gather(local_end.astype(jnp.bfloat16), "seq").astype(jnp.float32)
-    sums = lax.all_gather(running[-1], "seq")
+    ends = lax.all_gather(local_end, SEQ)
+    sums = lax.all_gather(running[-1], SEQ)
     devices = sums.shape[0]
     order = jnp.arange(devices, dtype=jnp.int32)
     masked = jnp.where((order < mine)[:, None], sums, 0.0)
@@ -128,15 +129,17 @@
     w_gate,
     w_up,
     w_down,
+    *,
+    seq_count,
 ):
     values = ssm_in.astype(jnp.float32)
     deltas = ssm_dt.astype(jnp.float32)
     local_end, local_read = sweep(values, deltas, ssm_a, ssm_b, ssm_c)
     ssm_out = ssm_correct(local_read, local_end, deltas, ssm_a, ssm_c)
     count = attn_q.shape[0]
-    block_index = lax.axis_index("seq")
-    one_back = shifted(attn_kv, "seq", 1)
-    two_back = shifted(attn_kv, "seq", 2)
+    block_index = lax.axis_index(SEQ)
+    one_back = shifted(attn_kv, SEQ, 1, seq_count)
+    two_back = shifted(attn_kv, SEQ, 2, seq_count)
     window = jnp.concatenate([two_back, one_back, attn_kv], axis=0)
     first_row = block_index * count
     query_pos = first_row + jnp.arange(count, dtype=jnp.int32)
@@ -147,7 +150,6 @@
     ).astype(jnp.bfloat16)
     local_tokens = stream.shape[0]
     width = stream.shape[1]
-    seq_count = lax.axis_size("seq")
     group = seq_count // EXP_WIN
     expert_ids = jnp.arange(EXP_WIN, dtype=jnp.int32)
     matches = moe_routes[:, :, None] == expert_ids[None, None, :]
@@ -160,14 +162,16 @@
     packed = jnp.einsum(
         "tek,td->ekd", picker.astype(jnp.bfloat16), stream, preferred_element_type=jnp.float32
     ).astype(jnp.bfloat16)
-    outgoing = jnp.repeat(packed, group, axis=0)
-    arrived = lax.all_to_all(outgoing, "seq", split_axis=0, concat_axis=0, tiled=True)
-    gathered = arrived.reshape(-1, arrived.shape[-1])
+    by_expert = lax.all_to_all(packed, "eg", split_axis=0, concat_axis=0, tiled=True)
+    outgoing = jnp.broadcast_to(by_expert[None], (group,) + by_expert.shape)
+    arrived = lax.all_to_all(outgoing, "kg", split_axis=0, concat_axis=0, tiled=True)
+    gathered = arrived.reshape(-1, width)
     partial_value = expert_partial(gathered, w_gate, w_up, w_down)
-    returned = lax.all_to_all(
-        partial_value.reshape(arrived.shape), "seq", split_axis=0, concat_axis=0, tiled=True
-    )
-    summed = jnp.sum(returned.reshape(EXP_WIN, group, SLOTS, width), axis=1, dtype=jnp.float32)
+    blocks = lax.all_to_all(
+        partial_value.reshape(arrived.shape), "kg", split_axis=0, concat_axis=0, tiled=True
+    )
+    block_sum = jnp.sum(blocks, axis=0, dtype=jnp.float32)
+    summed = lax.all_to_all(block_sum, "eg", split_axis=0, concat_axis=0, tiled=True)
     weighting = (picker.astype(jnp.float32) * route_share[:, :, None]).reshape(
         local_tokens, EXP_WIN * SLOTS
     )
@@ -182,24 +186,30 @@
 
 
 def solution(mesh):
+    groups = mesh.shape["grp"]
+    seq_count = mesh.shape["seq"]
+    fine = Mesh(
+        mesh.devices.reshape(groups, EXP_WIN, seq_count // EXP_WIN), ("grp",) + SEQ
+    )
+    rows = P(("grp",) + SEQ, None)
     return jax.shard_map(
-        body,
-        mesh=mesh,
+        functools.partial(body, seq_count=seq_count),
+        mesh=fine,
         in_specs=(
-            P(("grp", "seq"), None),
-            P(("grp", "seq"), None),
+            rows,
+            rows,
             P(),
-            P(None, ("grp", "seq")),
-            P(None, ("grp", "seq")),
-            P(("grp", "seq"), None),
-            P(("grp", "seq"), None),
-            P(("grp", "seq"), None),
-            P(("grp", "seq"), None),
-            P(("grp", "seq"), None),
-            P(None, "seq"),
-            P(None, "seq"),
-            P("seq", None),
+            P(None, ("grp",) + SEQ),
+            P(None, ("grp",) + SEQ),
+            rows,
+            rows,
+            rows,
+            rows,
+            rows,
+            P(None, SEQ),
+            P(None, SEQ),
+            P(SEQ, None),
         ),
-        out_specs=(P(("grp", "seq"), None), P(("grp", "seq"), None), P(("grp", "seq"), None)),
+        out_specs=(rows, rows, rows),
         check_vma=False,
     )

time: 203 us -> 210 us (1.034)
  the two profiles are of different devices: /device:TPU:11 before, /device:TPU:0 now
where the time goes in v8:
time: 210 us; the launch traced here: 209 us
  blocking collectives  97.8 us (47%)
  waiting for transfers between devices  36.7 us (17%)
  other arithmetic  15.1 us (7%)
  between operations  14.3 us (7%)
  local copies, waits for them, and re-layouts  13.2 us (6%)
  matrix products  13.2 us (6%)
  starting transfers between devices  11.4 us (5%)
  Pallas kernels  7.33 us (3%)
    all_to_all x1, blocking collectives, body(): lax.all_to_all(partial_value.reshape(arrived.shape), 'kg', split_axis=0,...  29.3 us
    all_to_all x1, blocking collectives, body(): lax.all_to_all(outgoing, 'kg', split_axis=0, concat_axis=0, tiled=True)  28.3 us
    all_to_all x1, waiting for transfers between devices, body(): lax.all_to_all(block_sum, 'eg', split_axis=0, concat_axis=0, tiled=True)  25.6 us
    all_gather x1, blocking collectives, ssm_correct(): sums = lax.all_gather(running[-1], SEQ)  22.5 us
    all_to_all x1, blocking collectives, body(): lax.all_to_all(packed, 'eg', split_axis=0, concat_axis=0, tiled=True)  17.8 us
    all_gather x1, waiting for transfers between devices, ssm_correct(): ends = lax.all_gather(local_end, SEQ)  11.1 us
    unnamed x39, local copies, waits for them, and re-layouts  8.82 us
    ppermute x2, starting transfers between devices, shifted(): return lax.ppermute(value, axis, pairs)  7.83 us
  transfers between devices with their start and end apart: 4, of which 2 were waited for; matrix products, arithmetic and copies ran while one was open for 7% of the time, Pallas kernels for 0%

profile of v8, /device:TPU:0, one launch (start us, length us, event | category | flops | bytes accessed | tf_op | source)
XLA Modules:
  0.0 209.1 jit_solution(15508040530882957305)
XLA Ops:
  7.2 1.3 convert_bitcast_fusion
  8.5 1.2 copy.54
  9.8 1.2 copy.55
  11.0 0.8 copy.56
  11.8 7.3 %shard_map.148 = (f32[64,32,128]{2,1,0:T(8,128)}, f32[16,32,128]{2,1,0:T(8,128)}) custom-call(f32[16,64]{1,0:T(8,128)} %b_ref.1, f32[16,64]{1,0:T(8,128)} %c_ref.1, f32[64,32,128]{2,1,0:T(8,128)} %bitcast.56, f32[64,32,128]{2,1,0:T(8,128)} %bitcast.57, f32[16,32,128]{2,1,0:T(8,128)} %bitcast.59), custom_call_target="tpu_custom_call" | custom-call | tf_op jit(solution)/shard_map/pallas_call | solution.py:51
  19.1 1.7 all_gather_reshape.3
  20.9 5.7 %collective-permute-start = (bf16[64,2048]{1,0:T(8,128)(2,1)}, bf16[64,2048]{1,0:T(8,128)(2,1)}, u32[]{:S(2)}, u32[]{:S(2)}) collective-permute-start(bf16[64,2048]{1,0:T(8,128)(2,1)} %param.19), channel_id=1, source_target_pairs={{0,2},{1,3},{2,4},{3,5},{4,6},{5,7},{6,8},{7,9},{8,10},{9,11},{10,... | collective-permute-start | bytes 786440 | tf_op jit(solution)/shard_map/ppermute | solution.py:22
  26.5 2.2 %collective-permute-start.1 = (bf16[64,2048]{1,0:T(8,128)(2,1)}, bf16[64,2048]{1,0:T(8,128)(2,1)}, u32[]{:S(2)}, u32[]{:S(2)}) collective-permute-start(bf16[64,2048]{1,0:T(8,128)(2,1)} %param.19), channel_id=1, source_target_pairs={{0,1},{1,2},{2,3},{3,4},{4,5},{5,6},{6,7},{7,8},{8,9},{9,10},{10,1... | collective-permute-start | bytes 786440 | tf_op jit(solution)/shard_map/ppermute | solution.py:22
  28.7 1.9 reduce_window_sum.33
  30.6 0.9 slice_bitcast_fusion.2
  31.5 22.5 %all-gather = f32[16,1,4096]{2,1,0:T(1,128)S(1)} all-gather(f32[1,1,4096]{2,1,0:T(1,128)S(1)} %slice_bitcast_fusion.2), channel_id=1, replica_groups=mesh['grp'=2,'eg'=4,'kg'=4] {'eg','kg'}, dimensions={0}, use_global_device_ids=true | all-gather | bytes 278528 | tf_op jit(solution)/shard_map/all_gather | solution.py:77
  54.6 0.7 subtract_maximum_fusion
  56.0 1.0 constant_dynamic-update-slice_fusion.2
  57.0 1.0 constant_dynamic-update-slice_fusion.1
  58.0 1.0 constant_dynamic-update-slice_fusion
  59.1 0.8 copy.58
  59.9 2.2 %fusion.49 = (f32[8,4,64]{2,1,0:T(4,128)S(1)}, f32[8,4,64,192]{3,2,1,0:T(8,128)}) fusion(pred[64,192]{1,0:T(8,128)(4,1)S(1)} %compare_and_fusion, bf16[64,8,4,128]{3,2,1,0:T(4,128)(2,1)S(1)} %reshape.148, bf16[192,8,128,1]{2,1,0,3:T(8,128)(2,1)S(1)} %bitcast.61), kind=kOutput, calls=%fused_computation.67 | convolution fusion | flops 102236352 | bytes 2510848 | tf_op jit(solution)/shard_map/sub | solution.py:103
  62.2 2.2 %fusion.3 = bf16[64,8,4,128]{3,0,2,1:T(8,128)(2,1)S(1)} fusion(f32[8,4,64,192]{3,2,1,0:T(8,128)} %get-tuple-element.14, f32[8,4,64]{2,1,0:T(4,128)S(1)} %get-tuple-element.13, bf16[192,8,128,1]{2,1,0,3:T(8,128)(2,1)} %bitcast.62), kind=kOutput, calls=%fused_computation.13 | convolution fusion | flops 101711872 | bytes 2498560 | tf_op jit(solution)/shard_map/kyje,eku->jkyu/dot_general | solution.py:105
  65.2 11.1 %all-gather.3.cloned.1.call-done = f32[16,16,4096]{2,1,0:T(8,128)} async-done(((f32[1,16,4096]{2,1,0:T(8,128)}), f32[16,16,4096]{2,1,0:T(8,128)}) %all-gather.3.cloned.1.call-update) | async-done | bytes 4194320 | tf_op jit(solution)/shard_map/all_gather | solution.py:76
  76.3 3.1 %select_reduce_fusion = f32[16,4096]{1,0:T(8,128)S(1)} fusion(f32[16,16,4096]{2,1,0:T(8,128)} %all-gather.3.cloned.1.call-done, f32[16,4096]{1,0:T(8,128)} %subtract_maximum_fusion, f32[16,4096]{1,0:T(8,128)S(1)} %copy-done.7, pred[16]{0:T(512)(128)(4,1)S(1)} %iota_compare_fusion.2), kind=kLoop, calls=%fused_computation.7 | loop fusion | flops 4128768 | bytes 4980752 | tf_op jit(solution)/shard_map/reduce_sum | solution.py:84
  79.5 5.3 %multiply_reduce_fusion = f32[64,4096]{1,0:T(8,128)S(1)} fusion(f32[16,4096]{1,0:T(8,128)S(1)} %select_reduce_fusion, f32[64,4096]{1,0:T(8,128)S(1)} %copy-done.6, f32[16,4096]{1,0:T(8,128)S(1)} %copy-done.7, f32[64,16]{1,0:T(8,128)S(1)} %copy.40), kind=kLoop, calls=%fused_computation.1 | loop fusion | flops 16515072 | bytes 2625536 | tf_op jit(solution)/shard_map/reduce_sum | solution.py:86
  84.9 0.7 fusion.5
  86.4 17.8 %all_to_all.20 = bf16[4,16,4096]{2,1,0:T(8,128)(2,1)S(1)} all-to-all(bf16[4,16,4096]{2,1,0:T(8,128)(2,1)S(1)} %convolution_convert_fusion.1), channel_id=1, replica_groups=mesh['grp'=2,'eg'=4,'kg'=4] {'eg'}, dimensions={0} | all-to-all | bytes 1048576 | tf_op jit(solution)/shard_map/all_to_all | solution.py:165
  104.4 28.3 %all_to_all.21 = bf16[4,4,16,4096]{3,2,1,0:T(8,128)(2,1)S(1)} all-to-all(bf16[4,4,16,4096]{3,2,1,0:T(8,128)(2,1)S(1)} %broadcast_in_dim.84), channel_id=1, replica_groups=mesh['grp'=2,'eg'=4,'kg'=4] {'kg'}, dimensions={0} | all-to-all | bytes 4194304 | tf_op jit(solution)/shard_map/all_to_all | solution.py:167
  132.7 1.3 copy-done.1
  134.1 0.7 fusion.54
  134.8 5.9 %convolution_convert_fusion = bf16[256,4096]{1,0:T(8,128)(2,1)} fusion(bf16[256,4096]{1,0:T(8,128)(2,1)S(1)} %copy-done, bf16[256,4096]{1,0:T(8,128)(2,1)} %bitcast.54, bf16[4096,256]{1,0:T(8,128)(2,1)} %param.24, f32[256,256]{1,0:T(8,128)S(1)} %fusion.54), kind=kOutput, calls=%fused_computation.2 | convolution fusion | flops 1075183616 | bytes 8650752 | tf_op jit(solution)/shard_map/dot_general | solution.py:115
  140.7 29.3 %all_to_all.22 = bf16[4,4,16,4096]{3,2,1,0:T(8,128)(2,1)S(1)} all-to-all(bf16[4,4,16,4096]{3,2,1,0:T(8,128)(2,1)} %bitcast.55), channel_id=1, replica_groups=mesh['grp'=2,'eg'=4,'kg'=4] {'kg'}, dimensions={0} | all-to-all | bytes 4194304 | tf_op jit(solution)/shard_map/all_to_all | solution.py:170
  170.0 1.3 convert_reduce_fusion
  171.3 3.5 %all-to-all-start.3 = ((f32[4,16,4096]{2,1,0:T(8,128)}), f32[4,16,4096]{2,1,0:T(8,128)S(1)}, u32[]{:S(2)}, u32[]{:S(2)}) async-start(f32[4,16,4096]{2,1,0:T(8,128)} %convert_reduce_fusion), calls=%async_computation.3 | async-start | bytes 2097152 | tf_op jit(solution)/shard_map/all_to_all | solution.py:174
  174.8 25.6 %all-to-all-done.3 = f32[4,16,4096]{2,1,0:T(8,128)S(1)} async-done(((f32[4,16,4096]{2,1,0:T(8,128)}), f32[4,16,4096]{2,1,0:T(8,128)S(1)}, u32[]{:S(2)}, u32[]{:S(2)}) %all-to-all-start.3) | async-done | bytes 1048608 | tf_op jit(solution)/shard_map/all_to_all | solution.py:174
  200.4 1.8 fusion.1
  (56 shorter events, 3.4 us)
Async XLA Ops:
  7.2 127.6 %copy-start = (bf16[256,4096]{1,0:T(8,128)(2,1)S(1)}, bf16[256,4096]{1,0:T(8,128)(2,1)}, u32[]{:S(2)}) copy-start(bf16[256,4096]{1,0:T(8,128)(2,1)} %param.25) | copy-start | bytes 6291460
  7.2 2.5 %copy-start.2 = (bf16[64,4096]{1,0:T(8,128)(2,1)S(1)}, bf16[64,4096]{1,0:T(8,128)(2,1)}, u32[]{:S(2)}) copy-start(bf16[64,4096]{1,0:T(8,128)(2,1)} %param.14) | copy-start | bytes 1572868
  7.2 2.5 %copy-start.10 = (bf16[64,4096]{1,0:T(8,128)(2,1)S(1)}, bf16[64,4096]{1,0:T(8,128)(2,1)}, u32[]{:S(2)}) copy-start(bf16[64,4096]{1,0:T(8,128)(2,1)} %param.13) | copy-start | bytes 1572868
  7.2 69.1 %all-gather.3.cloned.1.call-start = ((), (), s32[]{:S(2)}) async-start(), calls=%async_computation.4 | async-start | bytes 4456448 | tf_op jit(solution)/shard_map/all_gather | solution.py:76
  9.7 1.3 copy-start.7
  19.1 35.3 %copy-start.13 = (s32[64,2]{0,1:T(2,128)S(1)}, s32[64,2]{0,1:T(2,128)}, u32[]{:S(2)}) copy-start(s32[64,2]{0,1:T(2,128)} %param.21) | copy-start | bytes 1540
  20.8 34.6 %copy-start.12 = (f32[16,64]{1,0:T(8,128)S(1)}, f32[16,64]{1,0:T(8,128)}, u32[]{:S(2)}) copy-start(f32[16,64]{1,0:T(8,128)} %c_ref.1) | copy-start | bytes 12292
  20.8 34.7 %copy-start.9 = (bf16[64,4096]{1,0:T(8,128)(2,1)S(1)}, bf16[64,4096]{1,0:T(8,128)(2,1)}, u32[]{:S(2)}) copy-start(bf16[64,4096]{1,0:T(8,128)(2,1)} %param.18) | copy-start | bytes 1572868
  20.9 35.1 %collective-permute-start = (bf16[64,2048]{1,0:T(8,128)(2,1)}, bf16[64,2048]{1,0:T(8,128)(2,1)}, u32[]{:S(2)}, u32[]{:S(2)}) collective-permute-start(bf16[64,2048]{1,0:T(8,128)(2,1)} %param.19), channel_id=1, source_target_pairs={{0,2},{1,3},{2,4},{3,5},{4,6},{5,7},{6,8},{7,9},{8,10},{9,11},{10,... | collective-permute-start | bytes 786440 | tf_op jit(solution)/shard_map/ppermute | solution.py:22
  26.5 30.5 %collective-permute-start.1 = (bf16[64,2048]{1,0:T(8,128)(2,1)}, bf16[64,2048]{1,0:T(8,128)(2,1)}, u32[]{:S(2)}, u32[]{:S(2)}) collective-permute-start(bf16[64,2048]{1,0:T(8,128)(2,1)} %param.19), channel_id=1, source_target_pairs={{0,1},{1,2},{2,3},{3,4},{4,5},{5,6},{6,7},{7,8},{8,9},{9,10},{10,1... | collective-permute-start | bytes 786440 | tf_op jit(solution)/shard_map/ppermute | solution.py:22
  65.2 20.4 %copy-start.5 = (bf16[64,4096]{1,0:T(8,128)(2,1)}, bf16[64,4096]{1,0:T(8,128)(2,1)S(1)}, u32[]{:S(2)}) copy-start(bf16[64,4096]{1,0:T(8,128)(2,1)S(1)} %convert_element_type.67) | copy-start | bytes 1572868
  76.3 3.1 %copy-start.6 = (f32[64,4096]{1,0:T(8,128)S(1)}, f32[64,4096]{1,0:T(8,128)}, u32[]{:S(2)}) copy-start(f32[64,4096]{1,0:T(8,128)} %reduce_window_sum.33) | copy-start | bytes 3145732
  79.5 5.4 %copy-start.8 = (f32[64,32,128]{2,1,0:T(8,128)S(1)}, f32[64,32,128]{2,1,0:T(8,128)}, u32[]{:S(2)}) copy-start(f32[64,32,128]{2,1,0:T(8,128)} %get-tuple-element.5) | copy-start | bytes 3145732
  84.9 1.0 copy-start.11
  85.6 0.8 copy-start.4
  104.4 29.7 %copy-start.3 = (bf16[4096,256]{1,0:T(8,128)(2,1)S(1)}, bf16[4096,256]{1,0:T(8,128)(2,1)}, u32[]{:S(2)}) copy-start(bf16[4096,256]{1,0:T(8,128)(2,1)} %param.23) | copy-start | bytes 6291460
  132.7 1.4 copy-start.1
  170.0 4.9 %copy-start.14 = (f32[64,2]{0,1:T(2,128)S(1)}, f32[64,2]{0,1:T(2,128)}, u32[]{:S(2)}) copy-start(f32[64,2]{0,1:T(2,128)} %param.22) | copy-start | bytes 1540
  171.3 29.1 %all-to-all-start.3 = ((f32[4,16,4096]{2,1,0:T(8,128)}), f32[4,16,4096]{2,1,0:T(8,128)S(1)}, u32[]{:S(2)}, u32[]{:S(2)}) async-start(f32[4,16,4096]{2,1,0:T(8,128)} %convert_reduce_fusion), calls=%async_computation.3 | async-start | bytes 2097152 | tf_op jit(solution)/shard_map/all_to_all | solution.py:174
Sparse Core Ops, SparseCore 0:
  21.0 55.3 all-gather.2

commit v9 on v8

--- a/solution.py
+++ b/solution.py
@@ -167,11 +167,11 @@
     arrived = lax.all_to_all(outgoing, "kg", split_axis=0, concat_axis=0, tiled=True)
     gathered = arrived.reshape(-1, width)
     partial_value = expert_partial(gathered, w_gate, w_up, w_down)
-    blocks = lax.all_to_all(
-        partial_value.reshape(arrived.shape), "kg", split_axis=0, concat_axis=0, tiled=True
-    )
-    block_sum = jnp.sum(blocks, axis=0, dtype=jnp.float32)
-    summed = lax.all_to_all(block_sum, "eg", split_axis=0, concat_axis=0, tiled=True)
+    by_source = jnp.swapaxes(partial_value.reshape(arrived.shape), 0, 1)
+    returned = lax.all_to_all(
+        by_source.reshape((seq_count,) + arrived.shape[2:]), SEQ, split_axis=0, concat_axis=0, tiled=True
+    )
+    summed = jnp.sum(returned.reshape(EXP_WIN, group, SLOTS, width), axis=1, dtype=jnp.float32)
     weighting = (picker.astype(jnp.float32) * route_share[:, :, None]).reshape(
         local_tokens, EXP_WIN * SLOTS
     )

time: 210 us -> 206 us (0.981)
  the two profiles are of different devices: /device:TPU:0 before, /device:TPU:11 now
where the time goes in v9:
time: 206 us
  blocking collectives  62.5 us (30%)
  waiting for transfers between devices  61.2 us (30%)
  local copies, waits for them, and re-layouts  16.1 us (8%)
  other arithmetic  15.8 us (8%)
  starting transfers between devices  14.9 us (7%)
  between operations  14.3 us (7%)
  matrix products  13.3 us (6%)
  Pallas kernels  7.33 us (4%)
    all_to_all x1, waiting for transfers between devices, body(): lax.all_to_all(by_source.reshape((seq_count,) + arrived.shape[2:]), SEQ,...  47.5 us
    all_to_all x1, blocking collectives, body(): lax.all_to_all(outgoing, 'kg', split_axis=0, concat_axis=0, tiled=True)  29.1 us
    all_gather x1, blocking collectives, ssm_correct(): sums = lax.all_gather(running[-1], SEQ)  18.4 us
    all_to_all x1, blocking collectives, body(): lax.all_to_all(packed, 'eg', split_axis=0, concat_axis=0, tiled=True)  15.1 us
    all_gather x1, waiting for transfers between devices, ssm_correct(): ends = lax.all_gather(local_end, SEQ)  13.7 us
    unnamed x39, local copies, waits for them, and re-layouts  8.67 us
    all_to_all x1, starting transfers between devices, body(): lax.all_to_all(by_source.reshape((seq_count,) + arrived.shape[2:]), SEQ,...  7.58 us
    pallas_call x1, Pallas kernels, sweep(): pl.pallas_call(scan_kernel, grid=(rows // tile,), in_specs=[pl.BlockSpec(...  7.33 us
  transfers between devices with their start and end apart: 4, of which 2 were waited for; matrix products, arithmetic and copies ran while one was open for 7% of the time, Pallas kernels for 0%

profile of v9, /device:TPU:11, one launch (start us, length us, event | category | flops | bytes accessed | tf_op | source)
XLA Modules:
  0.0 205.6 jit_solution(1223383634352480664)
XLA Ops:
  7.2 1.3 convert_bitcast_fusion
  8.5 1.2 copy.57
  9.8 1.2 copy.58
  11.0 0.8 copy.59
  11.8 7.3 %shard_map.148 = (f32[64,32,128]{2,1,0:T(8,128)}, f32[16,32,128]{2,1,0:T(8,128)}) custom-call(f32[16,64]{1,0:T(8,128)} %b_ref.1, f32[16,64]{1,0:T(8,128)} %c_ref.1, f32[64,32,128]{2,1,0:T(8,128)} %bitcast.63, f32[64,32,128]{2,1,0:T(8,128)} %bitcast.64, f32[16,32,128]{2,1,0:T(8,128)} %bitcast.66), custom_call_target="tpu_custom_call" | custom-call | tf_op jit(solution)/shard_map/pallas_call | solution.py:51
  19.1 1.7 all_gather_reshape.3
  20.9 3.3 %collective-permute-start = (bf16[64,2048]{1,0:T(8,128)(2,1)}, bf16[64,2048]{1,0:T(8,128)(2,1)}, u32[]{:S(2)}, u32[]{:S(2)}) collective-permute-start(bf16[64,2048]{1,0:T(8,128)(2,1)} %param.19), channel_id=1, source_target_pairs={{0,2},{1,3},{2,4},{3,5},{4,6},{5,7},{6,8},{7,9},{8,10},{9,11},{10,... | collective-permute-start | bytes 786440 | tf_op jit(solution)/shard_map/ppermute | solution.py:22
  24.2 4.0 %collective-permute-start.1 = (bf16[64,2048]{1,0:T(8,128)(2,1)}, bf16[64,2048]{1,0:T(8,128)(2,1)}, u32[]{:S(2)}, u32[]{:S(2)}) collective-permute-start(bf16[64,2048]{1,0:T(8,128)(2,1)} %param.19), channel_id=1, source_target_pairs={{0,1},{1,2},{2,3},{3,4},{4,5},{5,6},{6,7},{7,8},{8,9},{9,10},{10,1... | collective-permute-start | bytes 786440 | tf_op jit(solution)/shard_map/ppermute | solution.py:22
  28.2 1.9 reduce_window_sum.33
  30.0 0.9 slice_bitcast_fusion.2
  30.9 18.4 %all-gather = f32[16,1,4096]{2,1,0:T(1,128)S(1)} all-gather(f32[1,1,4096]{2,1,0:T(1,128)S(1)} %slice_bitcast_fusion.2), channel_id=1, replica_groups=mesh['grp'=2,'eg'=4,'kg'=4] {'eg','kg'}, dimensions={0}, use_global_device_ids=true | all-gather | bytes 278528 | tf_op jit(solution)/shard_map/all_gather | solution.py:77
  50.0 0.7 subtract_maximum_fusion
  51.4 1.0 constant_dynamic-update-slice_fusion.2
  52.4 1.0 constant_dynamic-update-slice_fusion.1
  53.4 1.0 constant_dynamic-update-slice_fusion
  54.5 0.8 copy.61
  55.3 2.2 %fusion.49 = (f32[8,4,64]{2,1,0:T(4,128)S(1)}, f32[8,4,64,192]{3,2,1,0:T(8,128)}) fusion(pred[64,192]{1,0:T(8,128)(4,1)S(1)} %compare_and_fusion, bf16[64,8,4,128]{3,2,1,0:T(4,128)(2,1)S(1)} %reshape.154, bf16[192,8,128,1]{2,1,0,3:T(8,128)(2,1)S(1)} %bitcast.68), kind=kOutput, calls=%fused_computation.67 | convolution fusion | flops 102236352 | bytes 2510848 | tf_op jit(solution)/shard_map/sub | solution.py:103
  57.5 2.3 %fusion.3 = bf16[64,8,4,128]{3,0,2,1:T(8,128)(2,1)S(1)} fusion(f32[8,4,64,192]{3,2,1,0:T(8,128)} %get-tuple-element.14, f32[8,4,64]{2,1,0:T(4,128)S(1)} %get-tuple-element.13, bf16[192,8,128,1]{2,1,0,3:T(8,128)(2,1)} %bitcast.69), kind=kOutput, calls=%fused_computation.13 | convolution fusion | flops 101711872 | bytes 2498560 | tf_op jit(solution)/shard_map/kyje,eku->jkyu/dot_general | solution.py:105
  60.6 13.7 %all-gather.3.cloned.1.call-done = f32[16,16,4096]{2,1,0:T(8,128)} async-done(((f32[1,16,4096]{2,1,0:T(8,128)}), f32[16,16,4096]{2,1,0:T(8,128)}) %all-gather.3.cloned.1.call-update) | async-done | bytes 4194320 | tf_op jit(solution)/shard_map/all_gather | solution.py:76
  74.3 3.1 %select_reduce_fusion = f32[16,4096]{1,0:T(8,128)S(1)} fusion(f32[16,16,4096]{2,1,0:T(8,128)} %all-gather.3.cloned.1.call-done, f32[16,4096]{1,0:T(8,128)} %subtract_maximum_fusion, f32[16,4096]{1,0:T(8,128)S(1)} %copy-done.7, pred[16]{0:T(512)(128)(4,1)S(1)} %iota_compare_fusion.2), kind=kLoop, calls=%fused_computation.7 | loop fusion | flops 4128768 | bytes 4980752 | tf_op jit(solution)/shard_map/reduce_sum | solution.py:84
  77.5 5.3 %multiply_reduce_fusion = f32[64,4096]{1,0:T(8,128)S(1)} fusion(f32[16,4096]{1,0:T(8,128)S(1)} %select_reduce_fusion, f32[64,4096]{1,0:T(8,128)S(1)} %copy-done.6, f32[16,4096]{1,0:T(8,128)S(1)} %copy-done.7, f32[64,16]{1,0:T(8,128)S(1)} %copy.42), kind=kLoop, calls=%fused_computation.1 | loop fusion | flops 16515072 | bytes 2625536 | tf_op jit(solution)/shard_map/reduce_sum | solution.py:86
  82.8 0.7 fusion.5
  84.2 15.1 %all_to_all.15 = bf16[4,16,4096]{2,1,0:T(8,128)(2,1)S(1)} all-to-all(bf16[4,16,4096]{2,1,0:T(8,128)(2,1)S(1)} %convolution_convert_fusion.1), channel_id=1, replica_groups=mesh['grp'=2,'eg'=4,'kg'=4] {'eg'}, dimensions={0} | all-to-all | bytes 1048576 | tf_op jit(solution)/shard_map/all_to_all | solution.py:165
  99.5 29.1 %all_to_all.16 = bf16[4,4,16,4096]{3,2,1,0:T(8,128)(2,1)S(1)} all-to-all(bf16[4,4,16,4096]{3,2,1,0:T(8,128)(2,1)S(1)} %broadcast_in_dim.84), channel_id=1, replica_groups=mesh['grp'=2,'eg'=4,'kg'=4] {'kg'}, dimensions={0} | all-to-all | bytes 4194304 | tf_op jit(solution)/shard_map/all_to_all | solution.py:167
  128.7 1.3 copy-done.1
  129.9 0.7 fusion.54
  130.7 5.9 %convolution_convert_fusion = bf16[256,4096]{1,0:T(8,128)(2,1)} fusion(bf16[256,4096]{1,0:T(8,128)(2,1)S(1)} %copy-done, bf16[256,4096]{1,0:T(8,128)(2,1)} %bitcast.60, bf16[4096,256]{1,0:T(8,128)(2,1)} %param.24, f32[256,256]{1,0:T(8,128)S(1)} %fusion.54), kind=kOutput, calls=%fused_computation.2 | convolution fusion | flops 1075183616 | bytes 8650752 | tf_op jit(solution)/shard_map/dot_general | solution.py:115
  136.6 3.1 %copy.49 = bf16[4,4,16,4096]{3,2,0,1:T(8,128)(2,1)} copy(bf16[4,4,16,4096]{3,2,1,0:T(8,128)(2,1)} %bitcast.62) | data formatting | bytes 4194304 | tf_op jit(solution)/shard_map/reshape | solution.py:170
  139.7 7.6 %all-to-all-start.2 = ((bf16[16,16,4096]{2,1,0:T(8,128)(2,1)}), bf16[16,16,4096]{2,1,0:T(8,128)(2,1)}, u32[]{:S(2)}, u32[]{:S(2)}) async-start(bf16[16,16,4096]{2,1,0:T(8,128)(2,1)} %bitcast.61), calls=%async_computation.2 | async-start | bytes 4194304 | tf_op jit(solution)/shard_map/all_to_all | solution.py:171
  147.3 47.5 %all-to-all-done.2 = bf16[16,16,4096]{2,1,0:T(8,128)(2,1)} async-done(((bf16[16,16,4096]{2,1,0:T(8,128)(2,1)}), bf16[16,16,4096]{2,1,0:T(8,128)(2,1)}, u32[]{:S(2)}, u32[]{:S(2)}) %all-to-all-start.2) | async-done | bytes 2097184 | tf_op jit(solution)/shard_map/all_to_all | solution.py:171
  194.8 2.1 convert_reduce_fusion
  196.9 1.8 fusion.1
  (56 shorter events, 3.3 us)
Async XLA Ops:
  7.2 123.5 %copy-start = (bf16[256,4096]{1,0:T(8,128)(2,1)S(1)}, bf16[256,4096]{1,0:T(8,128)(2,1)}, u32[]{:S(2)}) copy-start(bf16[256,4096]{1,0:T(8,128)(2,1)} %param.25) | copy-start | bytes 6291460
  7.2 2.5 %copy-start.2 = (bf16[64,4096]{1,0:T(8,128)(2,1)S(1)}, bf16[64,4096]{1,0:T(8,128)(2,1)}, u32[]{:S(2)}) copy-start(bf16[64,4096]{1,0:T(8,128)(2,1)} %param.14) | copy-start | bytes 1572868
  7.2 2.5 %copy-start.10 = (bf16[64,4096]{1,0:T(8,128)(2,1)S(1)}, bf16[64,4096]{1,0:T(8,128)(2,1)}, u32[]{:S(2)}) copy-start(bf16[64,4096]{1,0:T(8,128)(2,1)} %param.13) | copy-start | bytes 1572868
  7.2 67.1 %all-gather.3.cloned.1.call-start = ((), (), s32[]{:S(2)}) async-start(), calls=%async_computation.3 | async-start | bytes 4456448 | tf_op jit(solution)/shard_map/all_gather | solution.py:76
  9.7 1.3 copy-start.7
  19.1 30.6 %copy-start.13 = (s32[64,2]{0,1:T(2,128)S(1)}, s32[64,2]{0,1:T(2,128)}, u32[]{:S(2)}) copy-start(s32[64,2]{0,1:T(2,128)} %param.21) | copy-start | bytes 1540
  20.8 30.0 %copy-start.12 = (f32[16,64]{1,0:T(8,128)S(1)}, f32[16,64]{1,0:T(8,128)}, u32[]{:S(2)}) copy-start(f32[16,64]{1,0:T(8,128)} %c_ref.1) | copy-start | bytes 12292
  20.8 30.1 %copy-start.9 = (bf16[64,4096]{1,0:T(8,128)(2,1)S(1)}, bf16[64,4096]{1,0:T(8,128)(2,1)}, u32[]{:S(2)}) copy-start(bf16[64,4096]{1,0:T(8,128)(2,1)} %param.18) | copy-start | bytes 1572868
  20.9 30.5 %collective-permute-start = (bf16[64,2048]{1,0:T(8,128)(2,1)}, bf16[64,2048]{1,0:T(8,128)(2,1)}, u32[]{:S(2)}, u32[]{:S(2)}) collective-permute-start(bf16[64,2048]{1,0:T(8,128)(2,1)} %param.19), channel_id=1, source_target_pairs={{0,2},{1,3},{2,4},{3,5},{4,6},{5,7},{6,8},{7,9},{8,10},{9,11},{10,... | collective-permute-start | bytes 786440 | tf_op jit(solution)/shard_map/ppermute | solution.py:22
  24.2 28.2 %collective-permute-start.1 = (bf16[64,2048]{1,0:T(8,128)(2,1)}, bf16[64,2048]{1,0:T(8,128)(2,1)}, u32[]{:S(2)}, u32[]{:S(2)}) collective-permute-start(bf16[64,2048]{1,0:T(8,128)(2,1)} %param.19), channel_id=1, source_target_pairs={{0,1},{1,2},{2,3},{3,4},{4,5},{5,6},{6,7},{7,8},{8,9},{9,10},{10,1... | collective-permute-start | bytes 786440 | tf_op jit(solution)/shard_map/ppermute | solution.py:22
  60.6 22.9 %copy-start.5 = (bf16[64,4096]{1,0:T(8,128)(2,1)}, bf16[64,4096]{1,0:T(8,128)(2,1)S(1)}, u32[]{:S(2)}) copy-start(bf16[64,4096]{1,0:T(8,128)(2,1)S(1)} %convert_element_type.70) | copy-start | bytes 1572868
  74.3 3.1 %copy-start.6 = (f32[64,4096]{1,0:T(8,128)S(1)}, f32[64,4096]{1,0:T(8,128)}, u32[]{:S(2)}) copy-start(f32[64,4096]{1,0:T(8,128)} %reduce_window_sum.33) | copy-start | bytes 3145732
  77.5 5.4 %copy-start.8 = (f32[64,32,128]{2,1,0:T(8,128)S(1)}, f32[64,32,128]{2,1,0:T(8,128)}, u32[]{:S(2)}) copy-start(f32[64,32,128]{2,1,0:T(8,128)} %get-tuple-element.5) | copy-start | bytes 3145732
  82.8 1.0 copy-start.11
  83.5 16.0 %copy-start.4 = (bf16[64,4096]{1,0:T(8,128)(2,1)}, bf16[64,4096]{1,0:T(8,128)(2,1)S(1)}, u32[]{:S(2)}) copy-start(bf16[64,4096]{1,0:T(8,128)(2,1)S(1)} %fusion.5) | copy-start | bytes 1572868
  99.5 30.4 %copy-start.3 = (bf16[4096,256]{1,0:T(8,128)(2,1)S(1)}, bf16[4096,256]{1,0:T(8,128)(2,1)}, u32[]{:S(2)}) copy-start(bf16[4096,256]{1,0:T(8,128)(2,1)} %param.23) | copy-start | bytes 6291460
  128.7 1.3 copy-start.1
  139.7 7.6 %copy-start.14 = (f32[64,2]{0,1:T(2,128)S(1)}, f32[64,2]{0,1:T(2,128)}, u32[]{:S(2)}) copy-start(f32[64,2]{0,1:T(2,128)} %param.22) | copy-start | bytes 1540
  139.7 55.1 %all-to-all-start.2 = ((bf16[16,16,4096]{2,1,0:T(8,128)(2,1)}), bf16[16,16,4096]{2,1,0:T(8,128)(2,1)}, u32[]{:S(2)}, u32[]{:S(2)}) async-start(bf16[16,16,4096]{2,1,0:T(8,128)(2,1)} %bitcast.61), calls=%async_computation.2 | async-start | bytes 4194304 | tf_op jit(solution)/shard_map/all_to_all | solution.py:171
Sparse Core Ops, SparseCore 0:
  21.0 53.2 all-gather.2

commit v10 on v9

--- a/solution.py
+++ b/solution.py
@@ -167,11 +167,14 @@
     arrived = lax.all_to_all(outgoing, "kg", split_axis=0, concat_axis=0, tiled=True)
     gathered = arrived.reshape(-1, width)
     partial_value = expert_partial(gathered, w_gate, w_up, w_down)
-    by_source = jnp.swapaxes(partial_value.reshape(arrived.shape), 0, 1)
     returned = lax.all_to_all(
-        by_source.reshape((seq_count,) + arrived.shape[2:]), SEQ, split_axis=0, concat_axis=0, tiled=True
-    )
-    summed = jnp.sum(returned.reshape(EXP_WIN, group, SLOTS, width), axis=1, dtype=jnp.float32)
+        partial_value.reshape((seq_count,) + arrived.shape[2:]),
+        ("kg", "eg"),
+        split_axis=0,
+        concat_axis=0,
+        tiled=True,
+    )
+    summed = jnp.sum(returned.reshape(group, EXP_WIN, SLOTS, width), axis=0, dtype=jnp.float32)
     weighting = (picker.astype(jnp.float32) * route_share[:, :, None]).reshape(
         local_tokens, EXP_WIN * SLOTS
     )

time: 206 us -> 206 us (level)
  the two profiles are of different devices: /device:TPU:11 before, /device:TPU:0 now
where the time goes in v10:
time: 206 us; the launch traced here: 205 us
  blocking collectives  68.6 us (33%)
  waiting for transfers between devices  60.6 us (29%)
  other arithmetic  15.8 us (8%)
  between operations  14.3 us (7%)
  matrix products  13.3 us (6%)
  local copies, waits for them, and re-layouts  13 us (6%)
  starting transfers between devices  12.4 us (6%)
  Pallas kernels  7.33 us (4%)
    all_to_all x1, waiting for transfers between devices, body(): lax.all_to_all(partial_value.reshape((seq_count,) + arrived.shape[2:]), (...  49.4 us
    all_to_all x1, blocking collectives, body(): lax.all_to_all(outgoing, 'kg', split_axis=0, concat_axis=0, tiled=True)  28.3 us
    all_gather x1, blocking collectives, ssm_correct(): sums = lax.all_gather(running[-1], SEQ)  22.5 us
    all_to_all x1, blocking collectives, body(): lax.all_to_all(packed, 'eg', split_axis=0, concat_axis=0, tiled=True)  17.8 us
    all_gather x1, waiting for transfers between devices, ssm_correct(): ends = lax.all_gather(local_end, SEQ)  11.1 us
    unnamed x39, local copies, waits for them, and re-layouts  8.65 us
    ppermute x2, starting transfers between devices, shifted(): return lax.ppermute(value, axis, pairs)  7.83 us
    pallas_call x1, Pallas kernels, sweep(): pl.pallas_call(scan_kernel, grid=(rows // tile,), in_specs=[pl.BlockSpec(...  7.33 us
  transfers between devices with their start and end apart: 4, of which 2 were waited for; matrix products, arithmetic and copies ran while one was open for 7% of the time, Pallas kernels for 0%

profile of v10, /device:TPU:0, one launch (start us, length us, event | category | flops | bytes accessed | tf_op | source)
XLA Modules:
  0.0 205.4 jit_solution(5541473120486646409)
XLA Ops:
  7.2 1.3 convert_bitcast_fusion
  8.5 1.2 copy.54
  9.8 1.2 copy.55
  11.0 0.8 copy.56
  11.8 7.3 %shard_map.148 = (f32[64,32,128]{2,1,0:T(8,128)}, f32[16,32,128]{2,1,0:T(8,128)}) custom-call(f32[16,64]{1,0:T(8,128)} %b_ref.1, f32[16,64]{1,0:T(8,128)} %c_ref.1, f32[64,32,128]{2,1,0:T(8,128)} %bitcast.58, f32[64,32,128]{2,1,0:T(8,128)} %bitcast.59, f32[16,32,128]{2,1,0:T(8,128)} %bitcast.61), custom_call_target="tpu_custom_call" | custom-call | tf_op jit(solution)/shard_map/pallas_call | solution.py:51
  19.1 1.7 all_gather_reshape.3
  20.9 5.7 %collective-permute-start = (bf16[64,2048]{1,0:T(8,128)(2,1)}, bf16[64,2048]{1,0:T(8,128)(2,1)}, u32[]{:S(2)}, u32[]{:S(2)}) collective-permute-start(bf16[64,2048]{1,0:T(8,128)(2,1)} %param.19), channel_id=1, source_target_pairs={{0,2},{1,3},{2,4},{3,5},{4,6},{5,7},{6,8},{7,9},{8,10},{9,11},{10,... | collective-permute-start | bytes 786440 | tf_op jit(solution)/shard_map/ppermute | solution.py:22
  26.5 2.2 %collective-permute-start.1 = (bf16[64,2048]{1,0:T(8,128)(2,1)}, bf16[64,2048]{1,0:T(8,128)(2,1)}, u32[]{:S(2)}, u32[]{:S(2)}) collective-permute-start(bf16[64,2048]{1,0:T(8,128)(2,1)} %param.19), channel_id=1, source_target_pairs={{0,1},{1,2},{2,3},{3,4},{4,5},{5,6},{6,7},{7,8},{8,9},{9,10},{10,1... | collective-permute-start | bytes 786440 | tf_op jit(solution)/shard_map/ppermute | solution.py:22
  28.7 1.9 reduce_window_sum.33
  30.6 0.9 slice_bitcast_fusion.2
  31.5 22.5 %all-gather = f32[16,1,4096]{2,1,0:T(1,128)S(1)} all-gather(f32[1,1,4096]{2,1,0:T(1,128)S(1)} %slice_bitcast_fusion.2), channel_id=1, replica_groups=mesh['grp'=2,'eg'=4,'kg'=4] {'eg','kg'}, dimensions={0}, use_global_device_ids=true | all-gather | bytes 278528 | tf_op jit(solution)/shard_map/all_gather | solution.py:77
  54.6 0.7 subtract_maximum_fusion
  56.0 1.0 constant_dynamic-update-slice_fusion.2
  57.0 1.0 constant_dynamic-update-slice_fusion.1
  58.0 1.0 constant_dynamic-update-slice_fusion
  59.1 0.8 copy.58
  59.9 2.2 %fusion.49 = (f32[8,4,64]{2,1,0:T(4,128)S(1)}, f32[8,4,64,192]{3,2,1,0:T(8,128)}) fusion(pred[64,192]{1,0:T(8,128)(4,1)S(1)} %compare_and_fusion, bf16[64,8,4,128]{3,2,1,0:T(4,128)(2,1)S(1)} %reshape.151, bf16[192,8,128,1]{2,1,0,3:T(8,128)(2,1)S(1)} %bitcast.63), kind=kOutput, calls=%fused_computation.67 | convolution fusion | flops 102236352 | bytes 2510848 | tf_op jit(solution)/shard_map/sub | solution.py:103
  62.2 2.2 %fusion.3 = bf16[64,8,4,128]{3,0,2,1:T(8,128)(2,1)S(1)} fusion(f32[8,4,64,192]{3,2,1,0:T(8,128)} %get-tuple-element.14, f32[8,4,64]{2,1,0:T(4,128)S(1)} %get-tuple-element.13, bf16[192,8,128,1]{2,1,0,3:T(8,128)(2,1)} %bitcast.64), kind=kOutput, calls=%fused_computation.13 | convolution fusion | flops 101711872 | bytes 2498560 | tf_op jit(solution)/shard_map/kyje,eku->jkyu/dot_general | solution.py:105
  64.4 0.4 copy.44
  65.2 11.1 %all-gather.3.cloned.1.call-done = f32[16,16,4096]{2,1,0:T(8,128)} async-done(((f32[1,16,4096]{2,1,0:T(8,128)}), f32[16,16,4096]{2,1,0:T(8,128)}) %all-gather.3.cloned.1.call-update) | async-done | bytes 4194320 | tf_op jit(solution)/shard_map/all_gather | solution.py:76
  76.3 3.1 %select_reduce_fusion = f32[16,4096]{1,0:T(8,128)S(1)} fusion(f32[16,16,4096]{2,1,0:T(8,128)} %all-gather.3.cloned.1.call-done, f32[16,4096]{1,0:T(8,128)} %subtract_maximum_fusion, f32[16,4096]{1,0:T(8,128)S(1)} %copy-done.7, pred[16]{0:T(512)(128)(4,1)S(1)} %iota_compare_fusion.2), kind=kLoop, calls=%fused_computation.7 | loop fusion | flops 4128768 | bytes 4980752 | tf_op jit(solution)/shard_map/reduce_sum | solution.py:84
  79.5 5.3 %multiply_reduce_fusion = f32[64,4096]{1,0:T(8,128)S(1)} fusion(f32[16,4096]{1,0:T(8,128)S(1)} %select_reduce_fusion, f32[64,4096]{1,0:T(8,128)S(1)} %copy-done.6, f32[16,4096]{1,0:T(8,128)S(1)} %copy-done.7, f32[64,16]{1,0:T(8,128)S(1)} %copy.40), kind=kLoop, calls=%fused_computation.1 | loop fusion | flops 16515072 | bytes 2625536 | tf_op jit(solution)/shard_map/reduce_sum | solution.py:86
  84.9 0.7 fusion.5
  86.3 17.8 %all_to_all.15 = bf16[4,16,4096]{2,1,0:T(8,128)(2,1)S(1)} all-to-all(bf16[4,16,4096]{2,1,0:T(8,128)(2,1)S(1)} %convolution_convert_fusion.1), channel_id=1, replica_groups=mesh['grp'=2,'eg'=4,'kg'=4] {'eg'}, dimensions={0} | all-to-all | bytes 1048576 | tf_op jit(solution)/shard_map/all_to_all | solution.py:165
  104.3 28.3 %all_to_all.16 = bf16[4,4,16,4096]{3,2,1,0:T(8,128)(2,1)S(1)} all-to-all(bf16[4,4,16,4096]{3,2,1,0:T(8,128)(2,1)S(1)} %broadcast_in_dim.84), channel_id=1, replica_groups=mesh['grp'=2,'eg'=4,'kg'=4] {'kg'}, dimensions={0} | all-to-all | bytes 4194304 | tf_op jit(solution)/shard_map/all_to_all | solution.py:167
  132.6 1.3 copy-done.1
  133.9 0.7 fusion.54
  134.7 5.9 %convolution_convert_fusion = bf16[256,4096]{1,0:T(8,128)(2,1)} fusion(bf16[256,4096]{1,0:T(8,128)(2,1)S(1)} %copy-done, bf16[256,4096]{1,0:T(8,128)(2,1)} %bitcast.56, bf16[4096,256]{1,0:T(8,128)(2,1)} %param.24, f32[256,256]{1,0:T(8,128)S(1)} %fusion.54), kind=kOutput, calls=%fused_computation.2 | convolution fusion | flops 1075183616 | bytes 8650752 | tf_op jit(solution)/shard_map/dot_general | solution.py:115
  140.6 4.6 %all-to-all-start.2 = ((bf16[16,16,4096]{2,1,0:T(8,128)(2,1)}), bf16[16,16,4096]{2,1,0:T(8,128)(2,1)}, u32[]{:S(2)}, u32[]{:S(2)}) async-start(bf16[16,16,4096]{2,1,0:T(8,128)(2,1)} %bitcast.57), calls=%async_computation.2 | async-start | bytes 4194304 | tf_op jit(solution)/shard_map/all_to_all | solution.py:170
  145.2 49.4 %all-to-all-done.2 = bf16[16,16,4096]{2,1,0:T(8,128)(2,1)} async-done(((bf16[16,16,4096]{2,1,0:T(8,128)(2,1)}), bf16[16,16,4096]{2,1,0:T(8,128)(2,1)}, u32[]{:S(2)}, u32[]{:S(2)}) %all-to-all-start.2) | async-done | bytes 2097184 | tf_op jit(solution)/shard_map/all_to_all | solution.py:170
  194.6 2.1 convert_reduce_fusion
  196.7 1.8 fusion.1
  (55 shorter events, 2.9 us)
Async XLA Ops:
  7.2 127.5 %copy-start = (bf16[256,4096]{1,0:T(8,128)(2,1)S(1)}, bf16[256,4096]{1,0:T(8,128)(2,1)}, u32[]{:S(2)}) copy-start(bf16[256,4096]{1,0:T(8,128)(2,1)} %param.25) | copy-start | bytes 6291460
  7.2 2.5 %copy-start.2 = (bf16[64,4096]{1,0:T(8,128)(2,1)S(1)}, bf16[64,4096]{1,0:T(8,128)(2,1)}, u32[]{:S(2)}) copy-start(bf16[64,4096]{1,0:T(8,128)(2,1)} %param.14) | copy-start | bytes 1572868
  7.2 2.5 %copy-start.10 = (bf16[64,4096]{1,0:T(8,128)(2,1)S(1)}, bf16[64,4096]{1,0:T(8,128)(2,1)}, u32[]{:S(2)}) copy-start(bf16[64,4096]{1,0:T(8,128)(2,1)} %param.13) | copy-start | bytes 1572868
  7.2 69.1 %all-gather.3.cloned.1.call-start = ((), (), s32[]{:S(2)}) async-start(), calls=%async_computation.3 | async-start | bytes 4456448 | tf_op jit(solution)/shard_map/all_gather | solution.py:76
  9.7 1.3 copy-start.7
  19.1 35.3 %copy-start.13 = (s32[64,2]{0,1:T(2,128)S(1)}, s32[64,2]{0,1:T(2,128)}, u32[]{:S(2)}) copy-start(s32[64,2]{0,1:T(2,128)} %param.21) | copy-start | bytes 1540
  20.8 34.6 %copy-start.12 = (f32[16,64]{1,0:T(8,128)S(1)}, f32[16,64]{1,0:T(8,128)}, u32[]{:S(2)}) copy-start(f32[16,64]{1,0:T(8,128)} %c_ref.1) | copy-start | bytes 12292
  20.8 34.7 %copy-start.9 = (bf16[64,4096]{1,0:T(8,128)(2,1)S(1)}, bf16[64,4096]{1,0:T(8,128)(2,1)}, u32[]{:S(2)}) copy-start(bf16[64,4096]{1,0:T(8,128)(2,1)} %param.18) | copy-start | bytes 1572868
  20.9 35.1 %collective-permute-start = (bf16[64,2048]{1,0:T(8,128)(2,1)}, bf16[64,2048]{1,0:T(8,128)(2,1)}, u32[]{:S(2)}, u32[]{:S(2)}) collective-permute-start(bf16[64,2048]{1,0:T(8,128)(2,1)} %param.19), channel_id=1, source_target_pairs={{0,2},{1,3},{2,4},{3,5},{4,6},{5,7},{6,8},{7,9},{8,10},{9,11},{10,... | collective-permute-start | bytes 786440 | tf_op jit(solution)/shard_map/ppermute | solution.py:22
  26.5 30.5 %collective-permute-start.1 = (bf16[64,2048]{1,0:T(8,128)(2,1)}, bf16[64,2048]{1,0:T(8,128)(2,1)}, u32[]{:S(2)}, u32[]{:S(2)}) collective-permute-start(bf16[64,2048]{1,0:T(8,128)(2,1)} %param.19), channel_id=1, source_target_pairs={{0,1},{1,2},{2,3},{3,4},{4,5},{5,6},{6,7},{7,8},{8,9},{9,10},{10,1... | collective-permute-start | bytes 786440 | tf_op jit(solution)/shard_map/ppermute | solution.py:22
  65.2 20.4 %copy-start.5 = (bf16[64,4096]{1,0:T(8,128)(2,1)}, bf16[64,4096]{1,0:T(8,128)(2,1)S(1)}, u32[]{:S(2)}) copy-start(bf16[64,4096]{1,0:T(8,128)(2,1)S(1)} %convert_element_type.70) | copy-start | bytes 1572868
  76.3 3.1 %copy-start.6 = (f32[64,4096]{1,0:T(8,128)S(1)}, f32[64,4096]{1,0:T(8,128)}, u32[]{:S(2)}) copy-start(f32[64,4096]{1,0:T(8,128)} %reduce_window_sum.33) | copy-start | bytes 3145732
  79.5 5.4 %copy-start.8 = (f32[64,32,128]{2,1,0:T(8,128)S(1)}, f32[64,32,128]{2,1,0:T(8,128)}, u32[]{:S(2)}) copy-start(f32[64,32,128]{2,1,0:T(8,128)} %get-tuple-element.5) | copy-start | bytes 3145732
  84.9 1.0 copy-start.11
  85.6 18.7 %copy-start.4 = (bf16[64,4096]{1,0:T(8,128)(2,1)}, bf16[64,4096]{1,0:T(8,128)(2,1)S(1)}, u32[]{:S(2)}) copy-start(bf16[64,4096]{1,0:T(8,128)(2,1)S(1)} %fusion.5) | copy-start | bytes 1572868
  104.3 29.6 %copy-start.3 = (bf16[4096,256]{1,0:T(8,128)(2,1)S(1)}, bf16[4096,256]{1,0:T(8,128)(2,1)}, u32[]{:S(2)}) copy-start(bf16[4096,256]{1,0:T(8,128)(2,1)} %param.23) | copy-start | bytes 6291460
  132.6 1.3 copy-start.1
  140.6 4.6 %copy-start.14 = (f32[64,2]{0,1:T(2,128)S(1)}, f32[64,2]{0,1:T(2,128)}, u32[]{:S(2)}) copy-start(f32[64,2]{0,1:T(2,128)} %param.22) | copy-start | bytes 1540
  140.6 54.0 %all-to-all-start.2 = ((bf16[16,16,4096]{2,1,0:T(8,128)(2,1)}), bf16[16,16,4096]{2,1,0:T(8,128)(2,1)}, u32[]{:S(2)}, u32[]{:S(2)}) async-start(bf16[16,16,4096]{2,1,0:T(8,128)(2,1)} %bitcast.57), calls=%async_computation.2 | async-start | bytes 4194304 | tf_op jit(solution)/shard_map/all_to_all | solution.py:170
Sparse Core Ops, SparseCore 0:
  21.0 55.3 all-gather.2

commit v11 on v9

--- a/solution.py
+++ b/solution.py
@@ -37,6 +37,17 @@
         read_ref[t] = total
     for n in range(states):
         end_ref[n] = h[n]
+
+
+def fix_kernel(c_ref, run_ref, read_ref, a_ref, in_ref, out_ref):
+    states = a_ref.shape[0]
+    for t in range(run_ref.shape[0]):
+        r = run_ref[t]
+        total = None
+        for n in range(states):
+            term = c_ref[n, t] * (jnp.exp(r * a_ref[n]) * in_ref[n])
+            total = term if total is None else total + term
+        out_ref[t] = read_ref[t] + total
 
 
 def sweep(values, deltas, rates, inject_rows, read_rows):
@@ -67,7 +78,7 @@
             jax.ShapeDtypeStruct((states, rows, lanes), jnp.float32),
         ],
     )(inject_rows, read_rows, dt3, inj3, a3)
-    return end3.reshape(states, channels), read3.reshape(steps, channels)
+    return end3.reshape(states, channels), read3
 
 
 def ssm_correct(local_read, local_end, deltas, rates, read_rows):
@@ -82,9 +93,30 @@
     after = jnp.maximum(after, 0.0)
     carry = jnp.exp(rates[None] * after[:, None, :]) * ends
     incoming = jnp.sum(jnp.where((order < mine)[:, None, None], carry, 0.0), axis=0)
-    growth = jnp.exp(rates[None] * running[:, None, :]) * incoming[None]
-    fix = jnp.sum(read_rows.T[:, :, None] * growth, axis=1)
-    return (local_read + fix).astype(jnp.bfloat16)
+    steps, rows, lanes = local_read.shape
+    states = rates.shape[0]
+    tile = 8
+    tiled = lambda lead: pl.BlockSpec((lead, tile, lanes), lambda j: (0, j, 0))
+    out3 = pl.pallas_call(
+        fix_kernel,
+        grid=(rows // tile,),
+        in_specs=[
+            pl.BlockSpec(memory_space=pltpu.SMEM),
+            tiled(steps),
+            tiled(steps),
+            tiled(states),
+            tiled(states),
+        ],
+        out_specs=tiled(steps),
+        out_shape=jax.ShapeDtypeStruct((steps, rows, lanes), jnp.float32),
+    )(
+        read_rows,
+        running.reshape(steps, rows, lanes),
+        local_read,
+        rates.reshape(states, rows, lanes),
+        incoming.reshape(states, rows, lanes),
+    )
+    return out3.reshape(steps, rows * lanes).astype(jnp.bfloat16)
 
 
 def attend(queries, window, query_pos, key_pos):

time: 206 us -> 209 us (1.015)
  Pallas kernels: 7.33 us -> 13.2 us
  waiting for transfers between devices: 61.2 us -> 56.4 us
  local copies, waits for them, and re-layouts: 16.1 us -> 20.2 us
  other arithmetic: 15.8 us -> 13.2 us
    pallas_call x0 -> x1, Pallas kernels: none -> 5.86 us  [ssm_correct(): pl.pallas_call(fix_kernel, grid=(rows // tile,), in_specs=[pl.BlockSpec(m...]
    reduce_sum x1 -> x0, other arithmetic: 5.35 us -> none  [ssm_correct(): fix = jnp.sum(read_rows.T[:, :, None] * growth, axis=1)]
    all_gather x1, waiting for transfers between devices: 13.7 us -> 8.91 us  [ssm_correct(): ends = lax.all_gather(local_end, SEQ)]
    unnamed x39 -> x40, local copies, waits for them, and re-layouts: 8.67 us -> 11 us
  transfers between devices with their start and end apart: 4 -> 4, of which waited for: 2 -> 2; matrix products, arithmetic and copies ran while one was open for 7% -> 9% of each run, Pallas kernels for 0% -> 0%
where the time goes in v11:
time: 209 us; the launch traced here: 208 us
  blocking collectives  62.3 us (30%)
  waiting for transfers between devices  56.4 us (27%)
  local copies, waits for them, and re-layouts  20.2 us (10%)
  starting transfers between devices  14.8 us (7%)
  between operations  14.3 us (7%)
  matrix products  13.8 us (7%)
  other arithmetic  13.2 us (6%)
  Pallas kernels  13.2 us (6%)
    all_to_all x1, waiting for transfers between devices, body(): lax.all_to_all(by_source.reshape((seq_count,) + arrived.shape[2:]), SEQ,...  47.5 us
    all_to_all x1, blocking collectives, body(): lax.all_to_all(outgoing, 'kg', split_axis=0, concat_axis=0, tiled=True)  29.1 us
    all_gather x1, blocking collectives, ssm_correct(): sums = lax.all_gather(running[-1], SEQ)  18.1 us
    all_to_all x1, blocking collectives, body(): lax.all_to_all(packed, 'eg', split_axis=0, concat_axis=0, tiled=True)  15.1 us
    unnamed x40, local copies, waits for them, and re-layouts  11 us
    all_gather x1, waiting for transfers between devices, ssm_correct(): ends = lax.all_gather(local_end, SEQ)  8.91 us
    all_to_all x1, starting transfers between devices, body(): lax.all_to_all(by_source.reshape((seq_count,) + arrived.shape[2:]), SEQ,...  7.58 us
    pallas_call x1, Pallas kernels, sweep(): pl.pallas_call(scan_kernel, grid=(rows // tile,), in_specs=[pl.BlockSpec(...  7.33 us
  transfers between devices with their start and end apart: 4, of which 2 were waited for; matrix products, arithmetic and copies ran while one was open for 9% of the time, Pallas kernels for 0%

profile of v11, /device:TPU:11, one launch (start us, length us, event | category | flops | bytes accessed | tf_op | source)
XLA Modules:
  0.0 208.1 jit_solution(13246339322983580756)
XLA Ops:
  7.2 1.9 copy.56
  9.1 1.1 convert_bitcast_fusion
  10.2 1.2 copy.54
  11.5 1.2 copy.55
  12.7 7.3 %shard_map.148 = (f32[64,32,128]{2,1,0:T(8,128)}, f32[16,32,128]{2,1,0:T(8,128)}) custom-call(f32[16,64]{1,0:T(8,128)} %b_ref.1, f32[16,64]{1,0:T(8,128)} %c_ref.3, f32[64,32,128]{2,1,0:T(8,128)} %bitcast.67, f32[64,32,128]{2,1,0:T(8,128)} %bitcast.68, f32[16,32,128]{2,1,0:T(8,128)} %bitcast.69), custom_call_target="tpu_custom_call" | custom-call | tf_op jit(solution)/shard_map/pallas_call | solution.py:62
  20.1 1.7 all_gather_reshape.3
  21.8 3.2 %collective-permute-start = (bf16[64,2048]{1,0:T(8,128)(2,1)}, bf16[64,2048]{1,0:T(8,128)(2,1)}, u32[]{:S(2)}, u32[]{:S(2)}) collective-permute-start(bf16[64,2048]{1,0:T(8,128)(2,1)} %param.19), channel_id=1, source_target_pairs={{0,2},{1,3},{2,4},{3,5},{4,6},{5,7},{6,8},{7,9},{8,10},{9,11},{10,... | collective-permute-start | bytes 786440 | tf_op jit(solution)/shard_map/ppermute | solution.py:22
  25.0 4.0 %collective-permute-start.1 = (bf16[64,2048]{1,0:T(8,128)(2,1)}, bf16[64,2048]{1,0:T(8,128)(2,1)}, u32[]{:S(2)}, u32[]{:S(2)}) collective-permute-start(bf16[64,2048]{1,0:T(8,128)(2,1)} %param.19), channel_id=1, source_target_pairs={{0,1},{1,2},{2,3},{3,4},{4,5},{5,6},{6,7},{7,8},{8,9},{9,10},{10,1... | collective-permute-start | bytes 786440 | tf_op jit(solution)/shard_map/ppermute | solution.py:22
  29.0 1.9 reduce_window_sum.33
  30.8 1.0 slice_bitcast_fusion.2
  31.9 18.1 %all-gather = f32[16,1,4096]{2,1,0:T(1,128)S(1)} all-gather(f32[1,1,4096]{2,1,0:T(1,128)S(1)} %slice_bitcast_fusion.2), channel_id=1, replica_groups=mesh['grp'=2,'eg'=4,'kg'=4] {'eg','kg'}, dimensions={0}, use_global_device_ids=true | all-gather | bytes 278528 | tf_op jit(solution)/shard_map/all_gather | solution.py:88
  51.3 1.7 subtract_maximum_fusion
  53.7 2.2 %reshape.158 = bf16[64,8,4,128]{3,2,1,0:T(4,128)(2,1)} reshape(bf16[64,4096]{1,0:T(8,128)(2,1)} %param.18) | data formatting | bytes 1048576 | tf_op jit(solution)/shard_map/reshape | solution.py:126
  55.9 1.2 copy.53
  57.1 1.0 constant_dynamic-update-slice_fusion.2
  58.2 1.0 constant_dynamic-update-slice_fusion.1
  59.2 1.0 constant_dynamic-update-slice_fusion
  60.4 2.8 %fusion.48 = (f32[8,4,64]{2,1,0:T(4,128)}, f32[8,4,64,192]{3,2,1,0:T(8,128)}) fusion(pred[64,192]{1,0:T(8,128)(4,1)S(1)} %copy-done.11, bf16[64,8,4,128]{3,2,1,0:T(4,128)(2,1)S(1)} %copy-done.8, bf16[192,8,128,1]{2,1,0,3:T(8,128)(2,1)S(1)} %bitcast.77), kind=kOutput, calls=%fused_computation.65 | convolution fusion | flops 102236352 | bytes 2510848 | tf_op jit(solution)/shard_map/sub | solution.py:135
  63.2 2.1 %fusion.3 = bf16[64,8,4,128]{3,0,2,1:T(8,128)(2,1)S(1)} fusion(f32[8,4,64,192]{3,2,1,0:T(8,128)} %get-tuple-element.14, f32[8,4,64]{2,1,0:T(4,128)} %get-tuple-element.13, bf16[192,8,128,1]{2,1,0,3:T(8,128)(2,1)S(1)} %bitcast.78), kind=kOutput, calls=%fused_computation.12 | convolution fusion | flops 101711872 | bytes 2498560 | tf_op jit(solution)/shard_map/kyje,eku->jkyu/dot_general | solution.py:137
  66.1 8.9 %all-gather.3.cloned.1.call-done = f32[16,16,4096]{2,1,0:T(8,128)} async-done(((f32[1,16,4096]{2,1,0:T(8,128)}), f32[16,16,4096]{2,1,0:T(8,128)}) %all-gather.3.cloned.1.call-update) | async-done | bytes 4194320 | tf_op jit(solution)/shard_map/all_gather | solution.py:87
  75.1 3.1 %select_reduce_fusion = f32[16,4096]{1,0:T(8,128)S(1)} fusion(f32[16,16,4096]{2,1,0:T(8,128)} %all-gather.3.cloned.1.call-done, f32[16,4096]{1,0:T(8,128)} %subtract_maximum_fusion, f32[16,4096]{1,0:T(8,128)S(1)} %copy-done.7, pred[16]{0:T(512)(128)(4,1)S(1)} %iota_compare_fusion.2), kind=kLoop, calls=%fused_computation.6 | loop fusion | flops 4128768 | bytes 4980752 | tf_op jit(solution)/shard_map/reduce_sum | solution.py:95
  78.9 5.9 %shard_map.149 = f32[64,32,128]{2,1,0:T(8,128)} custom-call(f32[16,64]{1,0:T(8,128)} %c_ref.3, f32[64,32,128]{2,1,0:T(8,128)} %bitcast.66, f32[64,32,128]{2,1,0:T(8,128)} %get-tuple-element.5.read_ref, f32[16,32,128]{2,1,0:T(8,128)} %bitcast.70, f32[16,32,128]{2,1,0:T(8,128)} %bitcast.74), custom_call_target="tpu_custom_call" | custom-call | tf_op jit(solution)/shard_map/pallas_call | solution.py:100
  84.7 1.4 convert_element_type.69
  86.7 15.1 %all_to_all.15 = bf16[4,16,4096]{2,1,0:T(8,128)(2,1)S(1)} all-to-all(bf16[4,16,4096]{2,1,0:T(8,128)(2,1)S(1)} %convolution_convert_fusion.1), channel_id=1, replica_groups=mesh['grp'=2,'eg'=4,'kg'=4] {'eg'}, dimensions={0} | all-to-all | bytes 1048576 | tf_op jit(solution)/shard_map/all_to_all | solution.py:197
  102.1 29.1 %all_to_all.16 = bf16[4,4,16,4096]{3,2,1,0:T(8,128)(2,1)S(1)} all-to-all(bf16[4,4,16,4096]{3,2,1,0:T(8,128)(2,1)S(1)} %broadcast_in_dim.80), channel_id=1, replica_groups=mesh['grp'=2,'eg'=4,'kg'=4] {'kg'}, dimensions={0} | all-to-all | bytes 4194304 | tf_op jit(solution)/shard_map/all_to_all | solution.py:199
  131.1 1.3 copy-done.1
  133.2 5.9 %convolution_convert_fusion = bf16[256,4096]{1,0:T(8,128)(2,1)} fusion(bf16[256,4096]{1,0:T(8,128)(2,1)S(1)} %copy-done, bf16[256,4096]{1,0:T(8,128)(2,1)} %bitcast.62, bf16[4096,256]{1,0:T(8,128)(2,1)} %param.24, f32[256,256]{1,0:T(8,128)S(1)} %fusion.53), kind=kOutput, calls=%fused_computation.1 | convolution fusion | flops 1075183616 | bytes 8650752 | tf_op jit(solution)/shard_map/dot_general | solution.py:147
  139.1 3.1 %copy.45 = bf16[4,4,16,4096]{3,2,0,1:T(8,128)(2,1)} copy(bf16[4,4,16,4096]{3,2,1,0:T(8,128)(2,1)} %bitcast.64) | data formatting | bytes 4194304 | tf_op jit(solution)/shard_map/reshape | solution.py:202
  142.2 7.6 %all-to-all-start.2 = ((bf16[16,16,4096]{2,1,0:T(8,128)(2,1)}), bf16[16,16,4096]{2,1,0:T(8,128)(2,1)}, u32[]{:S(2)}, u32[]{:S(2)}) async-start(bf16[16,16,4096]{2,1,0:T(8,128)(2,1)} %bitcast.63), calls=%async_computation.2 | async-start | bytes 4194304 | tf_op jit(solution)/shard_map/all_to_all | solution.py:203
  149.8 47.5 %all-to-all-done.2 = bf16[16,16,4096]{2,1,0:T(8,128)(2,1)} async-done(((bf16[16,16,4096]{2,1,0:T(8,128)(2,1)}), bf16[16,16,4096]{2,1,0:T(8,128)(2,1)}, u32[]{:S(2)}, u32[]{:S(2)}) %all-to-all-start.2) | async-done | bytes 2097184 | tf_op jit(solution)/shard_map/all_to_all | solution.py:203
  197.3 2.1 convert_reduce_fusion
  199.4 1.8 fusion.1
  (56 shorter events, 5.6 us)
Async XLA Ops:
  7.2 126.0 %copy-start = (bf16[256,4096]{1,0:T(8,128)(2,1)S(1)}, bf16[256,4096]{1,0:T(8,128)(2,1)}, u32[]{:S(2)}) copy-start(bf16[256,4096]{1,0:T(8,128)(2,1)} %param.25) | copy-start | bytes 6291460
  7.2 67.9 %all-gather.3.cloned.1.call-start = ((), (), s32[]{:S(2)}) async-start(), calls=%async_computation.3 | async-start | bytes 4456448 | tf_op jit(solution)/shard_map/all_gather | solution.py:87
  7.2 4.2 %copy-start.2 = (bf16[64,4096]{1,0:T(8,128)(2,1)S(1)}, bf16[64,4096]{1,0:T(8,128)(2,1)}, u32[]{:S(2)}) copy-start(bf16[64,4096]{1,0:T(8,128)(2,1)} %param.14) | copy-start | bytes 1572868
  7.2 4.2 %copy-start.9 = (bf16[64,4096]{1,0:T(8,128)(2,1)S(1)}, bf16[64,4096]{1,0:T(8,128)(2,1)}, u32[]{:S(2)}) copy-start(bf16[64,4096]{1,0:T(8,128)(2,1)} %param.13) | copy-start | bytes 1572868
  20.1 31.0 %copy-start.12 = (s32[64,2]{0,1:T(2,128)S(1)}, s32[64,2]{0,1:T(2,128)}, u32[]{:S(2)}) copy-start(s32[64,2]{0,1:T(2,128)} %param.21) | copy-start | bytes 1540
  21.8 35.3 %collective-permute-start = (bf16[64,2048]{1,0:T(8,128)(2,1)}, bf16[64,2048]{1,0:T(8,128)(2,1)}, u32[]{:S(2)}, u32[]{:S(2)}) collective-permute-start(bf16[64,2048]{1,0:T(8,128)(2,1)} %param.19), channel_id=1, source_target_pairs={{0,2},{1,3},{2,4},{3,5},{4,6},{5,7},{6,8},{7,9},{8,10},{9,11},{10,... | collective-permute-start | bytes 786440 | tf_op jit(solution)/shard_map/ppermute | solution.py:22
  25.0 33.1 %collective-permute-start.1 = (bf16[64,2048]{1,0:T(8,128)(2,1)}, bf16[64,2048]{1,0:T(8,128)(2,1)}, u32[]{:S(2)}, u32[]{:S(2)}) collective-permute-start(bf16[64,2048]{1,0:T(8,128)(2,1)} %param.19), channel_id=1, source_target_pairs={{0,1},{1,2},{2,3},{3,4},{4,5},{5,6},{6,7},{7,8},{8,9},{9,10},{10,1... | collective-permute-start | bytes 786440 | tf_op jit(solution)/shard_map/ppermute | solution.py:22
  30.8 25.0 %copy-start.3 = (f32[64,4096]{1,0:T(8,128)S(1)}, f32[64,4096]{1,0:T(8,128)}, u32[]{:S(2)}) copy-start(f32[64,4096]{1,0:T(8,128)} %reduce_window_sum.33) | copy-start | bytes 3145732
  58.1 2.2 %copy-start.8 = (bf16[64,8,4,128]{3,2,1,0:T(4,128)(2,1)S(1)}, bf16[64,8,4,128]{3,2,1,0:T(4,128)(2,1)}, u32[]{:S(2)}) copy-start(bf16[64,8,4,128]{3,2,1,0:T(4,128)(2,1)} %reshape.158) | copy-start | bytes 1572868
  58.1 2.2 %copy-start.11 = (pred[64,192]{1,0:T(8,128)(4,1)S(1)}, pred[64,192]{1,0:T(8,128)(4,1)}, u32[]{:S(2)}) copy-start(pred[64,192]{1,0:T(8,128)(4,1)} %compare_and_fusion) | copy-start | bytes 36868
  65.3 9.7 %copy-start.7 = (f32[16,4096]{1,0:T(8,128)S(1)}, f32[16,4096]{1,0:T(8,128)}, u32[]{:S(2)}) copy-start(f32[16,4096]{1,0:T(8,128)} %param.15) | copy-start | bytes 786436
  66.1 20.2 %copy-start.5 = (bf16[64,4096]{1,0:T(8,128)(2,1)}, bf16[64,4096]{1,0:T(8,128)(2,1)S(1)}, u32[]{:S(2)}) copy-start(bf16[64,4096]{1,0:T(8,128)(2,1)S(1)} %convert_element_type.74) | copy-start | bytes 1572868
  84.7 1.6 copy-start.10
  86.3 15.7 %copy-start.6 = (bf16[8,8,32,128]{3,1,2,0:T(8,128)(2,1)}, bf16[8,8,32,128]{3,1,2,0:T(8,128)(2,1)S(1)}, u32[]{:S(2)}) copy-start(bf16[8,8,32,128]{3,1,2,0:T(8,128)(2,1)S(1)} %copy.86) | copy-start | bytes 1572868
  102.0 30.4 %copy-start.4 = (bf16[4096,256]{1,0:T(8,128)(2,1)S(1)}, bf16[4096,256]{1,0:T(8,128)(2,1)}, u32[]{:S(2)}) copy-start(bf16[4096,256]{1,0:T(8,128)(2,1)} %param.23) | copy-start | bytes 6291460
  131.1 1.3 copy-start.1
  142.2 7.6 %copy-start.13 = (f32[64,2]{0,1:T(2,128)S(1)}, f32[64,2]{0,1:T(2,128)}, u32[]{:S(2)}) copy-start(f32[64,2]{0,1:T(2,128)} %param.22) | copy-start | bytes 1540
  142.2 55.1 %all-to-all-start.2 = ((bf16[16,16,4096]{2,1,0:T(8,128)(2,1)}), bf16[16,16,4096]{2,1,0:T(8,128)(2,1)}, u32[]{:S(2)}, u32[]{:S(2)}) async-start(bf16[16,16,4096]{2,1,0:T(8,128)(2,1)} %bitcast.63), calls=%async_computation.2 | async-start | bytes 4194304 | tf_op jit(solution)/shard_map/all_to_all | solution.py:203
Sparse Core Ops, SparseCore 0:
  21.9 53.0 all-gather.2

commit v12 on v10

--- a/solution.py
+++ b/solution.py
@@ -163,8 +163,12 @@
         "tek,td->ekd", picker.astype(jnp.bfloat16), stream, preferred_element_type=jnp.float32
     ).astype(jnp.bfloat16)
     by_expert = lax.all_to_all(packed, "eg", split_axis=0, concat_axis=0, tiled=True)
-    outgoing = jnp.broadcast_to(by_expert[None], (group,) + by_expert.shape)
-    arrived = lax.all_to_all(outgoing, "kg", split_axis=0, concat_axis=0, tiled=True)
+    pieces = [by_expert]
+    for by in range(1, group):
+        pairs = [(i, (i + by) % group) for i in range(group)]
+        pieces.append(lax.ppermute(by_expert, "kg", pairs))
+    mine = lax.axis_index("kg")
+    arrived = jnp.take(jnp.stack(pieces), (mine - jnp.arange(group)) % group, axis=0)
     gathered = arrived.reshape(-1, width)
     partial_value = expert_partial(gathered, w_gate, w_up, w_down)
     returned = lax.all_to_all(

time: 206 us -> 211 us (1.024)
  blocking collectives: 68.6 us -> 40.3 us
  waiting for transfers between devices: 60.6 us -> 84.4 us
  other arithmetic: 15.8 us -> 20.8 us
  local copies, waits for them, and re-layouts: 13 us -> 16.5 us
    all_to_all x1 -> x0, blocking collectives: 28.3 us -> none  [body(): lax.all_to_all(outgoing, 'kg', split_axis=0, concat_axis=0, tiled=True)]
    ppermute x0 -> x3, waiting for transfers between devices: none -> 23.9 us  [body(): pieces.append(lax.ppermute(by_expert, 'kg', pairs))]
    gather x0 -> x1, local copies, waits for them, and re-layouts: none -> 3.56 us  [body(): jnp.take(jnp.stack(pieces), (mine - jnp.arange(group)) % group, axis=0)]
    another operation x0 -> x1, other arithmetic: none -> 2.97 us  [body(): jnp.stack(pieces)]
  transfers between devices with their start and end apart: 4 -> 7, of which waited for: 2 -> 5; matrix products, arithmetic and copies ran while one was open for 7% -> 7% of each run, Pallas kernels for 0% -> 0%
where the time goes in v12:
time: 211 us; the launch traced here: 210 us
  waiting for transfers between devices  84.4 us (40%)
  blocking collectives  40.3 us (19%)
  other arithmetic  20.8 us (10%)
  local copies, waits for them, and re-layouts  16.5 us (8%)
  between operations  14.3 us (7%)
  matrix products  13.3 us (6%)
  starting transfers between devices  13.2 us (6%)
  Pallas kernels  7.33 us (3%)
    all_to_all x1, waiting for transfers between devices, body(): lax.all_to_all(partial_value.reshape((seq_count,) + arrived.shape[2:]), (...  49.4 us
    ppermute x3, waiting for transfers between devices, body(): pieces.append(lax.ppermute(by_expert, 'kg', pairs))  23.9 us
    all_gather x1, blocking collectives, ssm_correct(): sums = lax.all_gather(running[-1], SEQ)  22.5 us
    all_to_all x1, blocking collectives, body(): lax.all_to_all(packed, 'eg', split_axis=0, concat_axis=0, tiled=True)  17.8 us
    all_gather x1, waiting for transfers between devices, ssm_correct(): ends = lax.all_gather(local_end, SEQ)  11.1 us
    unnamed x39, local copies, waits for them, and re-layouts  8.64 us
    ppermute x2, starting transfers between devices, shifted(): return lax.ppermute(value, axis, pairs)  7.83 us
    pallas_call x1, Pallas kernels, sweep(): pl.pallas_call(scan_kernel, grid=(rows // tile,), in_specs=[pl.BlockSpec(...  7.33 us
  transfers between devices with their start and end apart: 7, of which 5 were waited for; matrix products, arithmetic and copies ran while one was open for 7% of the time, Pallas kernels for 0%

profile of v12, /device:TPU:0, one launch (start us, length us, event | category | flops | bytes accessed | tf_op | source)
XLA Modules:
  0.0 210.2 jit_solution(12634529110836886082)
XLA Ops:
  7.2 1.3 convert_bitcast_fusion
  8.5 1.2 copy.54
  9.8 1.2 copy.55
  11.8 7.3 %shard_map.148 = (f32[64,32,128]{2,1,0:T(8,128)}, f32[16,32,128]{2,1,0:T(8,128)}) custom-call(f32[16,64]{1,0:T(8,128)} %b_ref.1, f32[16,64]{1,0:T(8,128)} %c_ref.1, f32[64,32,128]{2,1,0:T(8,128)} %bitcast.63, f32[64,32,128]{2,1,0:T(8,128)} %bitcast.64, f32[16,32,128]{2,1,0:T(8,128)} %bitcast.67), custom_call_target="tpu_custom_call" | custom-call | tf_op jit(solution)/shard_map/pallas_call | solution.py:51
  19.1 1.7 all_gather_reshape.3
  20.9 5.7 %collective-permute-start = (bf16[64,2048]{1,0:T(8,128)(2,1)}, bf16[64,2048]{1,0:T(8,128)(2,1)}, u32[]{:S(2)}, u32[]{:S(2)}) collective-permute-start(bf16[64,2048]{1,0:T(8,128)(2,1)} %param.19), channel_id=1, source_target_pairs={{0,2},{1,3},{2,4},{3,5},{4,6},{5,7},{6,8},{7,9},{8,10},{9,11},{10,... | collective-permute-start | bytes 786440 | tf_op jit(solution)/shard_map/ppermute | solution.py:22
  26.5 2.2 %collective-permute-start.1 = (bf16[64,2048]{1,0:T(8,128)(2,1)}, bf16[64,2048]{1,0:T(8,128)(2,1)}, u32[]{:S(2)}, u32[]{:S(2)}) collective-permute-start(bf16[64,2048]{1,0:T(8,128)(2,1)} %param.19), channel_id=1, source_target_pairs={{0,1},{1,2},{2,3},{3,4},{4,5},{5,6},{6,7},{7,8},{8,9},{9,10},{10,1... | collective-permute-start | bytes 786440 | tf_op jit(solution)/shard_map/ppermute | solution.py:22
  28.7 1.9 reduce_window_sum.33
  30.6 0.9 slice_bitcast_fusion.2
  31.5 22.5 %all-gather = f32[16,1,4096]{2,1,0:T(1,128)S(1)} all-gather(f32[1,1,4096]{2,1,0:T(1,128)S(1)} %slice_bitcast_fusion.2), channel_id=1, replica_groups=mesh['grp'=2,'eg'=4,'kg'=4] {'eg','kg'}, dimensions={0}, use_global_device_ids=true | all-gather | bytes 278528 | tf_op jit(solution)/shard_map/all_gather | solution.py:77
  56.0 1.0 constant_dynamic-update-slice_fusion.2
  57.0 1.0 constant_dynamic-update-slice_fusion.1
  58.0 1.0 constant_dynamic-update-slice_fusion
  59.1 0.8 copy.58
  59.9 2.2 %fusion.52 = (f32[8,4,64]{2,1,0:T(4,128)S(1)}, f32[8,4,64,192]{3,2,1,0:T(8,128)}) fusion(pred[64,192]{1,0:T(8,128)(4,1)S(1)} %compare_and_fusion, bf16[64,8,4,128]{3,2,1,0:T(4,128)(2,1)S(1)} %reshape.204, bf16[192,8,128,1]{2,1,0,3:T(8,128)(2,1)S(1)} %bitcast.69), kind=kOutput, calls=%fused_computation.83 | convolution fusion | flops 102236352 | bytes 2510848 | tf_op jit(solution)/shard_map/sub | solution.py:103
  62.2 2.2 %fusion.3 = bf16[64,8,4,128]{3,0,2,1:T(8,128)(2,1)S(1)} fusion(f32[8,4,64,192]{3,2,1,0:T(8,128)} %get-tuple-element.14, f32[8,4,64]{2,1,0:T(4,128)S(1)} %get-tuple-element.13, bf16[192,8,128,1]{2,1,0,3:T(8,128)(2,1)} %bitcast.70), kind=kOutput, calls=%fused_computation.16 | convolution fusion | flops 101711872 | bytes 2498560 | tf_op jit(solution)/shard_map/kyje,eku->jkyu/dot_general | solution.py:105
  65.2 11.1 %all-gather.3.cloned.1.call-done = f32[16,16,4096]{2,1,0:T(8,128)} async-done(((f32[1,16,4096]{2,1,0:T(8,128)}), f32[16,16,4096]{2,1,0:T(8,128)}) %all-gather.3.cloned.1.call-update) | async-done | bytes 4194320 | tf_op jit(solution)/shard_map/all_gather | solution.py:76
  76.3 3.1 %select_reduce_fusion = f32[16,4096]{1,0:T(8,128)S(1)} fusion(f32[16,16,4096]{2,1,0:T(8,128)} %all-gather.3.cloned.1.call-done, f32[16,4096]{1,0:T(8,128)} %subtract_maximum_fusion, f32[16,4096]{1,0:T(8,128)S(1)} %copy-done.7, pred[16]{0:T(512)(128)(4,1)S(1)} %iota_compare_fusion.2), kind=kLoop, calls=%fused_computation.8 | loop fusion | flops 4128768 | bytes 4980752 | tf_op jit(solution)/shard_map/reduce_sum | solution.py:84
  79.5 5.3 %multiply_reduce_fusion = f32[64,4096]{1,0:T(8,128)S(1)} fusion(f32[16,4096]{1,0:T(8,128)S(1)} %select_reduce_fusion, f32[64,4096]{1,0:T(8,128)S(1)} %copy-done.6, f32[16,4096]{1,0:T(8,128)S(1)} %copy-done.7, f32[64,16]{1,0:T(8,128)S(1)} %copy.40), kind=kLoop, calls=%fused_computation.2 | loop fusion | flops 16515072 | bytes 2625536 | tf_op jit(solution)/shard_map/reduce_sum | solution.py:86
  86.3 17.8 %all_to_all.10 = bf16[4,16,4096]{2,1,0:T(8,128)(2,1)S(1)} all-to-all(bf16[4,16,4096]{2,1,0:T(8,128)(2,1)S(1)} %convolution_convert_fusion.1), channel_id=1, replica_groups=mesh['grp'=2,'eg'=4,'kg'=4] {'eg'}, dimensions={0} | all-to-all | bytes 1048576 | tf_op jit(solution)/shard_map/all_to_all | solution.py:165
  105.1 11.2 %collective-permute-done.4 = bf16[4,16,4096]{2,1,0:T(8,128)(2,1)} collective-permute-done((bf16[4,16,4096]{2,1,0:T(8,128)(2,1)S(1)}, bf16[4,16,4096]{2,1,0:T(8,128)(2,1)}, u32[]{:S(2)}, u32[]{:S(2)}) %collective-permute-start.4) | collective-permute-done | bytes 524320 | tf_op jit(solution)/shard_map/ppermute | solution.py:169
  116.3 11.9 %collective-permute-done.3 = bf16[4,16,4096]{2,1,0:T(8,128)(2,1)} collective-permute-done((bf16[4,16,4096]{2,1,0:T(8,128)(2,1)S(1)}, bf16[4,16,4096]{2,1,0:T(8,128)(2,1)}, u32[]{:S(2)}, u32[]{:S(2)}) %collective-permute-start.3) | collective-permute-done | bytes 524320 | tf_op jit(solution)/shard_map/ppermute | solution.py:169
  128.2 0.8 collective-permute-done.2
  128.9 3.0 %pad_maximum_fusion = bf16[4,4,16,4096]{3,2,1,0:T(8,128)(2,1)} fusion(bf16[1,4,16,4096]{3,2,1,0:T(8,128)(2,1)} %bitcast.10, bf16[1,4,16,4096]{3,2,1,0:T(8,128)(2,1)} %bitcast.9, bf16[1,4,16,4096]{3,2,1,0:T(8,128)(2,1)} %bitcast.8, bf16[1,4,16,4096]{3,2,1,0:T(8,128)(2,1)S(1)} %bitcast.65), kind=kLoop, calls=%fused_computation.9 | loop fusion | flops 3145728 | bytes 4194304 | tf_op jit(solution)/shard_map/stack | solution.py:171
  131.9 3.6 %gather_fusion = bf16[4,4,16,4096]{3,2,1,0:T(8,128)(2,1)} fusion(bf16[4,4,16,4096]{3,2,1,0:T(8,128)(2,1)} %pad_maximum_fusion, s32[1024]{0:T(1024)S(1)} %pad_clamp_fusion), kind=kCustom, calls=%fused_computation | custom fusion | bytes 4194320 | tf_op jit(solution)/shard_map/jit(_take)/gather | solution.py:171
  135.5 2.0 bitcast_select_fusion
  137.5 1.3 copy-done.1
  139.5 5.9 %convolution_convert_fusion = bf16[256,4096]{1,0:T(8,128)(2,1)} fusion(bf16[256,4096]{1,0:T(8,128)(2,1)S(1)} %copy-done, bf16[256,4096]{1,0:T(8,128)(2,1)} %copy-done.1, bf16[4096,256]{1,0:T(8,128)(2,1)} %param.24, f32[256,256]{1,0:T(8,128)S(1)} %fusion.57), kind=kOutput, calls=%fused_computation.3 | convolution fusion | flops 1075183616 | bytes 8650752 | tf_op jit(solution)/shard_map/dot_general | solution.py:115
  145.4 4.6 %all-to-all-start.1 = ((bf16[16,16,4096]{2,1,0:T(8,128)(2,1)}), bf16[16,16,4096]{2,1,0:T(8,128)(2,1)}, u32[]{:S(2)}, u32[]{:S(2)}) async-start(bf16[16,16,4096]{2,1,0:T(8,128)(2,1)} %bitcast.62), calls=%async_computation.1 | async-start | bytes 4194304 | tf_op jit(solution)/shard_map/all_to_all | solution.py:174
  150.0 49.4 %all-to-all-done.1 = bf16[16,16,4096]{2,1,0:T(8,128)(2,1)} async-done(((bf16[16,16,4096]{2,1,0:T(8,128)(2,1)}), bf16[16,16,4096]{2,1,0:T(8,128)(2,1)}, u32[]{:S(2)}, u32[]{:S(2)}) %all-to-all-start.1) | async-done | bytes 2097184 | tf_op jit(solution)/shard_map/all_to_all | solution.py:174
  199.5 2.1 convert_reduce_fusion
  201.5 1.8 fusion.1
  (67 shorter events, 6.9 us)
Async XLA Ops:
  7.2 132.3 %copy-start = (bf16[256,4096]{1,0:T(8,128)(2,1)S(1)}, bf16[256,4096]{1,0:T(8,128)(2,1)}, u32[]{:S(2)}) copy-start(bf16[256,4096]{1,0:T(8,128)(2,1)} %param.25) | copy-start | bytes 6291460
  7.2 2.5 %copy-start.2 = (bf16[64,4096]{1,0:T(8,128)(2,1)S(1)}, bf16[64,4096]{1,0:T(8,128)(2,1)}, u32[]{:S(2)}) copy-start(bf16[64,4096]{1,0:T(8,128)(2,1)} %param.14) | copy-start | bytes 1572868
  7.2 2.5 %copy-start.10 = (bf16[64,4096]{1,0:T(8,128)(2,1)S(1)}, bf16[64,4096]{1,0:T(8,128)(2,1)}, u32[]{:S(2)}) copy-start(bf16[64,4096]{1,0:T(8,128)(2,1)} %param.13) | copy-start | bytes 1572868
  7.2 69.1 %all-gather.3.cloned.1.call-start = ((), (), s32[]{:S(2)}) async-start(), calls=%async_computation.2 | async-start | bytes 4456448 | tf_op jit(solution)/shard_map/all_gather | solution.py:76
  9.7 1.3 copy-start.7
  19.1 35.3 %copy-start.13 = (s32[64,2]{0,1:T(2,128)S(1)}, s32[64,2]{0,1:T(2,128)}, u32[]{:S(2)}) copy-start(s32[64,2]{0,1:T(2,128)} %param.21) | copy-start | bytes 1540
  20.8 34.6 %copy-start.12 = (f32[16,64]{1,0:T(8,128)S(1)}, f32[16,64]{1,0:T(8,128)}, u32[]{:S(2)}) copy-start(f32[16,64]{1,0:T(8,128)} %c_ref.1) | copy-start | bytes 12292
  20.8 34.7 %copy-start.9 = (bf16[64,4096]{1,0:T(8,128)(2,1)S(1)}, bf16[64,4096]{1,0:T(8,128)(2,1)}, u32[]{:S(2)}) copy-start(bf16[64,4096]{1,0:T(8,128)(2,1)} %param.18) | copy-start | bytes 1572868
  20.9 35.1 %collective-permute-start = (bf16[64,2048]{1,0:T(8,128)(2,1)}, bf16[64,2048]{1,0:T(8,128)(2,1)}, u32[]{:S(2)}, u32[]{:S(2)}) collective-permute-start(bf16[64,2048]{1,0:T(8,128)(2,1)} %param.19), channel_id=1, source_target_pairs={{0,2},{1,3},{2,4},{3,5},{4,6},{5,7},{6,8},{7,9},{8,10},{9,11},{10,... | collective-permute-start | bytes 786440 | tf_op jit(solution)/shard_map/ppermute | solution.py:22
  26.5 30.5 %collective-permute-start.1 = (bf16[64,2048]{1,0:T(8,128)(2,1)}, bf16[64,2048]{1,0:T(8,128)(2,1)}, u32[]{:S(2)}, u32[]{:S(2)}) collective-permute-start(bf16[64,2048]{1,0:T(8,128)(2,1)} %param.19), channel_id=1, source_target_pairs={{0,1},{1,2},{2,3},{3,4},{4,5},{5,6},{6,7},{7,8},{8,9},{9,10},{10,1... | collective-permute-start | bytes 786440 | tf_op jit(solution)/shard_map/ppermute | solution.py:22
  65.2 20.4 %copy-start.5 = (bf16[64,4096]{1,0:T(8,128)(2,1)}, bf16[64,4096]{1,0:T(8,128)(2,1)S(1)}, u32[]{:S(2)}) copy-start(bf16[64,4096]{1,0:T(8,128)(2,1)S(1)} %convert_element_type.70) | copy-start | bytes 1572868
  76.3 3.1 %copy-start.6 = (f32[64,4096]{1,0:T(8,128)S(1)}, f32[64,4096]{1,0:T(8,128)}, u32[]{:S(2)}) copy-start(f32[64,4096]{1,0:T(8,128)} %reduce_window_sum.33) | copy-start | bytes 3145732
  79.5 5.4 %copy-start.8 = (f32[64,32,128]{2,1,0:T(8,128)S(1)}, f32[64,32,128]{2,1,0:T(8,128)}, u32[]{:S(2)}) copy-start(f32[64,32,128]{2,1,0:T(8,128)} %get-tuple-element.5) | copy-start | bytes 3145732
  84.9 1.0 copy-start.11
  85.6 46.3 %copy-start.4 = (bf16[64,4096]{1,0:T(8,128)(2,1)}, bf16[64,4096]{1,0:T(8,128)(2,1)S(1)}, u32[]{:S(2)}) copy-start(bf16[64,4096]{1,0:T(8,128)(2,1)S(1)} %fusion.5) | copy-start | bytes 1572868
  104.1 12.2 %collective-permute-start.4 = (bf16[4,16,4096]{2,1,0:T(8,128)(2,1)S(1)}, bf16[4,16,4096]{2,1,0:T(8,128)(2,1)}, u32[]{:S(2)}, u32[]{:S(2)}) collective-permute-start(bf16[4,16,4096]{2,1,0:T(8,128)(2,1)S(1)} %all_to_all.10), channel_id=1, source_target_pairs={{0,3},{1,0},{2,1},{3,2},{4,7},{5,4},{6,5},{7,6},{8,11},{9,8},{10,9... | collective-permute-start | bytes 1572872 | tf_op jit(solution)/shard_map/ppermute | solution.py:169
  104.1 24.1 %collective-permute-start.3 = (bf16[4,16,4096]{2,1,0:T(8,128)(2,1)S(1)}, bf16[4,16,4096]{2,1,0:T(8,128)(2,1)}, u32[]{:S(2)}, u32[]{:S(2)}) collective-permute-start(bf16[4,16,4096]{2,1,0:T(8,128)(2,1)S(1)} %all_to_all.10), channel_id=1, source_target_pairs={{0,2},{1,3},{2,0},{3,1},{4,6},{5,7},{6,4},{7,5},{8,10},{9,11},{10,... | collective-permute-start | bytes 1572872 | tf_op jit(solution)/shard_map/ppermute | solution.py:169
  104.8 24.1 %collective-permute-start.2 = (bf16[4,16,4096]{2,1,0:T(8,128)(2,1)S(1)}, bf16[4,16,4096]{2,1,0:T(8,128)(2,1)}, u32[]{:S(2)}, u32[]{:S(2)}) collective-permute-start(bf16[4,16,4096]{2,1,0:T(8,128)(2,1)S(1)} %all_to_all.10), channel_id=1, source_target_pairs={{0,1},{1,2},{2,3},{3,0},{4,5},{5,6},{6,7},{7,4},{8,9},{9,10},{10,1... | collective-permute-start | bytes 1572872 | tf_op jit(solution)/shard_map/ppermute | solution.py:169
  135.5 3.3 %copy-start.3 = (bf16[4096,256]{1,0:T(8,128)(2,1)S(1)}, bf16[4096,256]{1,0:T(8,128)(2,1)}, u32[]{:S(2)}) copy-start(bf16[4096,256]{1,0:T(8,128)(2,1)} %param.23) | copy-start | bytes 6291460
  137.5 1.3 copy-start.1
  145.4 4.6 %copy-start.14 = (f32[64,2]{0,1:T(2,128)S(1)}, f32[64,2]{0,1:T(2,128)}, u32[]{:S(2)}) copy-start(f32[64,2]{0,1:T(2,128)} %param.22) | copy-start | bytes 1540
  145.4 54.0 %all-to-all-start.1 = ((bf16[16,16,4096]{2,1,0:T(8,128)(2,1)}), bf16[16,16,4096]{2,1,0:T(8,128)(2,1)}, u32[]{:S(2)}, u32[]{:S(2)}) async-start(bf16[16,16,4096]{2,1,0:T(8,128)(2,1)} %bitcast.62), calls=%async_computation.1 | async-start | bytes 4194304 | tf_op jit(solution)/shard_map/all_to_all | solution.py:174
Sparse Core Ops, SparseCore 0:
  21.0 55.3 all-gather.2

commit v13 on v9

--- a/solution.py
+++ b/solution.py
@@ -163,13 +163,12 @@
         "tek,td->ekd", picker.astype(jnp.bfloat16), stream, preferred_element_type=jnp.float32
     ).astype(jnp.bfloat16)
     by_expert = lax.all_to_all(packed, "eg", split_axis=0, concat_axis=0, tiled=True)
-    outgoing = jnp.broadcast_to(by_expert[None], (group,) + by_expert.shape)
-    arrived = lax.all_to_all(outgoing, "kg", split_axis=0, concat_axis=0, tiled=True)
+    outgoing = jnp.broadcast_to(by_expert[:, None], (EXP_WIN, group) + by_expert.shape[1:])
+    arrived = lax.all_to_all(outgoing, "kg", split_axis=1, concat_axis=1, tiled=True)
     gathered = arrived.reshape(-1, width)
     partial_value = expert_partial(gathered, w_gate, w_up, w_down)
-    by_source = jnp.swapaxes(partial_value.reshape(arrived.shape), 0, 1)
     returned = lax.all_to_all(
-        by_source.reshape((seq_count,) + arrived.shape[2:]), SEQ, split_axis=0, concat_axis=0, tiled=True
+        partial_value.reshape((seq_count,) + arrived.shape[2:]), SEQ, split_axis=0, concat_axis=0, tiled=True
     )
     summed = jnp.sum(returned.reshape(EXP_WIN, group, SLOTS, width), axis=1, dtype=jnp.float32)
     weighting = (picker.astype(jnp.float32) * route_share[:, :, None]).reshape(

time: 206 us -> 204 us (level)
    reshape x1 -> x0, local copies, waits for them, and re-layouts: 3.1 us -> none  [body(): by_source = jnp.swapaxes(partial_value.reshape(arrived.shape), 0, 1)]
where the time goes in v13:
time: 204 us; the launch traced here: 203 us
  blocking collectives  62.4 us (31%)
  waiting for transfers between devices  61.2 us (30%)
  other arithmetic  15.8 us (8%)
  starting transfers between devices  14.9 us (7%)
  between operations  14.3 us (7%)
  local copies, waits for them, and re-layouts  14.1 us (7%)
  matrix products  13.3 us (7%)
  Pallas kernels  7.33 us (4%)
    all_to_all x1, waiting for transfers between devices, body(): lax.all_to_all(partial_value.reshape((seq_count,) + arrived.shape[2:]), S...  47.5 us
    all_to_all x1, blocking collectives, body(): lax.all_to_all(outgoing, 'kg', split_axis=1, concat_axis=1, tiled=True)  29 us
    all_gather x1, blocking collectives, ssm_correct(): sums = lax.all_gather(running[-1], SEQ)  18.4 us
    all_to_all x1, blocking collectives, body(): lax.all_to_all(packed, 'eg', split_axis=0, concat_axis=0, tiled=True)  15.1 us
    all_gather x1, waiting for transfers between devices, ssm_correct(): ends = lax.all_gather(local_end, SEQ)  13.7 us
    unnamed x39, local copies, waits for them, and re-layouts  9.5 us
    all_to_all x1, starting transfers between devices, body(): lax.all_to_all(partial_value.reshape((seq_count,) + arrived.shape[2:]), S...  7.59 us
    pallas_call x1, Pallas kernels, sweep(): pl.pallas_call(scan_kernel, grid=(rows // tile,), in_specs=[pl.BlockSpec(...  7.33 us
  transfers between devices with their start and end apart: 4, of which 2 were waited for; matrix products, arithmetic and copies ran while one was open for 7% of the time, Pallas kernels for 0%

profile of v13, /device:TPU:11, one launch (start us, length us, event | category | flops | bytes accessed | tf_op | source)
XLA Modules:
  0.0 203.4 jit_solution(8581412777317441559)
XLA Ops:
  7.2 1.3 convert_bitcast_fusion
  8.5 1.2 copy.65
  9.8 1.2 copy.66
  11.0 0.8 copy.67
  11.8 7.3 %shard_map.148 = (f32[64,32,128]{2,1,0:T(8,128)}, f32[16,32,128]{2,1,0:T(8,128)}) custom-call(f32[16,64]{1,0:T(8,128)} %b_ref.1, f32[16,64]{1,0:T(8,128)} %c_ref.1, f32[64,32,128]{2,1,0:T(8,128)} %bitcast.59, f32[64,32,128]{2,1,0:T(8,128)} %bitcast.60, f32[16,32,128]{2,1,0:T(8,128)} %bitcast.62), custom_call_target="tpu_custom_call" | custom-call | tf_op jit(solution)/shard_map/pallas_call | solution.py:51
  19.1 1.7 all_gather_reshape.3
  20.9 3.3 %collective-permute-start = (bf16[64,2048]{1,0:T(8,128)(2,1)}, bf16[64,2048]{1,0:T(8,128)(2,1)}, u32[]{:S(2)}, u32[]{:S(2)}) collective-permute-start(bf16[64,2048]{1,0:T(8,128)(2,1)} %param.19), channel_id=1, source_target_pairs={{0,2},{1,3},{2,4},{3,5},{4,6},{5,7},{6,8},{7,9},{8,10},{9,11},{10,... | collective-permute-start | bytes 786440 | tf_op jit(solution)/shard_map/ppermute | solution.py:22
  24.2 4.0 %collective-permute-start.1 = (bf16[64,2048]{1,0:T(8,128)(2,1)}, bf16[64,2048]{1,0:T(8,128)(2,1)}, u32[]{:S(2)}, u32[]{:S(2)}) collective-permute-start(bf16[64,2048]{1,0:T(8,128)(2,1)} %param.19), channel_id=1, source_target_pairs={{0,1},{1,2},{2,3},{3,4},{4,5},{5,6},{6,7},{7,8},{8,9},{9,10},{10,1... | collective-permute-start | bytes 786440 | tf_op jit(solution)/shard_map/ppermute | solution.py:22
  28.2 1.9 reduce_window_sum.33
  30.0 0.9 slice_bitcast_fusion.2
  30.9 18.4 %all-gather = f32[16,1,4096]{2,1,0:T(1,128)S(1)} all-gather(f32[1,1,4096]{2,1,0:T(1,128)S(1)} %slice_bitcast_fusion.2), channel_id=1, replica_groups=mesh['grp'=2,'eg'=4,'kg'=4] {'eg','kg'}, dimensions={0}, use_global_device_ids=true | all-gather | bytes 278528 | tf_op jit(solution)/shard_map/all_gather | solution.py:77
  50.0 0.7 subtract_maximum_fusion
  51.4 1.0 constant_dynamic-update-slice_fusion.2
  52.4 1.0 constant_dynamic-update-slice_fusion.1
  53.4 1.0 constant_dynamic-update-slice_fusion
  54.5 0.8 copy.69
  55.3 2.2 %fusion.49 = (f32[8,4,64]{2,1,0:T(4,128)S(1)}, f32[8,4,64,192]{3,2,1,0:T(8,128)}) fusion(pred[64,192]{1,0:T(8,128)(4,1)S(1)} %compare_and_fusion, bf16[64,8,4,128]{3,2,1,0:T(4,128)(2,1)S(1)} %reshape.151, bf16[192,8,128,1]{2,1,0,3:T(8,128)(2,1)S(1)} %bitcast.64), kind=kOutput, calls=%fused_computation.67 | convolution fusion | flops 102236352 | bytes 2510848 | tf_op jit(solution)/shard_map/sub | solution.py:103
  57.5 2.3 %fusion.3 = bf16[64,8,4,128]{3,0,2,1:T(8,128)(2,1)S(1)} fusion(f32[8,4,64,192]{3,2,1,0:T(8,128)} %get-tuple-element.14, f32[8,4,64]{2,1,0:T(4,128)S(1)} %get-tuple-element.13, bf16[192,8,128,1]{2,1,0,3:T(8,128)(2,1)} %bitcast.65), kind=kOutput, calls=%fused_computation.13 | convolution fusion | flops 101711872 | bytes 2498560 | tf_op jit(solution)/shard_map/kyje,eku->jkyu/dot_general | solution.py:105
  60.6 13.7 %all-gather.3.cloned.1.call-done = f32[16,16,4096]{2,1,0:T(8,128)} async-done(((f32[1,16,4096]{2,1,0:T(8,128)}), f32[16,16,4096]{2,1,0:T(8,128)}) %all-gather.3.cloned.1.call-update) | async-done | bytes 4194320 | tf_op jit(solution)/shard_map/all_gather | solution.py:76
  74.3 3.1 %select_reduce_fusion = f32[16,4096]{1,0:T(8,128)S(1)} fusion(f32[16,16,4096]{2,1,0:T(8,128)} %all-gather.3.cloned.1.call-done, f32[16,4096]{1,0:T(8,128)} %subtract_maximum_fusion, f32[16,4096]{1,0:T(8,128)S(1)} %copy-done.7, pred[16]{0:T(512)(128)(4,1)S(1)} %iota_compare_fusion.2), kind=kLoop, calls=%fused_computation.7 | loop fusion | flops 4128768 | bytes 4980752 | tf_op jit(solution)/shard_map/reduce_sum | solution.py:84
  77.5 5.3 %multiply_reduce_fusion = f32[64,4096]{1,0:T(8,128)S(1)} fusion(f32[16,4096]{1,0:T(8,128)S(1)} %select_reduce_fusion, f32[64,4096]{1,0:T(8,128)S(1)} %copy-done.6, f32[16,4096]{1,0:T(8,128)S(1)} %copy-done.7, f32[64,16]{1,0:T(8,128)S(1)} %copy.50), kind=kLoop, calls=%fused_computation.1 | loop fusion | flops 16515072 | bytes 2625536 | tf_op jit(solution)/shard_map/reduce_sum | solution.py:86
  82.8 0.7 fusion.5
  84.2 15.1 %all_to_all.15 = bf16[4,16,4096]{2,1,0:T(8,128)(2,1)S(1)} all-to-all(bf16[4,16,4096]{2,1,0:T(8,128)(2,1)S(1)} %convolution_convert_fusion.1), channel_id=1, replica_groups=mesh['grp'=2,'eg'=4,'kg'=4] {'eg'}, dimensions={0} | all-to-all | bytes 1048576 | tf_op jit(solution)/shard_map/all_to_all | solution.py:165
  99.5 29.0 %all_to_all.16 = bf16[4,4,16,4096]{3,2,0,1:T(8,128)(2,1)S(1)} all-to-all(bf16[4,4,16,4096]{3,2,0,1:T(8,128)(2,1)S(1)} %broadcast_in_dim.84), channel_id=1, replica_groups=mesh['grp'=2,'eg'=4,'kg'=4] {'kg'}, dimensions={1} | all-to-all | bytes 4194304 | tf_op jit(solution)/shard_map/all_to_all | solution.py:167
  128.7 1.3 copy-done.1
  130.0 0.8 copy-done.3
  130.9 0.7 fusion.54
  131.6 5.9 %convolution_convert_fusion = bf16[256,4096]{1,0:T(8,128)(2,1)} fusion(bf16[256,4096]{1,0:T(8,128)(2,1)S(1)} %copy-done, bf16[256,4096]{1,0:T(8,128)(2,1)} %bitcast.57, bf16[4096,256]{1,0:T(8,128)(2,1)} %param.24, f32[256,256]{1,0:T(8,128)S(1)} %fusion.54), kind=kOutput, calls=%fused_computation.2 | convolution fusion | flops 1075183616 | bytes 8650752 | tf_op jit(solution)/shard_map/dot_general | solution.py:115
  137.5 7.6 %all-to-all-start.2 = ((bf16[16,16,4096]{2,1,0:T(8,128)(2,1)}), bf16[16,16,4096]{2,1,0:T(8,128)(2,1)}, u32[]{:S(2)}, u32[]{:S(2)}) async-start(bf16[16,16,4096]{2,1,0:T(8,128)(2,1)} %bitcast.58), calls=%async_computation.2 | async-start | bytes 4194304 | tf_op jit(solution)/shard_map/all_to_all | solution.py:170
  145.1 47.5 %all-to-all-done.2 = bf16[16,16,4096]{2,1,0:T(8,128)(2,1)} async-done(((bf16[16,16,4096]{2,1,0:T(8,128)(2,1)}), bf16[16,16,4096]{2,1,0:T(8,128)(2,1)}, u32[]{:S(2)}, u32[]{:S(2)}) %all-to-all-start.2) | async-done | bytes 2097184 | tf_op jit(solution)/shard_map/all_to_all | solution.py:170
  192.7 2.1 %convert_reduce_fusion = f32[4,16,4096]{2,1,0:T(8,128)S(1)} fusion(bf16[16,16,4096]{2,1,0:T(8,128)(2,1)} %all-to-all-done.2), kind=kLoop, calls=%fused_computation.6 | loop fusion | flops 1835008 | bytes 3145728 | tf_op jit(solution)/shard_map/reduce_sum | solution.py:173
  194.7 1.8 fusion.1
  (56 shorter events, 3.5 us)
Async XLA Ops:
  7.2 124.4 %copy-start = (bf16[256,4096]{1,0:T(8,128)(2,1)S(1)}, bf16[256,4096]{1,0:T(8,128)(2,1)}, u32[]{:S(2)}) copy-start(bf16[256,4096]{1,0:T(8,128)(2,1)} %param.25) | copy-start | bytes 6291460
  7.2 2.5 %copy-start.2 = (bf16[64,4096]{1,0:T(8,128)(2,1)S(1)}, bf16[64,4096]{1,0:T(8,128)(2,1)}, u32[]{:S(2)}) copy-start(bf16[64,4096]{1,0:T(8,128)(2,1)} %param.14) | copy-start | bytes 1572868
  7.2 2.5 %copy-start.10 = (bf16[64,4096]{1,0:T(8,128)(2,1)S(1)}, bf16[64,4096]{1,0:T(8,128)(2,1)}, u32[]{:S(2)}) copy-start(bf16[64,4096]{1,0:T(8,128)(2,1)} %param.13) | copy-start | bytes 1572868
  7.2 67.1 %all-gather.3.cloned.1.call-start = ((), (), s32[]{:S(2)}) async-start(), calls=%async_computation.3 | async-start | bytes 4456448 | tf_op jit(solution)/shard_map/all_gather | solution.py:76
  9.7 1.3 copy-start.7
  19.1 30.6 %copy-start.13 = (s32[64,2]{0,1:T(2,128)S(1)}, s32[64,2]{0,1:T(2,128)}, u32[]{:S(2)}) copy-start(s32[64,2]{0,1:T(2,128)} %param.21) | copy-start | bytes 1540
  20.8 30.0 %copy-start.12 = (f32[16,64]{1,0:T(8,128)S(1)}, f32[16,64]{1,0:T(8,128)}, u32[]{:S(2)}) copy-start(f32[16,64]{1,0:T(8,128)} %c_ref.1) | copy-start | bytes 12292
  20.8 30.1 %copy-start.9 = (bf16[64,4096]{1,0:T(8,128)(2,1)S(1)}, bf16[64,4096]{1,0:T(8,128)(2,1)}, u32[]{:S(2)}) copy-start(bf16[64,4096]{1,0:T(8,128)(2,1)} %param.18) | copy-start | bytes 1572868
  20.9 30.5 %collective-permute-start = (bf16[64,2048]{1,0:T(8,128)(2,1)}, bf16[64,2048]{1,0:T(8,128)(2,1)}, u32[]{:S(2)}, u32[]{:S(2)}) collective-permute-start(bf16[64,2048]{1,0:T(8,128)(2,1)} %param.19), channel_id=1, source_target_pairs={{0,2},{1,3},{2,4},{3,5},{4,6},{5,7},{6,8},{7,9},{8,10},{9,11},{10,... | collective-permute-start | bytes 786440 | tf_op jit(solution)/shard_map/ppermute | solution.py:22
  24.2 28.2 %collective-permute-start.1 = (bf16[64,2048]{1,0:T(8,128)(2,1)}, bf16[64,2048]{1,0:T(8,128)(2,1)}, u32[]{:S(2)}, u32[]{:S(2)}) collective-permute-start(bf16[64,2048]{1,0:T(8,128)(2,1)} %param.19), channel_id=1, source_target_pairs={{0,1},{1,2},{2,3},{3,4},{4,5},{5,6},{6,7},{7,8},{8,9},{9,10},{10,1... | collective-permute-start | bytes 786440 | tf_op jit(solution)/shard_map/ppermute | solution.py:22
  60.6 22.9 %copy-start.5 = (bf16[64,4096]{1,0:T(8,128)(2,1)}, bf16[64,4096]{1,0:T(8,128)(2,1)S(1)}, u32[]{:S(2)}) copy-start(bf16[64,4096]{1,0:T(8,128)(2,1)S(1)} %convert_element_type.70) | copy-start | bytes 1572868
  74.3 3.1 %copy-start.6 = (f32[64,4096]{1,0:T(8,128)S(1)}, f32[64,4096]{1,0:T(8,128)}, u32[]{:S(2)}) copy-start(f32[64,4096]{1,0:T(8,128)} %reduce_window_sum.33) | copy-start | bytes 3145732
  77.5 5.4 %copy-start.8 = (f32[64,32,128]{2,1,0:T(8,128)S(1)}, f32[64,32,128]{2,1,0:T(8,128)}, u32[]{:S(2)}) copy-start(f32[64,32,128]{2,1,0:T(8,128)} %get-tuple-element.5) | copy-start | bytes 3145732
  82.8 1.0 copy-start.11
  83.5 16.0 %copy-start.4 = (bf16[64,4096]{1,0:T(8,128)(2,1)}, bf16[64,4096]{1,0:T(8,128)(2,1)S(1)}, u32[]{:S(2)}) copy-start(bf16[64,4096]{1,0:T(8,128)(2,1)S(1)} %fusion.5) | copy-start | bytes 1572868
  128.5 2.3 %copy-start.3 = (bf16[4096,256]{1,0:T(8,128)(2,1)S(1)}, bf16[4096,256]{1,0:T(8,128)(2,1)}, u32[]{:S(2)}) copy-start(bf16[4096,256]{1,0:T(8,128)(2,1)} %param.23) | copy-start | bytes 6291460
  128.7 1.3 copy-start.1
  137.5 7.6 %copy-start.14 = (f32[64,2]{0,1:T(2,128)S(1)}, f32[64,2]{0,1:T(2,128)}, u32[]{:S(2)}) copy-start(f32[64,2]{0,1:T(2,128)} %param.22) | copy-start | bytes 1540
  137.5 55.1 %all-to-all-start.2 = ((bf16[16,16,4096]{2,1,0:T(8,128)(2,1)}), bf16[16,16,4096]{2,1,0:T(8,128)(2,1)}, u32[]{:S(2)}, u32[]{:S(2)}) async-start(bf16[16,16,4096]{2,1,0:T(8,128)(2,1)} %bitcast.58), calls=%async_computation.2 | async-start | bytes 4194304 | tf_op jit(solution)/shard_map/all_to_all | solution.py:170
Sparse Core Ops, SparseCore 0:
  21.0 53.2 all-gather.2

commit v14 on v13

--- a/solution.py
+++ b/solution.py
@@ -80,10 +80,11 @@
     masked = jnp.where((order < mine)[:, None], sums, 0.0)
     after = jnp.sum(masked, axis=0)[None, :] - jnp.cumsum(masked, axis=0)
     after = jnp.maximum(after, 0.0)
-    carry = jnp.exp(rates[None] * after[:, None, :]) * ends
-    incoming = jnp.sum(jnp.where((order < mine)[:, None, None], carry, 0.0), axis=0)
-    growth = jnp.exp(rates[None] * running[:, None, :]) * incoming[None]
-    fix = jnp.sum(read_rows.T[:, :, None] * growth, axis=1)
+    through = jnp.where((order < mine)[:, None, None], jnp.exp(rates[None] * after[:, None, :]), 0.0)
+    growth = read_rows.T[:, :, None] * jnp.exp(rates[None] * running[:, None, :])
+    through, growth = lax.optimization_barrier((through, growth))
+    incoming = jnp.sum(through * ends, axis=0)
+    fix = jnp.sum(growth * incoming[None], axis=1)
     return (local_read + fix).astype(jnp.bfloat16)
 
 

time: 204 us -> 210 us (1.029)
  other arithmetic: 15.8 us -> 33.4 us
  waiting for transfers between devices: 61.2 us -> 52.1 us
    all_gather x1, waiting for transfers between devices: 13.7 us -> 4.58 us  [ssm_correct(): ends = lax.all_gather(local_end, SEQ)]
    mul x0 -> x1, other arithmetic: none -> 8.88 us  [ssm_correct(): read_rows.T[:, :, None] * jnp.exp(rates[None] * running[:, None, :])]
    reduce_sum x2, other arithmetic: 8.49 us -> 13.1 us  [the longest x1 9.26 us: ssm_correct(): fix = jnp.sum(growth * incoming[None], axis=1)]
    select_n x0 -> x1, other arithmetic: none -> 2.55 us  [ssm_correct(): jnp.where((order < mine)[:, None, None], jnp.exp(rates[None] * after[:, N...]
    unnamed x39 -> x41, local copies, waits for them, and re-layouts: 9.5 us -> 8.82 us
  transfers between devices with their start and end apart: 4 -> 4, of which waited for: 2 -> 2; matrix products, arithmetic and copies ran while one was open for 7% -> 12% of each run, Pallas kernels for 0% -> 0%
where the time goes in v14:
time: 210 us; the launch traced here: 209 us
  blocking collectives  61 us (29%)
  waiting for transfers between devices  52.1 us (25%)
  other arithmetic  33.4 us (16%)
  starting transfers between devices  14.7 us (7%)
  between operations  14.4 us (7%)
  local copies, waits for them, and re-layouts  13.2 us (6%)
  matrix products  13.2 us (6%)
  Pallas kernels  7.31 us (3%)
    all_to_all x1, waiting for transfers between devices, body(): lax.all_to_all(partial_value.reshape((seq_count,) + arrived.shape[2:]), S...  47.5 us
    all_to_all x1, blocking collectives, body(): lax.all_to_all(outgoing, 'kg', split_axis=1, concat_axis=1, tiled=True)  29.1 us
    all_gather x1, blocking collectives, ssm_correct(): sums = lax.all_gather(running[-1], SEQ)  16.9 us
    all_to_all x1, blocking collectives, body(): lax.all_to_all(packed, 'eg', split_axis=0, concat_axis=0, tiled=True)  15 us
    reduce_sum x1, other arithmetic, ssm_correct(): fix = jnp.sum(growth * incoming[None], axis=1)  9.26 us
    mul x1, other arithmetic, ssm_correct(): read_rows.T[:, :, None] * jnp.exp(rates[None] * running[:, None, :])  8.88 us
    unnamed x41, local copies, waits for them, and re-layouts  8.82 us
    all_to_all x1, starting transfers between devices, body(): lax.all_to_all(partial_value.reshape((seq_count,) + arrived.shape[2:]), S...  7.5 us
  transfers between devices with their start and end apart: 4, of which 2 were waited for; matrix products, arithmetic and copies ran while one was open for 12% of the time, Pallas kernels for 0%

profile of v14, /device:TPU:11, one launch (start us, length us, event | category | flops | bytes accessed | tf_op | source)
XLA Modules:
  0.0 209.3 jit_solution(7276754330131768698)
XLA Ops:
  7.2 1.3 convert_bitcast_fusion
  8.5 1.2 copy.65
  9.8 1.2 copy.66
  11.0 0.8 copy.67
  11.8 7.3 %shard_map.148 = (f32[64,32,128]{2,1,0:T(8,128)}, f32[16,32,128]{2,1,0:T(8,128)}) custom-call(f32[16,64]{1,0:T(8,128)} %b_ref.1, f32[16,64]{1,0:T(8,128)} %c_ref.1, f32[64,32,128]{2,1,0:T(8,128)} %bitcast.59, f32[64,32,128]{2,1,0:T(8,128)} %bitcast.60, f32[16,32,128]{2,1,0:T(8,128)} %bitcast.62), custom_call_target="tpu_custom_call" | custom-call | tf_op jit(solution)/shard_map/pallas_call | solution.py:51
  19.1 1.7 all_gather_reshape.3
  20.9 3.2 %collective-permute-start = (bf16[64,2048]{1,0:T(8,128)(2,1)S(1)}, bf16[64,2048]{1,0:T(8,128)(2,1)}, u32[]{:S(2)}, u32[]{:S(2)}) collective-permute-start(bf16[64,2048]{1,0:T(8,128)(2,1)S(1)} %copy-done.11), channel_id=1, source_target_pairs={{0,2},{1,3},{2,4},{3,5},{4,6},{5,7},{6,8},{7,9},{8,10},{9,11},{10,... | collective-permute-start | bytes 786440 | tf_op jit(solution)/shard_map/ppermute | solution.py:22
  24.1 4.0 %collective-permute-start.1 = (bf16[64,2048]{1,0:T(8,128)(2,1)S(1)}, bf16[64,2048]{1,0:T(8,128)(2,1)}, u32[]{:S(2)}, u32[]{:S(2)}) collective-permute-start(bf16[64,2048]{1,0:T(8,128)(2,1)S(1)} %copy-done.11), channel_id=1, source_target_pairs={{0,1},{1,2},{2,3},{3,4},{4,5},{5,6},{6,7},{7,8},{8,9},{9,10},{10,1... | collective-permute-start | bytes 786440 | tf_op jit(solution)/shard_map/ppermute | solution.py:22
  28.0 2.0 reduce_window_sum.33
  30.0 0.9 slice_bitcast_fusion.2
  30.9 16.9 %all-gather = f32[16,1,4096]{2,1,0:T(1,128)S(1)} all-gather(f32[1,1,4096]{2,1,0:T(1,128)S(1)} %slice_bitcast_fusion.2), channel_id=1, replica_groups=mesh['grp'=2,'eg'=4,'kg'=4] {'eg','kg'}, dimensions={0}, use_global_device_ids=true | all-gather | bytes 278528 | tf_op jit(solution)/shard_map/all_gather | solution.py:77
  48.6 2.6 %exponential_select_fusion = f32[16,16,4096]{2,1,0:T(8,128)} fusion(f32[16,4096]{1,0:T(8,128)S(1)} %subtract_maximum_fusion, f32[16,4096]{1,0:T(8,128)S(1)} %copy-done.4, pred[16]{0:T(512)(128)(4,1)S(1)} %iota_compare_fusion.2), kind=kLoop, calls=%fused_computation.9 | loop fusion | flops 2097152 | bytes 4718608 | tf_op jit(solution)/shard_map/jit(_where)/select_n | solution.py:83
  51.2 8.9 %exponential_multiply_fusion = f32[64,16,4096]{2,1,0:T(8,128)} fusion(f32[64,4096]{1,0:T(8,128)S(1)} %copy-done.3, f32[16,4096]{1,0:T(8,128)S(1)} %copy-done.4, f32[64,16]{1,0:T(8,128)S(1)} %copy.50), kind=kLoop, calls=%fused_computation.2 | loop fusion | flops 8388608 | bytes 18092032 | tf_op jit(solution)/shard_map/mul | solution.py:84
  61.2 1.0 constant_dynamic-update-slice_fusion.2
  62.2 1.0 constant_dynamic-update-slice_fusion.1
  63.4 2.3 %fusion.49 = (f32[8,4,64]{2,1,0:T(4,128)S(1)}, f32[8,4,64,192]{3,2,1,0:T(8,128)}) fusion(pred[64,192]{1,0:T(8,128)(4,1)S(1)} %copy-done.13, bf16[64,8,4,128]{3,2,1,0:T(4,128)(2,1)S(1)} %reshape.151, bf16[192,8,128,1]{2,1,0,3:T(8,128)(2,1)S(1)} %bitcast.64), kind=kOutput, calls=%fused_computation.69 | convolution fusion | flops 102236352 | bytes 2510848 | tf_op jit(solution)/shard_map/sub | solution.py:104
  65.7 2.1 fusion.3
  68.2 1.2 convert_element_type.70
  69.4 4.6 %all-gather.3.cloned.1.call-done = f32[16,16,4096]{2,1,0:T(8,128)} async-done(((f32[1,16,4096]{2,1,0:T(8,128)}), f32[16,16,4096]{2,1,0:T(8,128)}) %all-gather.3.cloned.1.call-update) | async-done | bytes 4194320 | tf_op jit(solution)/shard_map/all_gather | solution.py:76
  74.0 3.9 %multiply_reduce_fusion.1 = f32[16,4096]{1,0:T(8,128)S(1)} fusion(f32[16,16,4096]{2,1,0:T(8,128)} %exponential_select_fusion, f32[16,16,4096]{2,1,0:T(8,128)} %all-gather.3.cloned.1.call-done), kind=kLoop, calls=%fused_computation.8 | loop fusion | flops 2031616 | bytes 8650752 | tf_op jit(solution)/shard_map/reduce_sum | solution.py:86
  77.9 9.3 %multiply_reduce_fusion = f32[64,4096]{1,0:T(8,128)S(1)} fusion(f32[64,16,4096]{2,1,0:T(8,128)} %exponential_multiply_fusion, f32[16,4096]{1,0:T(8,128)S(1)} %multiply_reduce_fusion.1), kind=kLoop, calls=%fused_computation.1 | loop fusion | flops 8126464 | bytes 18087936 | tf_op jit(solution)/shard_map/reduce_sum | solution.py:87
  87.2 2.1 %fusion.5 = bf16[64,4096]{1,0:T(8,128)(2,1)S(1)} fusion(f32[64,4096]{1,0:T(8,128)S(1)} %multiply_reduce_fusion, f32[8,8,32,128]{3,2,1,0:T(8,128)} %bitcast.63), kind=kLoop, calls=%fused_computation.19 | loop fusion | flops 524288 | bytes 2621440 | tf_op jit(solution)/shard_map/convert_element_type | solution.py:88
  90.1 15.0 %all_to_all.15 = bf16[4,16,4096]{2,1,0:T(8,128)(2,1)S(1)} all-to-all(bf16[4,16,4096]{2,1,0:T(8,128)(2,1)S(1)} %convolution_convert_fusion.1), channel_id=1, replica_groups=mesh['grp'=2,'eg'=4,'kg'=4] {'eg'}, dimensions={0} | all-to-all | bytes 1048576 | tf_op jit(solution)/shard_map/all_to_all | solution.py:166
  105.4 29.1 %all_to_all.16 = bf16[4,4,16,4096]{3,2,0,1:T(8,128)(2,1)S(1)} all-to-all(bf16[4,4,16,4096]{3,2,0,1:T(8,128)(2,1)S(1)} %broadcast_in_dim.84), channel_id=1, replica_groups=mesh['grp'=2,'eg'=4,'kg'=4] {'kg'}, dimensions={1} | all-to-all | bytes 4194304 | tf_op jit(solution)/shard_map/all_to_all | solution.py:168
  134.7 1.3 copy-done.1
  136.0 0.8 copy-done.5
  136.8 0.7 fusion.54
  137.6 5.9 %convolution_convert_fusion = bf16[256,4096]{1,0:T(8,128)(2,1)} fusion(bf16[256,4096]{1,0:T(8,128)(2,1)S(1)} %copy-done, bf16[256,4096]{1,0:T(8,128)(2,1)} %bitcast.57, bf16[4096,256]{1,0:T(8,128)(2,1)} %param.24, f32[256,256]{1,0:T(8,128)S(1)} %fusion.54), kind=kOutput, calls=%fused_computation.3 | convolution fusion | flops 1075183616 | bytes 8650752 | tf_op jit(solution)/shard_map/dot_general | solution.py:116
  143.5 7.5 %all-to-all-start.2 = ((bf16[16,16,4096]{2,1,0:T(8,128)(2,1)}), bf16[16,16,4096]{2,1,0:T(8,128)(2,1)}, u32[]{:S(2)}, u32[]{:S(2)}) async-start(bf16[16,16,4096]{2,1,0:T(8,128)(2,1)} %bitcast.58), calls=%async_computation.2 | async-start | bytes 4194304 | tf_op jit(solution)/shard_map/all_to_all | solution.py:171
  151.0 47.5 %all-to-all-done.2 = bf16[16,16,4096]{2,1,0:T(8,128)(2,1)} async-done(((bf16[16,16,4096]{2,1,0:T(8,128)(2,1)}), bf16[16,16,4096]{2,1,0:T(8,128)(2,1)}, u32[]{:S(2)}, u32[]{:S(2)}) %all-to-all-start.2) | async-done | bytes 2097184 | tf_op jit(solution)/shard_map/all_to_all | solution.py:171
  198.6 2.1 convert_reduce_fusion
  200.6 1.8 fusion.1
  (60 shorter events, 4.0 us)
Async XLA Ops:
  7.2 130.4 %copy-start = (bf16[256,4096]{1,0:T(8,128)(2,1)S(1)}, bf16[256,4096]{1,0:T(8,128)(2,1)}, u32[]{:S(2)}) copy-start(bf16[256,4096]{1,0:T(8,128)(2,1)} %param.25) | copy-start | bytes 6291460
  7.2 2.5 %copy-start.2 = (bf16[64,4096]{1,0:T(8,128)(2,1)S(1)}, bf16[64,4096]{1,0:T(8,128)(2,1)}, u32[]{:S(2)}) copy-start(bf16[64,4096]{1,0:T(8,128)(2,1)} %param.14) | copy-start | bytes 1572868
  7.2 2.5 %copy-start.9 = (bf16[64,4096]{1,0:T(8,128)(2,1)S(1)}, bf16[64,4096]{1,0:T(8,128)(2,1)}, u32[]{:S(2)}) copy-start(bf16[64,4096]{1,0:T(8,128)(2,1)} %param.13) | copy-start | bytes 1572868
  7.2 66.8 %all-gather.3.cloned.1.call-start = ((), (), s32[]{:S(2)}) async-start(), calls=%async_computation.3 | async-start | bytes 4456448 | tf_op jit(solution)/shard_map/all_gather | solution.py:76
  9.7 1.3 copy-start.4
  11.0 9.8 %copy-start.11 = (bf16[64,2048]{1,0:T(8,128)(2,1)S(1)}, bf16[64,2048]{1,0:T(8,128)(2,1)}, u32[]{:S(2)}) copy-start(bf16[64,2048]{1,0:T(8,128)(2,1)} %param.19) | copy-start | bytes 786436
  19.1 29.1 %copy-start.12 = (f32[16,64]{1,0:T(8,128)S(1)}, f32[16,64]{1,0:T(8,128)}, u32[]{:S(2)}) copy-start(f32[16,64]{1,0:T(8,128)} %c_ref.1) | copy-start | bytes 12292
  19.1 29.2 %copy-start.14 = (s32[64,2]{0,1:T(2,128)S(1)}, s32[64,2]{0,1:T(2,128)}, u32[]{:S(2)}) copy-start(s32[64,2]{0,1:T(2,128)} %param.21) | copy-start | bytes 1540
  20.9 40.3 %collective-permute-start = (bf16[64,2048]{1,0:T(8,128)(2,1)S(1)}, bf16[64,2048]{1,0:T(8,128)(2,1)}, u32[]{:S(2)}, u32[]{:S(2)}) collective-permute-start(bf16[64,2048]{1,0:T(8,128)(2,1)S(1)} %copy-done.11), channel_id=1, source_target_pairs={{0,2},{1,3},{2,4},{3,5},{4,6},{5,7},{6,8},{7,9},{8,10},{9,11},{10,... | collective-permute-start | bytes 786440 | tf_op jit(solution)/shard_map/ppermute | solution.py:22
  24.1 38.1 %collective-permute-start.1 = (bf16[64,2048]{1,0:T(8,128)(2,1)S(1)}, bf16[64,2048]{1,0:T(8,128)(2,1)}, u32[]{:S(2)}, u32[]{:S(2)}) collective-permute-start(bf16[64,2048]{1,0:T(8,128)(2,1)S(1)} %copy-done.11), channel_id=1, source_target_pairs={{0,1},{1,2},{2,3},{3,4},{4,5},{5,6},{6,7},{7,8},{8,9},{9,10},{10,1... | collective-permute-start | bytes 786440 | tf_op jit(solution)/shard_map/ppermute | solution.py:22
  48.6 2.6 %copy-start.3 = (f32[64,4096]{1,0:T(8,128)S(1)}, f32[64,4096]{1,0:T(8,128)}, u32[]{:S(2)}) copy-start(f32[64,4096]{1,0:T(8,128)} %reduce_window_sum.33) | copy-start | bytes 3145732
  51.2 9.6 %copy-start.8 = (bf16[64,4096]{1,0:T(8,128)(2,1)S(1)}, bf16[64,4096]{1,0:T(8,128)(2,1)}, u32[]{:S(2)}) copy-start(bf16[64,4096]{1,0:T(8,128)(2,1)} %param.18) | copy-start | bytes 1572868
  62.2 1.2 copy-start.13
  87.1 2.2 %copy-start.7 = (bf16[64,4096]{1,0:T(8,128)(2,1)S(1)}, bf16[64,4096]{1,0:T(8,128)(2,1)}, u32[]{:S(2)}) copy-start(bf16[64,4096]{1,0:T(8,128)(2,1)} %convert_element_type.70) | copy-start | bytes 1572868
  87.2 2.2 %copy-start.10 = (bf16[64,4096]{1,0:T(8,128)(2,1)S(1)}, bf16[64,4096]{1,0:T(8,128)(2,1)}, u32[]{:S(2)}) copy-start(bf16[64,4096]{1,0:T(8,128)(2,1)} %param.20) | copy-start | bytes 1572868
  89.3 0.8 copy-start.6
  134.5 2.3 %copy-start.5 = (bf16[4096,256]{1,0:T(8,128)(2,1)S(1)}, bf16[4096,256]{1,0:T(8,128)(2,1)}, u32[]{:S(2)}) copy-start(bf16[4096,256]{1,0:T(8,128)(2,1)} %param.23) | copy-start | bytes 6291460
  134.7 1.3 copy-start.1
  143.5 7.5 %copy-start.15 = (f32[64,2]{0,1:T(2,128)S(1)}, f32[64,2]{0,1:T(2,128)}, u32[]{:S(2)}) copy-start(f32[64,2]{0,1:T(2,128)} %param.22) | copy-start | bytes 1540
  143.5 55.0 %all-to-all-start.2 = ((bf16[16,16,4096]{2,1,0:T(8,128)(2,1)}), bf16[16,16,4096]{2,1,0:T(8,128)(2,1)}, u32[]{:S(2)}, u32[]{:S(2)}) async-start(bf16[16,16,4096]{2,1,0:T(8,128)(2,1)} %bitcast.58), calls=%async_computation.2 | async-start | bytes 4194304 | tf_op jit(solution)/shard_map/all_to_all | solution.py:171
Sparse Core Ops, SparseCore 0:
  21.0 52.9 all-gather.2

commit v15 on v13

--- a/solution.py
+++ b/solution.py
@@ -170,13 +170,13 @@
     returned = lax.all_to_all(
         partial_value.reshape((seq_count,) + arrived.shape[2:]), SEQ, split_axis=0, concat_axis=0, tiled=True
     )
-    summed = jnp.sum(returned.reshape(EXP_WIN, group, SLOTS, width), axis=1, dtype=jnp.float32)
-    weighting = (picker.astype(jnp.float32) * route_share[:, :, None]).reshape(
-        local_tokens, EXP_WIN * SLOTS
-    )
+    weighting = picker.astype(jnp.float32) * route_share[:, :, None]
+    weighting = jnp.broadcast_to(
+        weighting[:, :, None, :], (local_tokens, EXP_WIN, group, SLOTS)
+    ).reshape(local_tokens, -1)
     combined = jnp.dot(
         weighting,
-        summed.reshape(EXP_WIN * SLOTS, width),
+        returned.reshape(-1, width).astype(jnp.float32),
         precision=lax.Precision.HIGHEST,
         preferred_element_type=jnp.float32,
     )

time: 204 us -> 204 us (level)
    reduce_sum x1 -> x0, other arithmetic: 2.05 us -> none  [body(): jnp.sum(returned.reshape(EXP_WIN, group, SLOTS, width), axis=1, dtype=jnp...]
where the time goes in v15:
time: 204 us; the launch traced here: 203 us
  blocking collectives  62.4 us (31%)
  waiting for transfers between devices  61.2 us (30%)
  matrix products  15.1 us (7%)
  starting transfers between devices  14.9 us (7%)
  between operations  14.4 us (7%)
  local copies, waits for them, and re-layouts  14.1 us (7%)
  other arithmetic  13.8 us (7%)
  Pallas kernels  7.33 us (4%)
    all_to_all x1, waiting for transfers between devices, body(): lax.all_to_all(partial_value.reshape((seq_count,) + arrived.shape[2:]), S...  47.5 us
    all_to_all x1, blocking collectives, body(): lax.all_to_all(outgoing, 'kg', split_axis=1, concat_axis=1, tiled=True)  29 us
    all_gather x1, blocking collectives, ssm_correct(): sums = lax.all_gather(running[-1], SEQ)  18.4 us
    all_to_all x1, blocking collectives, body(): lax.all_to_all(packed, 'eg', split_axis=0, concat_axis=0, tiled=True)  15.1 us
    all_gather x1, waiting for transfers between devices, ssm_correct(): ends = lax.all_gather(local_end, SEQ)  13.7 us
    unnamed x39, local copies, waits for them, and re-layouts  9.5 us
    all_to_all x1, starting transfers between devices, body(): lax.all_to_all(partial_value.reshape((seq_count,) + arrived.shape[2:]), S...  7.59 us
    pallas_call x1, Pallas kernels, sweep(): pl.pallas_call(scan_kernel, grid=(rows // tile,), in_specs=[pl.BlockSpec(...  7.33 us
  transfers between devices with their start and end apart: 4, of which 2 were waited for; matrix products, arithmetic and copies ran while one was open for 7% of the time, Pallas kernels for 0%

profile of v15, /device:TPU:11, one launch (start us, length us, event | category | flops | bytes accessed | tf_op | source)
XLA Modules:
  0.0 203.2 jit_solution(14830376437698121269)
XLA Ops:
  7.2 1.3 convert_bitcast_fusion
  8.5 1.2 copy.66
  9.8 1.2 copy.67
  11.0 0.8 copy.68
  11.8 7.3 %shard_map.148 = (f32[64,32,128]{2,1,0:T(8,128)}, f32[16,32,128]{2,1,0:T(8,128)}) custom-call(f32[16,64]{1,0:T(8,128)} %b_ref.1, f32[16,64]{1,0:T(8,128)} %c_ref.1, f32[64,32,128]{2,1,0:T(8,128)} %bitcast.55, f32[64,32,128]{2,1,0:T(8,128)} %bitcast.56, f32[16,32,128]{2,1,0:T(8,128)} %bitcast.58), custom_call_target="tpu_custom_call" | custom-call | tf_op jit(solution)/shard_map/pallas_call | solution.py:51
  19.1 1.7 all_gather_reshape.3
  20.9 3.3 %collective-permute-start = (bf16[64,2048]{1,0:T(8,128)(2,1)}, bf16[64,2048]{1,0:T(8,128)(2,1)}, u32[]{:S(2)}, u32[]{:S(2)}) collective-permute-start(bf16[64,2048]{1,0:T(8,128)(2,1)} %param.19), channel_id=1, source_target_pairs={{0,2},{1,3},{2,4},{3,5},{4,6},{5,7},{6,8},{7,9},{8,10},{9,11},{10,... | collective-permute-start | bytes 786440 | tf_op jit(solution)/shard_map/ppermute | solution.py:22
  24.2 4.0 %collective-permute-start.1 = (bf16[64,2048]{1,0:T(8,128)(2,1)}, bf16[64,2048]{1,0:T(8,128)(2,1)}, u32[]{:S(2)}, u32[]{:S(2)}) collective-permute-start(bf16[64,2048]{1,0:T(8,128)(2,1)} %param.19), channel_id=1, source_target_pairs={{0,1},{1,2},{2,3},{3,4},{4,5},{5,6},{6,7},{7,8},{8,9},{9,10},{10,1... | collective-permute-start | bytes 786440 | tf_op jit(solution)/shard_map/ppermute | solution.py:22
  28.2 1.9 reduce_window_sum.33
  30.0 0.9 slice_bitcast_fusion.2
  30.9 18.4 %all-gather = f32[16,1,4096]{2,1,0:T(1,128)S(1)} all-gather(f32[1,1,4096]{2,1,0:T(1,128)S(1)} %slice_bitcast_fusion.2), channel_id=1, replica_groups=mesh['grp'=2,'eg'=4,'kg'=4] {'eg','kg'}, dimensions={0}, use_global_device_ids=true | all-gather | bytes 278528 | tf_op jit(solution)/shard_map/all_gather | solution.py:77
  50.0 0.7 subtract_maximum_fusion
  51.4 1.0 constant_dynamic-update-slice_fusion.2
  52.4 1.0 constant_dynamic-update-slice_fusion.1
  53.4 1.0 constant_dynamic-update-slice_fusion
  54.5 0.8 copy.70
  55.3 2.2 %fusion.42 = (f32[8,4,64]{2,1,0:T(4,128)S(1)}, f32[8,4,64,192]{3,2,1,0:T(8,128)}) fusion(pred[64,192]{1,0:T(8,128)(4,1)S(1)} %compare_and_fusion, bf16[64,8,4,128]{3,2,1,0:T(4,128)(2,1)S(1)} %reshape.157, bf16[192,8,128,1]{2,1,0,3:T(8,128)(2,1)S(1)} %bitcast.61), kind=kOutput, calls=%fused_computation.60 | convolution fusion | flops 102236352 | bytes 2510848 | tf_op jit(solution)/shard_map/sub | solution.py:103
  57.5 2.3 %fusion.2 = bf16[64,8,4,128]{3,0,2,1:T(8,128)(2,1)S(1)} fusion(f32[8,4,64,192]{3,2,1,0:T(8,128)} %get-tuple-element.14, f32[8,4,64]{2,1,0:T(4,128)S(1)} %get-tuple-element.13, bf16[192,8,128,1]{2,1,0,3:T(8,128)(2,1)} %bitcast.62), kind=kOutput, calls=%fused_computation.11 | convolution fusion | flops 101711872 | bytes 2498560 | tf_op jit(solution)/shard_map/kyje,eku->jkyu/dot_general | solution.py:105
  59.8 0.4 copy.55
  60.6 13.7 %all-gather.3.cloned.1.call-done = f32[16,16,4096]{2,1,0:T(8,128)} async-done(((f32[1,16,4096]{2,1,0:T(8,128)}), f32[16,16,4096]{2,1,0:T(8,128)}) %all-gather.3.cloned.1.call-update) | async-done | bytes 4194320 | tf_op jit(solution)/shard_map/all_gather | solution.py:76
  74.3 3.1 %select_reduce_fusion = f32[16,4096]{1,0:T(8,128)S(1)} fusion(f32[16,16,4096]{2,1,0:T(8,128)} %all-gather.3.cloned.1.call-done, f32[16,4096]{1,0:T(8,128)} %subtract_maximum_fusion, f32[16,4096]{1,0:T(8,128)S(1)} %copy-done.7, pred[16]{0:T(512)(128)(4,1)S(1)} %iota_compare_fusion.2), kind=kLoop, calls=%fused_computation.5 | loop fusion | flops 4128768 | bytes 4980752 | tf_op jit(solution)/shard_map/reduce_sum | solution.py:84
  77.5 5.3 %multiply_reduce_fusion = f32[64,4096]{1,0:T(8,128)S(1)} fusion(f32[16,4096]{1,0:T(8,128)S(1)} %select_reduce_fusion, f32[64,4096]{1,0:T(8,128)S(1)} %copy-done.6, f32[16,4096]{1,0:T(8,128)S(1)} %copy-done.7, f32[64,16]{1,0:T(8,128)S(1)} %copy.51), kind=kLoop, calls=%fused_computation.1 | loop fusion | flops 16515072 | bytes 2625536 | tf_op jit(solution)/shard_map/reduce_sum | solution.py:86
  82.8 0.7 fusion.4
  84.2 15.1 %all_to_all.15 = bf16[4,16,4096]{2,1,0:T(8,128)(2,1)S(1)} all-to-all(bf16[4,16,4096]{2,1,0:T(8,128)(2,1)S(1)} %convolution_convert_fusion.1), channel_id=1, replica_groups=mesh['grp'=2,'eg'=4,'kg'=4] {'eg'}, dimensions={0} | all-to-all | bytes 1048576 | tf_op jit(solution)/shard_map/all_to_all | solution.py:165
  99.5 29.0 %all_to_all.16 = bf16[4,4,16,4096]{3,2,0,1:T(8,128)(2,1)S(1)} all-to-all(bf16[4,4,16,4096]{3,2,0,1:T(8,128)(2,1)S(1)} %broadcast_in_dim.61), channel_id=1, replica_groups=mesh['grp'=2,'eg'=4,'kg'=4] {'kg'}, dimensions={1} | all-to-all | bytes 4194304 | tf_op jit(solution)/shard_map/all_to_all | solution.py:167
  128.7 1.3 copy-done.1
  130.0 0.8 copy-done.3
  130.9 0.7 fusion.47
  131.6 5.9 %convolution_convert_fusion = bf16[256,4096]{1,0:T(8,128)(2,1)} fusion(bf16[256,4096]{1,0:T(8,128)(2,1)S(1)} %copy-done, bf16[256,4096]{1,0:T(8,128)(2,1)} %bitcast.53, bf16[4096,256]{1,0:T(8,128)(2,1)} %param.24, f32[256,256]{1,0:T(8,128)S(1)} %fusion.47), kind=kOutput, calls=%fused_computation.2 | convolution fusion | flops 1075183616 | bytes 8650752 | tf_op jit(solution)/shard_map/dot_general | solution.py:115
  137.5 7.6 %all-to-all-start.2 = ((bf16[16,16,4096]{2,1,0:T(8,128)(2,1)}), bf16[16,16,4096]{2,1,0:T(8,128)(2,1)}, u32[]{:S(2)}, u32[]{:S(2)}) async-start(bf16[16,16,4096]{2,1,0:T(8,128)(2,1)} %bitcast.54), calls=%async_computation.2 | async-start | bytes 4194304 | tf_op jit(solution)/shard_map/all_to_all | solution.py:170
  145.2 47.5 %all-to-all-done.2 = bf16[16,16,4096]{2,1,0:T(8,128)(2,1)} async-done(((bf16[16,16,4096]{2,1,0:T(8,128)(2,1)}), bf16[16,16,4096]{2,1,0:T(8,128)(2,1)}, u32[]{:S(2)}, u32[]{:S(2)}) %all-to-all-start.2) | async-done | bytes 2097184 | tf_op jit(solution)/shard_map/all_to_all | solution.py:170
  192.7 3.6 %convolution_convert_fusion.2 = bf16[64,4096]{1,0:T(8,128)(2,1)} fusion(f32[64,256]{0,1:T(8,128)S(1)} %bitcast.60, bf16[256,4096]{1,0:T(8,128)(2,1)} %bitcast.10), kind=kOutput, calls=%fused_computation.4 | convolution fusion | flops 805568512 | bytes 2686976 | tf_op jit(solution)/shard_map/dot_general | solution.py:177
  (57 shorter events, 3.1 us)
Async XLA Ops:
  7.2 124.4 %copy-start = (bf16[256,4096]{1,0:T(8,128)(2,1)S(1)}, bf16[256,4096]{1,0:T(8,128)(2,1)}, u32[]{:S(2)}) copy-start(bf16[256,4096]{1,0:T(8,128)(2,1)} %param.25) | copy-start | bytes 6291460
  7.2 2.5 %copy-start.2 = (bf16[64,4096]{1,0:T(8,128)(2,1)S(1)}, bf16[64,4096]{1,0:T(8,128)(2,1)}, u32[]{:S(2)}) copy-start(bf16[64,4096]{1,0:T(8,128)(2,1)} %param.14) | copy-start | bytes 1572868
  7.2 2.5 %copy-start.10 = (bf16[64,4096]{1,0:T(8,128)(2,1)S(1)}, bf16[64,4096]{1,0:T(8,128)(2,1)}, u32[]{:S(2)}) copy-start(bf16[64,4096]{1,0:T(8,128)(2,1)} %param.13) | copy-start | bytes 1572868
  7.2 67.1 %all-gather.3.cloned.1.call-start = ((), (), s32[]{:S(2)}) async-start(), calls=%async_computation.3 | async-start | bytes 4456448 | tf_op jit(solution)/shard_map/all_gather | solution.py:76
  9.7 1.3 copy-start.7
  19.1 30.6 %copy-start.14 = (s32[64,2]{0,1:T(2,128)S(1)}, s32[64,2]{0,1:T(2,128)}, u32[]{:S(2)}) copy-start(s32[64,2]{0,1:T(2,128)} %param.21) | copy-start | bytes 1540
  20.8 30.0 %copy-start.12 = (f32[16,64]{1,0:T(8,128)S(1)}, f32[16,64]{1,0:T(8,128)}, u32[]{:S(2)}) copy-start(f32[16,64]{1,0:T(8,128)} %c_ref.1) | copy-start | bytes 12292
  20.8 30.1 %copy-start.9 = (bf16[64,4096]{1,0:T(8,128)(2,1)S(1)}, bf16[64,4096]{1,0:T(8,128)(2,1)}, u32[]{:S(2)}) copy-start(bf16[64,4096]{1,0:T(8,128)(2,1)} %param.18) | copy-start | bytes 1572868
  20.9 30.5 %collective-permute-start = (bf16[64,2048]{1,0:T(8,128)(2,1)}, bf16[64,2048]{1,0:T(8,128)(2,1)}, u32[]{:S(2)}, u32[]{:S(2)}) collective-permute-start(bf16[64,2048]{1,0:T(8,128)(2,1)} %param.19), channel_id=1, source_target_pairs={{0,2},{1,3},{2,4},{3,5},{4,6},{5,7},{6,8},{7,9},{8,10},{9,11},{10,... | collective-permute-start | bytes 786440 | tf_op jit(solution)/shard_map/ppermute | solution.py:22
  24.2 28.2 %collective-permute-start.1 = (bf16[64,2048]{1,0:T(8,128)(2,1)}, bf16[64,2048]{1,0:T(8,128)(2,1)}, u32[]{:S(2)}, u32[]{:S(2)}) collective-permute-start(bf16[64,2048]{1,0:T(8,128)(2,1)} %param.19), channel_id=1, source_target_pairs={{0,1},{1,2},{2,3},{3,4},{4,5},{5,6},{6,7},{7,8},{8,9},{9,10},{10,1... | collective-permute-start | bytes 786440 | tf_op jit(solution)/shard_map/ppermute | solution.py:22
  60.6 22.9 %copy-start.5 = (bf16[64,4096]{1,0:T(8,128)(2,1)}, bf16[64,4096]{1,0:T(8,128)(2,1)S(1)}, u32[]{:S(2)}) copy-start(bf16[64,4096]{1,0:T(8,128)(2,1)S(1)} %convert_element_type.65) | copy-start | bytes 1572868
  74.3 3.1 %copy-start.6 = (f32[64,4096]{1,0:T(8,128)S(1)}, f32[64,4096]{1,0:T(8,128)}, u32[]{:S(2)}) copy-start(f32[64,4096]{1,0:T(8,128)} %reduce_window_sum.33) | copy-start | bytes 3145732
  77.5 5.4 %copy-start.8 = (f32[64,32,128]{2,1,0:T(8,128)S(1)}, f32[64,32,128]{2,1,0:T(8,128)}, u32[]{:S(2)}) copy-start(f32[64,32,128]{2,1,0:T(8,128)} %get-tuple-element.5) | copy-start | bytes 3145732
  82.8 1.0 copy-start.11
  83.5 16.0 %copy-start.4 = (bf16[64,4096]{1,0:T(8,128)(2,1)}, bf16[64,4096]{1,0:T(8,128)(2,1)S(1)}, u32[]{:S(2)}) copy-start(bf16[64,4096]{1,0:T(8,128)(2,1)S(1)} %fusion.4) | copy-start | bytes 1572868
  128.5 2.3 %copy-start.3 = (bf16[4096,256]{1,0:T(8,128)(2,1)S(1)}, bf16[4096,256]{1,0:T(8,128)(2,1)}, u32[]{:S(2)}) copy-start(bf16[4096,256]{1,0:T(8,128)(2,1)} %param.23) | copy-start | bytes 6291460
  128.7 1.3 copy-start.1
  137.5 7.6 %copy-start.13 = (f32[64,2]{0,1:T(2,128)S(1)}, f32[64,2]{0,1:T(2,128)}, u32[]{:S(2)}) copy-start(f32[64,2]{0,1:T(2,128)} %param.22) | copy-start | bytes 1540
  137.5 55.1 %all-to-all-start.2 = ((bf16[16,16,4096]{2,1,0:T(8,128)(2,1)}), bf16[16,16,4096]{2,1,0:T(8,128)(2,1)}, u32[]{:S(2)}, u32[]{:S(2)}) async-start(bf16[16,16,4096]{2,1,0:T(8,128)(2,1)} %bitcast.54), calls=%async_computation.2 | async-start | bytes 4194304 | tf_op jit(solution)/shard_map/all_to_all | solution.py:170
Sparse Core Ops, SparseCore 0:
  21.0 53.2 all-gather.2

commit v16 on v13

--- a/solution.py
+++ b/solution.py
@@ -27,8 +27,8 @@
     steps = dt_ref.shape[0]
     h = [jnp.zeros(dt_ref.shape[1:], jnp.float32) for _ in range(states)]
     for t in range(steps):
-        d = dt_ref[t]
-        u = inj_ref[t]
+        d = dt_ref[t].astype(jnp.float32)
+        u = d * inj_ref[t].astype(jnp.float32)
         total = None
         for n in range(states):
             h[n] = jnp.exp(d * a_ref[n]) * h[n] + b_ref[n, t] * u
@@ -44,9 +44,9 @@
     states = rates.shape[0]
     lanes = 128
     rows = channels // lanes
-    tile = 8
+    tile = 16
     dt3 = deltas.reshape(steps, rows, lanes)
-    inj3 = (deltas * values).reshape(steps, rows, lanes)
+    inj3 = values.reshape(steps, rows, lanes)
     a3 = rates.reshape(states, rows, lanes)
     read3, end3 = pl.pallas_call(
         scan_kernel,
@@ -132,9 +132,8 @@
     *,
     seq_count,
 ):
-    values = ssm_in.astype(jnp.float32)
     deltas = ssm_dt.astype(jnp.float32)
-    local_end, local_read = sweep(values, deltas, ssm_a, ssm_b, ssm_c)
+    local_end, local_read = sweep(ssm_in, ssm_dt, ssm_a, ssm_b, ssm_c)
     ssm_out = ssm_correct(local_read, local_end, deltas, ssm_a, ssm_c)
     count = attn_q.shape[0]
     block_index = lax.axis_index(SEQ)

time: 204 us -> 205 us (level)
    unnamed x39 -> x37, local copies, waits for them, and re-layouts: 9.5 us -> 11.2 us
where the time goes in v16:
time: 205 us; the launch traced here: 204 us
  blocking collectives  62.7 us (31%)
  waiting for transfers between devices  61.2 us (30%)
  local copies, waits for them, and re-layouts  15.7 us (8%)
  starting transfers between devices  14.8 us (7%)
  other arithmetic  14.5 us (7%)
  between operations  14.3 us (7%)
  matrix products  13.3 us (6%)
  Pallas kernels  7.43 us (4%)
    all_to_all x1, waiting for transfers between devices, body(): lax.all_to_all(partial_value.reshape((seq_count,) + arrived.shape[2:]), S...  47.5 us
    all_to_all x1, blocking collectives, body(): lax.all_to_all(outgoing, 'kg', split_axis=1, concat_axis=1, tiled=True)  29.1 us
    all_gather x1, blocking collectives, ssm_correct(): sums = lax.all_gather(running[-1], SEQ)  18.4 us
    all_to_all x1, blocking collectives, body(): lax.all_to_all(packed, 'eg', split_axis=0, concat_axis=0, tiled=True)  15.2 us
    all_gather x1, waiting for transfers between devices, ssm_correct(): ends = lax.all_gather(local_end, SEQ)  13.6 us
    unnamed x37, local copies, waits for them, and re-layouts  11.2 us
    all_to_all x1, starting transfers between devices, body(): lax.all_to_all(partial_value.reshape((seq_count,) + arrived.shape[2:]), S...  7.5 us
    pallas_call x1, Pallas kernels, sweep(): pl.pallas_call(scan_kernel, grid=(rows // tile,), in_specs=[pl.BlockSpec(...  7.43 us
  transfers between devices with their start and end apart: 4, of which 2 were waited for; matrix products, arithmetic and copies ran while one was open for 7% of the time, Pallas kernels for 0%

profile of v16, /device:TPU:11, one launch (start us, length us, event | category | flops | bytes accessed | tf_op | source)
XLA Modules:
  0.0 204.0 jit_solution(16211243805756963758)
XLA Ops:
  7.2 2.1 %copy.65 = bf16[8,8,32,128]{3,2,1,0:T(8,128)(2,1)} copy(bf16[8,8,32,128]{3,1,2,0:T(8,128)(2,1)} %bitcast.57) | data formatting | bytes 1048576
  9.3 2.0 copy.66
  11.3 0.8 copy.67
  12.1 7.4 %shard_map.148 = (f32[64,32,128]{2,1,0:T(8,128)}, f32[16,32,128]{2,1,0:T(8,128)}) custom-call(f32[16,64]{1,0:T(8,128)} %b_ref.1, f32[16,64]{1,0:T(8,128)} %c_ref.1, bf16[64,32,128]{2,1,0:T(8,128)(2,1)} %bitcast.58, bf16[64,32,128]{2,1,0:T(8,128)(2,1)} %bitcast.59, f32[16,32,128]{2,1,0:T(8,128)} %bitcast.62), custom_call_target="tpu_custom_call" | custom-call | tf_op jit(solution)/shard_map/pallas_call | solution.py:51
  19.5 1.7 all_gather_reshape.3
  21.3 3.3 %collective-permute-start = (bf16[64,2048]{1,0:T(8,128)(2,1)}, bf16[64,2048]{1,0:T(8,128)(2,1)}, u32[]{:S(2)}, u32[]{:S(2)}) collective-permute-start(bf16[64,2048]{1,0:T(8,128)(2,1)} %param.19), channel_id=1, source_target_pairs={{0,2},{1,3},{2,4},{3,5},{4,6},{5,7},{6,8},{7,9},{8,10},{9,11},{10,... | collective-permute-start | bytes 786440 | tf_op jit(solution)/shard_map/ppermute | solution.py:22
  24.6 4.0 %collective-permute-start.1 = (bf16[64,2048]{1,0:T(8,128)(2,1)}, bf16[64,2048]{1,0:T(8,128)(2,1)}, u32[]{:S(2)}, u32[]{:S(2)}) collective-permute-start(bf16[64,2048]{1,0:T(8,128)(2,1)} %param.19), channel_id=1, source_target_pairs={{0,1},{1,2},{2,3},{3,4},{4,5},{5,6},{6,7},{7,8},{8,9},{9,10},{10,1... | collective-permute-start | bytes 786440 | tf_op jit(solution)/shard_map/ppermute | solution.py:22
  28.6 1.9 reduce_window_sum.33
  30.4 0.9 slice_bitcast_fusion.2
  31.4 18.4 %all-gather = f32[16,1,4096]{2,1,0:T(1,128)S(1)} all-gather(f32[1,1,4096]{2,1,0:T(1,128)S(1)} %slice_bitcast_fusion.2), channel_id=1, replica_groups=mesh['grp'=2,'eg'=4,'kg'=4] {'eg','kg'}, dimensions={0}, use_global_device_ids=true | all-gather | bytes 278528 | tf_op jit(solution)/shard_map/all_gather | solution.py:77
  50.4 0.7 subtract_maximum_fusion
  51.8 1.0 constant_dynamic-update-slice_fusion.2
  52.8 1.0 constant_dynamic-update-slice_fusion.1
  53.8 1.0 constant_dynamic-update-slice_fusion
  54.9 0.8 copy.69
  55.7 2.2 %fusion.49 = (f32[8,4,64]{2,1,0:T(4,128)S(1)}, f32[8,4,64,192]{3,2,1,0:T(8,128)}) fusion(pred[64,192]{1,0:T(8,128)(4,1)S(1)} %compare_and_fusion, bf16[64,8,4,128]{3,2,1,0:T(4,128)(2,1)S(1)} %reshape.151, bf16[192,8,128,1]{2,1,0,3:T(8,128)(2,1)S(1)} %bitcast.64), kind=kOutput, calls=%fused_computation.65 | convolution fusion | flops 102236352 | bytes 2510848 | tf_op jit(solution)/shard_map/sub | solution.py:103
  58.0 2.3 %fusion.3 = bf16[64,8,4,128]{3,0,2,1:T(8,128)(2,1)S(1)} fusion(f32[8,4,64,192]{3,2,1,0:T(8,128)} %get-tuple-element.14, f32[8,4,64]{2,1,0:T(4,128)S(1)} %get-tuple-element.13, bf16[192,8,128,1]{2,1,0,3:T(8,128)(2,1)} %bitcast.65), kind=kOutput, calls=%fused_computation.13 | convolution fusion | flops 101711872 | bytes 2498560 | tf_op jit(solution)/shard_map/kyje,eku->jkyu/dot_general | solution.py:105
  60.2 0.4 copy.54
  61.0 13.6 %all-gather.3.cloned.1.call-done = f32[16,16,4096]{2,1,0:T(8,128)} async-done(((f32[1,16,4096]{2,1,0:T(8,128)}), f32[16,16,4096]{2,1,0:T(8,128)}) %all-gather.3.cloned.1.call-update) | async-done | bytes 4194320 | tf_op jit(solution)/shard_map/all_gather | solution.py:76
  74.7 3.1 %select_reduce_fusion = f32[16,4096]{1,0:T(8,128)S(1)} fusion(f32[16,16,4096]{2,1,0:T(8,128)} %all-gather.3.cloned.1.call-done, f32[16,4096]{1,0:T(8,128)} %subtract_maximum_fusion, f32[16,4096]{1,0:T(8,128)S(1)} %copy-done.7, pred[16]{0:T(512)(128)(4,1)S(1)} %iota_compare_fusion.2), kind=kLoop, calls=%fused_computation.7 | loop fusion | flops 4128768 | bytes 4980752 | tf_op jit(solution)/shard_map/reduce_sum | solution.py:84
  77.8 5.3 %multiply_reduce_fusion = f32[64,4096]{1,0:T(8,128)S(1)} fusion(f32[16,4096]{1,0:T(8,128)S(1)} %select_reduce_fusion, f32[64,4096]{1,0:T(8,128)S(1)} %copy-done.6, f32[16,4096]{1,0:T(8,128)S(1)} %copy-done.7, f32[64,16]{1,0:T(8,128)S(1)} %copy.50), kind=kLoop, calls=%fused_computation.1 | loop fusion | flops 16515072 | bytes 2625536 | tf_op jit(solution)/shard_map/reduce_sum | solution.py:86
  83.2 0.7 fusion.5
  84.6 15.2 %all_to_all.15 = bf16[4,16,4096]{2,1,0:T(8,128)(2,1)S(1)} all-to-all(bf16[4,16,4096]{2,1,0:T(8,128)(2,1)S(1)} %convolution_convert_fusion.1), channel_id=1, replica_groups=mesh['grp'=2,'eg'=4,'kg'=4] {'eg'}, dimensions={0} | all-to-all | bytes 1048576 | tf_op jit(solution)/shard_map/all_to_all | solution.py:164
  100.1 29.1 %all_to_all.16 = bf16[4,4,16,4096]{3,2,0,1:T(8,128)(2,1)S(1)} all-to-all(bf16[4,4,16,4096]{3,2,0,1:T(8,128)(2,1)S(1)} %broadcast_in_dim.84), channel_id=1, replica_groups=mesh['grp'=2,'eg'=4,'kg'=4] {'kg'}, dimensions={1} | all-to-all | bytes 4194304 | tf_op jit(solution)/shard_map/all_to_all | solution.py:166
  129.4 1.3 copy-done.1
  130.7 0.8 copy-done.2
  131.5 0.7 fusion.54
  132.2 5.9 %convolution_convert_fusion = bf16[256,4096]{1,0:T(8,128)(2,1)} fusion(bf16[256,4096]{1,0:T(8,128)(2,1)S(1)} %copy-done, bf16[256,4096]{1,0:T(8,128)(2,1)} %bitcast.55, bf16[4096,256]{1,0:T(8,128)(2,1)} %param.24, f32[256,256]{1,0:T(8,128)S(1)} %fusion.54), kind=kOutput, calls=%fused_computation.2 | convolution fusion | flops 1075183616 | bytes 8650752 | tf_op jit(solution)/shard_map/dot_general | solution.py:115
  138.2 7.5 %all-to-all-start.2 = ((bf16[16,16,4096]{2,1,0:T(8,128)(2,1)}), bf16[16,16,4096]{2,1,0:T(8,128)(2,1)}, u32[]{:S(2)}, u32[]{:S(2)}) async-start(bf16[16,16,4096]{2,1,0:T(8,128)(2,1)} %bitcast.56), calls=%async_computation.2 | async-start | bytes 4194304 | tf_op jit(solution)/shard_map/all_to_all | solution.py:169
  145.7 47.5 %all-to-all-done.2 = bf16[16,16,4096]{2,1,0:T(8,128)(2,1)} async-done(((bf16[16,16,4096]{2,1,0:T(8,128)(2,1)}), bf16[16,16,4096]{2,1,0:T(8,128)(2,1)}, u32[]{:S(2)}, u32[]{:S(2)}) %all-to-all-start.2) | async-done | bytes 2097184 | tf_op jit(solution)/shard_map/all_to_all | solution.py:169
  193.2 2.1 %convert_reduce_fusion = f32[4,16,4096]{2,1,0:T(8,128)S(1)} fusion(bf16[16,16,4096]{2,1,0:T(8,128)(2,1)} %all-to-all-done.2), kind=kLoop, calls=%fused_computation.6 | loop fusion | flops 1835008 | bytes 3145728 | tf_op jit(solution)/shard_map/reduce_sum | solution.py:172
  195.3 1.8 fusion.1
  (52 shorter events, 3.0 us)
Async XLA Ops:
  7.2 125.0 %copy-start = (bf16[256,4096]{1,0:T(8,128)(2,1)S(1)}, bf16[256,4096]{1,0:T(8,128)(2,1)}, u32[]{:S(2)}) copy-start(bf16[256,4096]{1,0:T(8,128)(2,1)} %param.25) | copy-start | bytes 6291460
  7.2 4.2 %copy-start.7 = (f32[16,4096]{1,0:T(8,128)S(1)}, f32[16,4096]{1,0:T(8,128)}, u32[]{:S(2)}) copy-start(f32[16,4096]{1,0:T(8,128)} %param.15) | copy-start | bytes 786436
  7.2 67.5 %all-gather.3.cloned.1.call-start = ((), (), s32[]{:S(2)}) async-start(), calls=%async_computation.3 | async-start | bytes 4456448 | tf_op jit(solution)/shard_map/all_gather | solution.py:76
  9.3 19.2 %copy-start.3 = (bf16[64,4096]{1,0:T(8,128)(2,1)S(1)}, bf16[64,4096]{1,0:T(8,128)(2,1)}, u32[]{:S(2)}) copy-start(bf16[64,4096]{1,0:T(8,128)(2,1)} %param.14) | copy-start | bytes 1572868
  19.5 30.6 %copy-start.12 = (s32[64,2]{0,1:T(2,128)S(1)}, s32[64,2]{0,1:T(2,128)}, u32[]{:S(2)}) copy-start(s32[64,2]{0,1:T(2,128)} %param.21) | copy-start | bytes 1540
  21.2 30.0 %copy-start.11 = (f32[16,64]{1,0:T(8,128)S(1)}, f32[16,64]{1,0:T(8,128)}, u32[]{:S(2)}) copy-start(f32[16,64]{1,0:T(8,128)} %c_ref.1) | copy-start | bytes 12292
  21.3 30.1 %copy-start.9 = (bf16[64,4096]{1,0:T(8,128)(2,1)S(1)}, bf16[64,4096]{1,0:T(8,128)(2,1)}, u32[]{:S(2)}) copy-start(bf16[64,4096]{1,0:T(8,128)(2,1)} %param.18) | copy-start | bytes 1572868
  21.3 30.5 %collective-permute-start = (bf16[64,2048]{1,0:T(8,128)(2,1)}, bf16[64,2048]{1,0:T(8,128)(2,1)}, u32[]{:S(2)}, u32[]{:S(2)}) collective-permute-start(bf16[64,2048]{1,0:T(8,128)(2,1)} %param.19), channel_id=1, source_target_pairs={{0,2},{1,3},{2,4},{3,5},{4,6},{5,7},{6,8},{7,9},{8,10},{9,11},{10,... | collective-permute-start | bytes 786440 | tf_op jit(solution)/shard_map/ppermute | solution.py:22
  24.6 28.2 %collective-permute-start.1 = (bf16[64,2048]{1,0:T(8,128)(2,1)}, bf16[64,2048]{1,0:T(8,128)(2,1)}, u32[]{:S(2)}, u32[]{:S(2)}) collective-permute-start(bf16[64,2048]{1,0:T(8,128)(2,1)} %param.19), channel_id=1, source_target_pairs={{0,1},{1,2},{2,3},{3,4},{4,5},{5,6},{6,7},{7,8},{8,9},{9,10},{10,1... | collective-permute-start | bytes 786440 | tf_op jit(solution)/shard_map/ppermute | solution.py:22
  61.0 22.9 %copy-start.5 = (bf16[64,4096]{1,0:T(8,128)(2,1)}, bf16[64,4096]{1,0:T(8,128)(2,1)S(1)}, u32[]{:S(2)}) copy-start(bf16[64,4096]{1,0:T(8,128)(2,1)S(1)} %convert_element_type.66) | copy-start | bytes 1572868
  74.7 3.1 %copy-start.6 = (f32[64,4096]{1,0:T(8,128)S(1)}, f32[64,4096]{1,0:T(8,128)}, u32[]{:S(2)}) copy-start(f32[64,4096]{1,0:T(8,128)} %reduce_window_sum.33) | copy-start | bytes 3145732
  77.8 5.4 %copy-start.8 = (f32[64,32,128]{2,1,0:T(8,128)S(1)}, f32[64,32,128]{2,1,0:T(8,128)}, u32[]{:S(2)}) copy-start(f32[64,32,128]{2,1,0:T(8,128)} %get-tuple-element.5) | copy-start | bytes 3145732
  83.2 1.0 copy-start.10
  83.9 16.2 %copy-start.4 = (bf16[64,4096]{1,0:T(8,128)(2,1)}, bf16[64,4096]{1,0:T(8,128)(2,1)S(1)}, u32[]{:S(2)}) copy-start(bf16[64,4096]{1,0:T(8,128)(2,1)S(1)} %fusion.5) | copy-start | bytes 1572868
  129.1 2.3 %copy-start.2 = (bf16[4096,256]{1,0:T(8,128)(2,1)S(1)}, bf16[4096,256]{1,0:T(8,128)(2,1)}, u32[]{:S(2)}) copy-start(bf16[4096,256]{1,0:T(8,128)(2,1)} %param.23) | copy-start | bytes 6291460
  129.4 1.3 copy-start.1
  138.2 7.5 %copy-start.13 = (f32[64,2]{0,1:T(2,128)S(1)}, f32[64,2]{0,1:T(2,128)}, u32[]{:S(2)}) copy-start(f32[64,2]{0,1:T(2,128)} %param.22) | copy-start | bytes 1540
  138.2 55.0 %all-to-all-start.2 = ((bf16[16,16,4096]{2,1,0:T(8,128)(2,1)}), bf16[16,16,4096]{2,1,0:T(8,128)(2,1)}, u32[]{:S(2)}, u32[]{:S(2)}) async-start(bf16[16,16,4096]{2,1,0:T(8,128)(2,1)} %bitcast.56), calls=%async_computation.2 | async-start | bytes 4194304 | tf_op jit(solution)/shard_map/all_to_all | solution.py:169
Sparse Core Ops, SparseCore 0:
  21.4 53.2 all-gather.2

commit v17 on v13

--- a/solution.py
+++ b/solution.py
@@ -44,7 +44,7 @@
     states = rates.shape[0]
     lanes = 128
     rows = channels // lanes
-    tile = 8
+    tile = 16
     dt3 = deltas.reshape(steps, rows, lanes)
     inj3 = (deltas * values).reshape(steps, rows, lanes)
     a3 = rates.reshape(states, rows, lanes)

time: 204 us -> 204 us (level)
  no operation moved by 1% of the time
where the time goes in v17:
time: 204 us; the launch traced here: 203 us
  blocking collectives  62.6 us (31%)
  waiting for transfers between devices  61.1 us (30%)
  other arithmetic  15.8 us (8%)
  starting transfers between devices  14.8 us (7%)
  between operations  14.3 us (7%)
  local copies, waits for them, and re-layouts  14 us (7%)
  matrix products  13.3 us (7%)
  Pallas kernels  7.47 us (4%)
    all_to_all x1, waiting for transfers between devices, body(): lax.all_to_all(partial_value.reshape((seq_count,) + arrived.shape[2:]), S...  47.5 us
    all_to_all x1, blocking collectives, body(): lax.all_to_all(outgoing, 'kg', split_axis=1, concat_axis=1, tiled=True)  29.1 us
    all_gather x1, blocking collectives, ssm_correct(): sums = lax.all_gather(running[-1], SEQ)  18.4 us
    all_to_all x1, blocking collectives, body(): lax.all_to_all(packed, 'eg', split_axis=0, concat_axis=0, tiled=True)  15.1 us
    all_gather x1, waiting for transfers between devices, ssm_correct(): ends = lax.all_gather(local_end, SEQ)  13.5 us
    unnamed x39, local copies, waits for them, and re-layouts  9.48 us
    all_to_all x1, starting transfers between devices, body(): lax.all_to_all(partial_value.reshape((seq_count,) + arrived.shape[2:]), S...  7.5 us
    pallas_call x1, Pallas kernels, sweep(): pl.pallas_call(scan_kernel, grid=(rows // tile,), in_specs=[pl.BlockSpec(...  7.47 us
  transfers between devices with their start and end apart: 4, of which 2 were waited for; matrix products, arithmetic and copies ran while one was open for 7% of the time, Pallas kernels for 0%

profile of v17, /device:TPU:11, one launch (start us, length us, event | category | flops | bytes accessed | tf_op | source)
XLA Modules:
  0.0 203.5 jit_solution(7640901065576041337)
XLA Ops:
  7.2 1.3 convert_bitcast_fusion
  8.5 1.2 copy.65
  9.8 1.2 copy.66
  11.0 0.8 copy.67
  11.8 7.5 %shard_map.148 = (f32[64,32,128]{2,1,0:T(8,128)}, f32[16,32,128]{2,1,0:T(8,128)}) custom-call(f32[16,64]{1,0:T(8,128)} %b_ref.1, f32[16,64]{1,0:T(8,128)} %c_ref.1, f32[64,32,128]{2,1,0:T(8,128)} %bitcast.59, f32[64,32,128]{2,1,0:T(8,128)} %bitcast.60, f32[16,32,128]{2,1,0:T(8,128)} %bitcast.62), custom_call_target="tpu_custom_call" | custom-call | tf_op jit(solution)/shard_map/pallas_call | solution.py:51
  19.3 1.7 all_gather_reshape.3
  21.0 3.3 %collective-permute-start = (bf16[64,2048]{1,0:T(8,128)(2,1)}, bf16[64,2048]{1,0:T(8,128)(2,1)}, u32[]{:S(2)}, u32[]{:S(2)}) collective-permute-start(bf16[64,2048]{1,0:T(8,128)(2,1)} %param.19), channel_id=1, source_target_pairs={{0,2},{1,3},{2,4},{3,5},{4,6},{5,7},{6,8},{7,9},{8,10},{9,11},{10,... | collective-permute-start | bytes 786440 | tf_op jit(solution)/shard_map/ppermute | solution.py:22
  24.3 4.0 %collective-permute-start.1 = (bf16[64,2048]{1,0:T(8,128)(2,1)}, bf16[64,2048]{1,0:T(8,128)(2,1)}, u32[]{:S(2)}, u32[]{:S(2)}) collective-permute-start(bf16[64,2048]{1,0:T(8,128)(2,1)} %param.19), channel_id=1, source_target_pairs={{0,1},{1,2},{2,3},{3,4},{4,5},{5,6},{6,7},{7,8},{8,9},{9,10},{10,1... | collective-permute-start | bytes 786440 | tf_op jit(solution)/shard_map/ppermute | solution.py:22
  28.3 1.9 reduce_window_sum.33
  30.2 0.9 slice_bitcast_fusion.2
  31.1 18.4 %all-gather = f32[16,1,4096]{2,1,0:T(1,128)S(1)} all-gather(f32[1,1,4096]{2,1,0:T(1,128)S(1)} %slice_bitcast_fusion.2), channel_id=1, replica_groups=mesh['grp'=2,'eg'=4,'kg'=4] {'eg','kg'}, dimensions={0}, use_global_device_ids=true | all-gather | bytes 278528 | tf_op jit(solution)/shard_map/all_gather | solution.py:77
  50.2 0.7 subtract_maximum_fusion
  51.6 1.0 constant_dynamic-update-slice_fusion.2
  52.6 1.0 constant_dynamic-update-slice_fusion.1
  53.6 1.0 constant_dynamic-update-slice_fusion
  54.7 0.8 copy.69
  55.5 2.2 %fusion.49 = (f32[8,4,64]{2,1,0:T(4,128)S(1)}, f32[8,4,64,192]{3,2,1,0:T(8,128)}) fusion(pred[64,192]{1,0:T(8,128)(4,1)S(1)} %compare_and_fusion, bf16[64,8,4,128]{3,2,1,0:T(4,128)(2,1)S(1)} %reshape.151, bf16[192,8,128,1]{2,1,0,3:T(8,128)(2,1)S(1)} %bitcast.64), kind=kOutput, calls=%fused_computation.67 | convolution fusion | flops 102236352 | bytes 2510848 | tf_op jit(solution)/shard_map/sub | solution.py:103
  57.7 2.3 %fusion.3 = bf16[64,8,4,128]{3,0,2,1:T(8,128)(2,1)S(1)} fusion(f32[8,4,64,192]{3,2,1,0:T(8,128)} %get-tuple-element.14, f32[8,4,64]{2,1,0:T(4,128)S(1)} %get-tuple-element.13, bf16[192,8,128,1]{2,1,0,3:T(8,128)(2,1)} %bitcast.65), kind=kOutput, calls=%fused_computation.13 | convolution fusion | flops 101711872 | bytes 2498560 | tf_op jit(solution)/shard_map/kyje,eku->jkyu/dot_general | solution.py:105
  60.8 13.5 %all-gather.3.cloned.1.call-done = f32[16,16,4096]{2,1,0:T(8,128)} async-done(((f32[1,16,4096]{2,1,0:T(8,128)}), f32[16,16,4096]{2,1,0:T(8,128)}) %all-gather.3.cloned.1.call-update) | async-done | bytes 4194320 | tf_op jit(solution)/shard_map/all_gather | solution.py:76
  74.3 3.1 %select_reduce_fusion = f32[16,4096]{1,0:T(8,128)S(1)} fusion(f32[16,16,4096]{2,1,0:T(8,128)} %all-gather.3.cloned.1.call-done, f32[16,4096]{1,0:T(8,128)} %subtract_maximum_fusion, f32[16,4096]{1,0:T(8,128)S(1)} %copy-done.7, pred[16]{0:T(512)(128)(4,1)S(1)} %iota_compare_fusion.2), kind=kLoop, calls=%fused_computation.7 | loop fusion | flops 4128768 | bytes 4980752 | tf_op jit(solution)/shard_map/reduce_sum | solution.py:84
  77.5 5.3 %multiply_reduce_fusion = f32[64,4096]{1,0:T(8,128)S(1)} fusion(f32[16,4096]{1,0:T(8,128)S(1)} %select_reduce_fusion, f32[64,4096]{1,0:T(8,128)S(1)} %copy-done.6, f32[16,4096]{1,0:T(8,128)S(1)} %copy-done.7, f32[64,16]{1,0:T(8,128)S(1)} %copy.50), kind=kLoop, calls=%fused_computation.1 | loop fusion | flops 16515072 | bytes 2625536 | tf_op jit(solution)/shard_map/reduce_sum | solution.py:86
  82.9 0.7 fusion.5
  84.3 15.1 %all_to_all.15 = bf16[4,16,4096]{2,1,0:T(8,128)(2,1)S(1)} all-to-all(bf16[4,16,4096]{2,1,0:T(8,128)(2,1)S(1)} %convolution_convert_fusion.1), channel_id=1, replica_groups=mesh['grp'=2,'eg'=4,'kg'=4] {'eg'}, dimensions={0} | all-to-all | bytes 1048576 | tf_op jit(solution)/shard_map/all_to_all | solution.py:165
  99.6 29.1 %all_to_all.16 = bf16[4,4,16,4096]{3,2,0,1:T(8,128)(2,1)S(1)} all-to-all(bf16[4,4,16,4096]{3,2,0,1:T(8,128)(2,1)S(1)} %broadcast_in_dim.84), channel_id=1, replica_groups=mesh['grp'=2,'eg'=4,'kg'=4] {'kg'}, dimensions={1} | all-to-all | bytes 4194304 | tf_op jit(solution)/shard_map/all_to_all | solution.py:167
  128.9 1.3 copy-done.1
  130.2 0.8 copy-done.3
  131.0 0.7 fusion.54
  131.7 5.9 %convolution_convert_fusion = bf16[256,4096]{1,0:T(8,128)(2,1)} fusion(bf16[256,4096]{1,0:T(8,128)(2,1)S(1)} %copy-done, bf16[256,4096]{1,0:T(8,128)(2,1)} %bitcast.57, bf16[4096,256]{1,0:T(8,128)(2,1)} %param.24, f32[256,256]{1,0:T(8,128)S(1)} %fusion.54), kind=kOutput, calls=%fused_computation.2 | convolution fusion | flops 1075183616 | bytes 8650752 | tf_op jit(solution)/shard_map/dot_general | solution.py:115
  137.7 7.5 %all-to-all-start.2 = ((bf16[16,16,4096]{2,1,0:T(8,128)(2,1)}), bf16[16,16,4096]{2,1,0:T(8,128)(2,1)}, u32[]{:S(2)}, u32[]{:S(2)}) async-start(bf16[16,16,4096]{2,1,0:T(8,128)(2,1)} %bitcast.58), calls=%async_computation.2 | async-start | bytes 4194304 | tf_op jit(solution)/shard_map/all_to_all | solution.py:170
  145.2 47.5 %all-to-all-done.2 = bf16[16,16,4096]{2,1,0:T(8,128)(2,1)} async-done(((bf16[16,16,4096]{2,1,0:T(8,128)(2,1)}), bf16[16,16,4096]{2,1,0:T(8,128)(2,1)}, u32[]{:S(2)}, u32[]{:S(2)}) %all-to-all-start.2) | async-done | bytes 2097184 | tf_op jit(solution)/shard_map/all_to_all | solution.py:170
  192.7 2.1 %convert_reduce_fusion = f32[4,16,4096]{2,1,0:T(8,128)S(1)} fusion(bf16[16,16,4096]{2,1,0:T(8,128)(2,1)} %all-to-all-done.2), kind=kLoop, calls=%fused_computation.6 | loop fusion | flops 1835008 | bytes 3145728 | tf_op jit(solution)/shard_map/reduce_sum | solution.py:173
  194.8 1.8 fusion.1
  (56 shorter events, 3.5 us)
Async XLA Ops:
  7.2 124.5 %copy-start = (bf16[256,4096]{1,0:T(8,128)(2,1)S(1)}, bf16[256,4096]{1,0:T(8,128)(2,1)}, u32[]{:S(2)}) copy-start(bf16[256,4096]{1,0:T(8,128)(2,1)} %param.25) | copy-start | bytes 6291460
  7.2 2.5 %copy-start.2 = (bf16[64,4096]{1,0:T(8,128)(2,1)S(1)}, bf16[64,4096]{1,0:T(8,128)(2,1)}, u32[]{:S(2)}) copy-start(bf16[64,4096]{1,0:T(8,128)(2,1)} %param.14) | copy-start | bytes 1572868
  7.2 2.5 %copy-start.10 = (bf16[64,4096]{1,0:T(8,128)(2,1)S(1)}, bf16[64,4096]{1,0:T(8,128)(2,1)}, u32[]{:S(2)}) copy-start(bf16[64,4096]{1,0:T(8,128)(2,1)} %param.13) | copy-start | bytes 1572868
  7.2 67.1 %all-gather.3.cloned.1.call-start = ((), (), s32[]{:S(2)}) async-start(), calls=%async_computation.3 | async-start | bytes 4456448 | tf_op jit(solution)/shard_map/all_gather | solution.py:76
  9.7 1.3 copy-start.7
  19.3 30.7 %copy-start.13 = (s32[64,2]{0,1:T(2,128)S(1)}, s32[64,2]{0,1:T(2,128)}, u32[]{:S(2)}) copy-start(s32[64,2]{0,1:T(2,128)} %param.21) | copy-start | bytes 1540
  21.0 30.1 %copy-start.12 = (f32[16,64]{1,0:T(8,128)S(1)}, f32[16,64]{1,0:T(8,128)}, u32[]{:S(2)}) copy-start(f32[16,64]{1,0:T(8,128)} %c_ref.1) | copy-start | bytes 12292
  21.0 30.2 %copy-start.9 = (bf16[64,4096]{1,0:T(8,128)(2,1)S(1)}, bf16[64,4096]{1,0:T(8,128)(2,1)}, u32[]{:S(2)}) copy-start(bf16[64,4096]{1,0:T(8,128)(2,1)} %param.18) | copy-start | bytes 1572868
  21.0 30.6 %collective-permute-start = (bf16[64,2048]{1,0:T(8,128)(2,1)}, bf16[64,2048]{1,0:T(8,128)(2,1)}, u32[]{:S(2)}, u32[]{:S(2)}) collective-permute-start(bf16[64,2048]{1,0:T(8,128)(2,1)} %param.19), channel_id=1, source_target_pairs={{0,2},{1,3},{2,4},{3,5},{4,6},{5,7},{6,8},{7,9},{8,10},{9,11},{10,... | collective-permute-start | bytes 786440 | tf_op jit(solution)/shard_map/ppermute | solution.py:22
  24.3 28.3 %collective-permute-start.1 = (bf16[64,2048]{1,0:T(8,128)(2,1)}, bf16[64,2048]{1,0:T(8,128)(2,1)}, u32[]{:S(2)}, u32[]{:S(2)}) collective-permute-start(bf16[64,2048]{1,0:T(8,128)(2,1)} %param.19), channel_id=1, source_target_pairs={{0,1},{1,2},{2,3},{3,4},{4,5},{5,6},{6,7},{7,8},{8,9},{9,10},{10,1... | collective-permute-start | bytes 786440 | tf_op jit(solution)/shard_map/ppermute | solution.py:22
  60.8 22.8 %copy-start.5 = (bf16[64,4096]{1,0:T(8,128)(2,1)}, bf16[64,4096]{1,0:T(8,128)(2,1)S(1)}, u32[]{:S(2)}) copy-start(bf16[64,4096]{1,0:T(8,128)(2,1)S(1)} %convert_element_type.70) | copy-start | bytes 1572868
  74.3 3.1 %copy-start.6 = (f32[64,4096]{1,0:T(8,128)S(1)}, f32[64,4096]{1,0:T(8,128)}, u32[]{:S(2)}) copy-start(f32[64,4096]{1,0:T(8,128)} %reduce_window_sum.33) | copy-start | bytes 3145732
  77.5 5.4 %copy-start.8 = (f32[64,32,128]{2,1,0:T(8,128)S(1)}, f32[64,32,128]{2,1,0:T(8,128)}, u32[]{:S(2)}) copy-start(f32[64,32,128]{2,1,0:T(8,128)} %get-tuple-element.5) | copy-start | bytes 3145732
  82.9 1.0 copy-start.11
  83.6 16.0 %copy-start.4 = (bf16[64,4096]{1,0:T(8,128)(2,1)}, bf16[64,4096]{1,0:T(8,128)(2,1)S(1)}, u32[]{:S(2)}) copy-start(bf16[64,4096]{1,0:T(8,128)(2,1)S(1)} %fusion.5) | copy-start | bytes 1572868
  128.6 2.3 %copy-start.3 = (bf16[4096,256]{1,0:T(8,128)(2,1)S(1)}, bf16[4096,256]{1,0:T(8,128)(2,1)}, u32[]{:S(2)}) copy-start(bf16[4096,256]{1,0:T(8,128)(2,1)} %param.23) | copy-start | bytes 6291460
  128.9 1.3 copy-start.1
  137.7 7.5 %copy-start.14 = (f32[64,2]{0,1:T(2,128)S(1)}, f32[64,2]{0,1:T(2,128)}, u32[]{:S(2)}) copy-start(f32[64,2]{0,1:T(2,128)} %param.22) | copy-start | bytes 1540
  137.7 55.0 %all-to-all-start.2 = ((bf16[16,16,4096]{2,1,0:T(8,128)(2,1)}), bf16[16,16,4096]{2,1,0:T(8,128)(2,1)}, u32[]{:S(2)}, u32[]{:S(2)}) async-start(bf16[16,16,4096]{2,1,0:T(8,128)(2,1)} %bitcast.58), calls=%async_computation.2 | async-start | bytes 4194304 | tf_op jit(solution)/shard_map/all_to_all | solution.py:170
Sparse Core Ops, SparseCore 0:
  21.1 53.1 all-gather.2
